TPU v7x, 256 devices: a whole 4x4x8 slice. The times are simulated.
256 devices in a mesh: pipe: 2 (over core), expert: 128 (over x, z, y).
Axes of the slice: x: 4, y: 4, z: 8, core: 2. Of those that a mesh axis runs over, the one named last changes fastest.
Arguments:
- section_inputs: bfloat16 [2, 16384, 7168], P('pipe', 'expert'), may hold values from -6 to 6
- output_grads: bfloat16 [2, 16384, 7168], P('pipe', 'expert'), may hold values from -6 to 6
- w_gate: bfloat16 [2, 7168, 16384], P('pipe', None, 'expert'), may hold values from -0.0625 to 0.0625
- w_up: bfloat16 [2, 7168, 16384], P('pipe', None, 'expert'), may hold values from -0.0625 to 0.0625
- w_down: bfloat16 [2, 16384, 7168], P('pipe', 'expert'), may hold values from -0.125 to 0.125
- route_ids: int32 [2, 16384, 8], P('pipe', 'expert'), may hold values from 0 to 255, all different within a row; in each aligned block of 128 rows (0 to 127, 128 to 255, ..., all dimensions but the last counted through in order) at most 5 rows name the same one
- route_gates: float32 [2, 16384, 8], P('pipe', 'expert'), may hold values from 0.25 to 1
Outputs:
- handed_grads: bfloat16 [2, 16384, 7168], P('pipe', 'expert')
- down_grads: bfloat16 [2, 16384, 7168], P('pipe', 'expert')
Inputs may be any that keep to these rules, and one draw needn't show every extreme that they name: `route_ids`: each row names 8 different experts. Within the 128 rows of one device of one section, no expert is named by more than 5 rows.
All inputs are finite; a program needn't handle non-finite values.
Results may differ from a plain program's by a relative error of at most 0.0057.
Values may be sent and summed in bfloat16 or wider, within the bound.
No kernel may reach another device: no remote copies, remote signals or barrier semaphores. Data moves between devices by JAX's collectives and lax.ppermute only.
A program may use at most 192 MiB of HBM per device.

v0:
```python
import jax
import jax.numpy as jnp
from jax import lax
from jax.sharding import PartitionSpec as P

SHARDS = 16
CAP = 5


def from_behind(value, axis, steps):
    count = lax.axis_size(axis)
    pairs = [(source, (source + steps) % count) for source in range(count)]
    return lax.ppermute(value, axis, pairs)


def expert_work(rows_in, rows_grad, gate_cols, up_cols, down_rows):
    count, slots, model_width = rows_in.shape
    flat_in = rows_in.reshape(count * slots, model_width)
    flat_grad = rows_grad.reshape(count * slots, model_width)
    gate_pre = jnp.dot(flat_in, gate_cols, preferred_element_type=jnp.float32)
    up_pre = jnp.dot(flat_in, up_cols, preferred_element_type=jnp.float32)
    sigma = jax.nn.sigmoid(gate_pre)
    silu_gate = gate_pre * sigma
    hidden = (silu_gate * up_pre).astype(jnp.bfloat16)
    contract = (((1,), (1,)), ((), ()))
    back_hidden = lax.dot_general(
        flat_grad, down_rows, contract, preferred_element_type=jnp.float32
    )
    grad_gate = (back_hidden * up_pre * sigma * (1.0 + gate_pre * (1.0 - sigma))).astype(
        jnp.bfloat16
    )
    grad_up = (back_hidden * silu_gate).astype(jnp.bfloat16)
    partial_value = lax.dot_general(
        grad_gate, gate_cols, contract, preferred_element_type=jnp.float32
    )
    partial_value = partial_value + lax.dot_general(
        grad_up, up_cols, contract, preferred_element_type=jnp.float32
    )
    return (
        partial_value.astype(jnp.bfloat16).reshape(count, slots, model_width),
        hidden.reshape(count, slots, -1),
    )


def body(section_inputs, output_grads, w_gate, w_up, w_down, route_ids, route_gates):
    inputs = section_inputs[0]
    grads = output_grads[0]
    route = route_ids[0]
    gate = route_gates[0]
    gate_cols = w_gate[0]
    up_cols = w_up[0]
    down_rows = w_down[0]
    tok_rows, model_width = inputs.shape
    block_width = gate_cols.shape[1]
    width = lax.axis_size("expert")
    live_count = width // SHARDS
    slot_count = CAP
    expert_ids = jnp.arange(live_count, dtype=jnp.int32)
    hit = route[:, :, None] == expert_ids
    member = jnp.sum(hit.astype(jnp.int32), axis=1)
    weight = jnp.sum(jnp.where(hit, gate[:, :, None], 0.0), axis=1)
    position = jnp.cumsum(member, axis=0) - member
    slot_ids = jnp.arange(slot_count, dtype=jnp.int32)
    pick = (member[:, :, None] == 1) & (position[:, :, None] == slot_ids)
    pick_mat = pick.astype(jnp.bfloat16).reshape(tok_rows, live_count * slot_count)
    rows_first = (((0,), (0,)), ((), ()))
    rows_in = lax.dot_general(
        pick_mat, inputs, rows_first, preferred_element_type=jnp.float32
    ).astype(jnp.bfloat16)
    chosen_grads = lax.dot_general(pick_mat, grads, rows_first, preferred_element_type=jnp.float32)
    slot_gate = jnp.sum(pick.astype(jnp.float32) * weight[:, :, None], axis=0).reshape(
        live_count * slot_count, 1
    )
    rows_grad = (chosen_grads * slot_gate).astype(jnp.bfloat16)
    send_in = jnp.broadcast_to(
        rows_in.reshape(live_count, 1, slot_count, model_width),
        (live_count, SHARDS, slot_count, model_width),
    ).reshape(width, slot_count, model_width)
    send_grad = jnp.broadcast_to(
        rows_grad.reshape(live_count, 1, slot_count, model_width),
        (live_count, SHARDS, slot_count, model_width),
    ).reshape(width, slot_count, model_width)
    got_in, got_grad = (
        lax.all_to_all(send_in, "expert", split_axis=0, concat_axis=0, tiled=True),
        lax.all_to_all(send_grad, "expert", split_axis=0, concat_axis=0, tiled=True),
    )
    partial_value, hidden = expert_work(got_in, got_grad, gate_cols, up_cols, down_rows)
    returned = lax.all_to_all(partial_value, "expert", split_axis=0, concat_axis=0, tiled=True)
    down_part = lax.dot_general(
        hidden.reshape(-1, block_width),
        got_grad.reshape(-1, model_width),
        rows_first,
        preferred_element_type=jnp.float32,
    ).astype(jnp.bfloat16)
    full_pick = jnp.broadcast_to(pick[:, :, None, :], (tok_rows, live_count, SHARDS, slot_count))
    full_pick = full_pick.astype(jnp.bfloat16).reshape(tok_rows, width * slot_count)
    branch = jnp.dot(
        full_pick,
        returned.reshape(width * slot_count, model_width),
        preferred_element_type=jnp.float32,
    )
    input_grad = (grads.astype(jnp.float32) + branch).astype(jnp.bfloat16)
    handed = from_behind(input_grad, "pipe", -1)
    return (handed[None], down_part[None])


def solution(mesh):
    return jax.shard_map(
        body,
        mesh=mesh,
        in_specs=(
            P("pipe", "expert", None),
            P("pipe", "expert", None),
            P("pipe", None, "expert"),
            P("pipe", None, "expert"),
            P("pipe", "expert", None),
            P("pipe", "expert", None),
            P("pipe", "expert", None),
        ),
        out_specs=(P("pipe", "expert", None), P("pipe", "expert", None)),
        check_vma=False,
    )
```

profile of v0, /device:TPU:33, one launch (start us, length us, event | category | flops | bytes accessed | tf_op | source)
XLA Modules:
  0.0 1101.8 jit_solution(733508926719845679)
XLA Ops:
  0.6 0.0 copy-start
  0.6 0.8 convert_reduce_fusion
  1.5 0.1 copy.15
  1.6 0.2 reduce_window_sum.11
  1.9 1.9 convolution_convert_fusion.1
  3.8 0.3 broadcast_in_dim.51
  4.0 7.1 broadcast_in_dim.52
  11.1 0.0 copy-start.5
  11.1 0.0 copy-start.6
  11.1 15.0 %all-to-all-start.1 = ((bf16[128,5,7168]{2,1,0:T(8,128)(2,1)}), bf16[128,5,7168]{2,1,0:T(8,128)(2,1)}, u32[]{:S(2)}, u32[]{:S(2)}) async-start(bf16[128,5,7168]{2,1,0:T(8,128)(2,1)} %bitcast.39), calls=%async_computation.1 | async-start | bytes 29360128 | tf_op jit(solution)/shard_map/all_to_all | solution.py:84
  26.1 0.0 copy-done.5
  26.1 0.0 copy-done.6
  26.1 0.1 select_reduce_fusion
  26.2 0.1 mul.41
  26.3 1.9 fusion.2
  28.2 0.3 broadcast_in_dim.49
  28.5 314.0 %all-to-all-done.1 = bf16[128,5,7168]{2,1,0:T(8,128)(2,1)} async-done(((bf16[128,5,7168]{2,1,0:T(8,128)(2,1)}), bf16[128,5,7168]{2,1,0:T(8,128)(2,1)}, u32[]{:S(2)}, u32[]{:S(2)}) %all-to-all-start.1) | async-done | bytes 9175072 | tf_op jit(solution)/shard_map/all_to_all | solution.py:84
  342.4 7.1 broadcast_in_dim.50
  349.5 13.8 %all-to-all-start = ((bf16[128,5,7168]{2,1,0:T(8,128)(2,1)}), bf16[128,5,7168]{2,1,0:T(8,128)(2,1)}, u32[]{:S(2)}, u32[]{:S(2)}) async-start(bf16[128,5,7168]{2,1,0:T(8,128)(2,1)} %bitcast.40), calls=%async_computation | async-start | bytes 29360128 | tf_op jit(solution)/shard_map/all_to_all | solution.py:85
  363.3 15.2 %reshape.117 = bf16[640,7168]{1,0:T(8,128)(2,1)} reshape(bf16[128,5,7168]{2,1,0:T(8,128)(2,1)} %all-to-all-done.1) | data formatting | bytes 18350080 | tf_op jit(solution)/shard_map/reshape | solution.py:18
  378.5 0.0 copy-done
  378.5 0.0 copy-start.2
  378.5 0.0 copy-start.4
  378.5 6.3 fusion.5
  384.7 0.0 copy-done.2
  384.8 0.4 copy-done.4
  385.2 2.5 fusion.8
  387.7 291.2 %all-to-all-done = bf16[128,5,7168]{2,1,0:T(8,128)(2,1)} async-done(((bf16[128,5,7168]{2,1,0:T(8,128)(2,1)}), bf16[128,5,7168]{2,1,0:T(8,128)(2,1)}, u32[]{:S(2)}, u32[]{:S(2)}) %all-to-all-start) | async-done | bytes 9175072 | tf_op jit(solution)/shard_map/all_to_all | solution.py:85
  678.9 15.1 %reshape.115 = bf16[640,7168]{1,0:T(8,128)(2,1)} reshape(bf16[128,5,7168]{2,1,0:T(8,128)(2,1)} %all-to-all-done) | data formatting | bytes 18350080 | tf_op jit(solution)/shard_map/reshape | solution.py:19
  694.0 6.6 fusion.11
  700.6 8.9 fusion.3
  709.5 12.9 %add_convert_fusion = bf16[640,7168]{1,0:T(8,128)(2,1)} fusion(f32[640,7168]{1,0:T(8,128)} %fusion.3, bf16[1,7168,128]{2,1,0:T(8,128)(2,1)} %param.10, f32[640,128]{1,0:T(8,128)S(1)} %fusion.11, f32[640,128]{1,0:T(8,128)S(1)} %fusion.5), kind=kOutput, calls=%fused_computation | convolution fusion | flops 1184071680 | bytes 30015488 | tf_op jit(solution)/shard_map/dot_general | solution.py:36
  722.4 14.8 %reshape.118 = bf16[128,5,7168]{2,1,0:T(8,128)(2,1)} reshape(bf16[640,7168]{1,0:T(8,128)(2,1)} %add_convert_fusion) | data formatting | bytes 18350080 | tf_op jit(solution)/shard_map/reshape | solution.py:40
  737.2 14.0 %all-to-all-start.2 = ((bf16[128,5,7168]{2,1,0:T(8,128)(2,1)}), bf16[128,5,7168]{2,1,0:T(8,128)(2,1)}, u32[]{:S(2)}, u32[]{:S(2)}) async-start(bf16[128,5,7168]{2,1,0:T(8,128)(2,1)} %reshape.118), calls=%async_computation.2 | async-start | bytes 29360128 | tf_op jit(solution)/shard_map/all_to_all | solution.py:88
  751.2 0.1 reshape.113
  751.3 0.0 copy-start.3
  751.3 315.3 %all-to-all-done.2 = bf16[128,5,7168]{2,1,0:T(8,128)(2,1)} async-done(((bf16[128,5,7168]{2,1,0:T(8,128)(2,1)}), bf16[128,5,7168]{2,1,0:T(8,128)(2,1)}, u32[]{:S(2)}, u32[]{:S(2)}) %all-to-all-start.2) | async-done | bytes 9175072 | tf_op jit(solution)/shard_map/all_to_all | solution.py:88
  1066.6 15.1 %reshape.119 = bf16[640,7168]{1,0:T(8,128)(2,1)} reshape(bf16[128,5,7168]{2,1,0:T(8,128)(2,1)} %all-to-all-done.2) | data formatting | bytes 18350080 | tf_op jit(solution)/shard_map/reshape | solution.py:99
  1081.8 0.0 copy-done.3
  1081.8 5.3 fusion
  1087.0 6.0 collective-permute-start
  1093.1 6.5 fusion.1
  1099.6 0.0 collective-permute-done
  1099.6 0.0 copy-start.1
  1099.6 1.2 copy.20
  1100.8 0.9 copy-done.1
  (7 shorter events, 0.2 us)
Async XLA Ops:
  0.6 377.8 %copy-start = (bf16[1,7168,128]{2,1,0:T(8,128)(2,1)S(1)}, bf16[1,7168,128]{2,1,0:T(8,128)(2,1)}, u32[]{:S(2)}) copy-start(bf16[1,7168,128]{2,1,0:T(8,128)(2,1)} %param.9) | copy-start | bytes 5505028
  11.1 15.0 %copy-start.5 = (s32[1,128,8]{1,2,0:T(8,128)S(1)}, s32[1,128,8]{1,2,0:T(8,128)}, u32[]{:S(2)}) copy-start(s32[1,128,8]{1,2,0:T(8,128)} %param.12) | copy-start | bytes 12292
  11.1 15.0 %copy-start.6 = (f32[1,128,8]{1,2,0:T(8,128)S(1)}, f32[1,128,8]{1,2,0:T(8,128)}, u32[]{:S(2)}) copy-start(f32[1,128,8]{1,2,0:T(8,128)} %param.13) | copy-start | bytes 12292
  11.1 331.3 %all-to-all-start.1 = ((bf16[128,5,7168]{2,1,0:T(8,128)(2,1)}), bf16[128,5,7168]{2,1,0:T(8,128)(2,1)}, u32[]{:S(2)}, u32[]{:S(2)}) async-start(bf16[128,5,7168]{2,1,0:T(8,128)(2,1)} %bitcast.39), calls=%async_computation.1 | async-start | bytes 29360128 | tf_op jit(solution)/shard_map/all_to_all | solution.py:84
  349.5 329.4 %all-to-all-start = ((bf16[128,5,7168]{2,1,0:T(8,128)(2,1)}), bf16[128,5,7168]{2,1,0:T(8,128)(2,1)}, u32[]{:S(2)}, u32[]{:S(2)}) async-start(bf16[128,5,7168]{2,1,0:T(8,128)(2,1)} %bitcast.40), calls=%async_computation | async-start | bytes 29360128 | tf_op jit(solution)/shard_map/all_to_all | solution.py:85
  378.5 6.3 copy-start.2
  378.5 6.7 copy-start.4
  737.2 329.4 %all-to-all-start.2 = ((bf16[128,5,7168]{2,1,0:T(8,128)(2,1)}), bf16[128,5,7168]{2,1,0:T(8,128)(2,1)}, u32[]{:S(2)}, u32[]{:S(2)}) async-start(bf16[128,5,7168]{2,1,0:T(8,128)(2,1)} %reshape.118), calls=%async_computation.2 | async-start | bytes 29360128 | tf_op jit(solution)/shard_map/all_to_all | solution.py:88
  751.3 330.4 %copy-start.3 = (bf16[1,128,7168]{2,1,0:T(8,128)(2,1)S(1)}, bf16[1,128,7168]{2,1,0:T(8,128)(2,1)}, u32[]{:S(2)}) copy-start(bf16[1,128,7168]{2,1,0:T(8,128)(2,1)} %param.8) | copy-start | bytes 5505028
  1087.0 12.6 %collective-permute-start = (bf16[128,7168]{1,0:T(8,128)(2,1)S(1)}, bf16[128,7168]{1,0:T(8,128)(2,1)S(1)}, u32[]{:S(2)}, u32[]{:S(2)}) collective-permute-start(bf16[128,7168]{1,0:T(8,128)(2,1)S(1)} %fusion), channel_id=1, source_target_pairs={{0,128},{128,0},{1,129},{129,1},{2,130},{130,2},{3,131},{131,3},{4... | collective-permute-start | bytes 5505032 | tf_op jit(solution)/shard_map/ppermute | solution.py:13
  1099.6 2.2 copy-start.1
where the time goes:
time: 1100 us
  waiting for transfers between devices  920 us (84%)
  local copies, waits for them, and re-layouts  77.8 us (7%)
  matrix products  52.8 us (5%)
  starting transfers between devices  48.8 us (4%)
    all_to_all x1, waiting for transfers between devices, body(): lax.all_to_all(partial_value, 'expert', split_axis=0, concat_axis=0, tile...  315 us
    all_to_all x1, waiting for transfers between devices, body(): lax.all_to_all(send_in, 'expert', split_axis=0, concat_axis=0, tiled=True)  314 us
    all_to_all x1, waiting for transfers between devices, body(): lax.all_to_all(send_grad, 'expert', split_axis=0, concat_axis=0, tiled=True)  291 us
  transfers between devices with their start and end apart: 4, of which 3 were waited for; matrix products, arithmetic and copies ran while one was open for 3% of the time, Pallas kernels for 0%

commit v1 on v0

v1 whole, which is shorter than its diff:
```python
import jax
import jax.numpy as jnp
from jax import lax
from jax.sharding import Mesh
from jax.sharding import PartitionSpec as P

SHARDS = 16
CAP = 5


def from_behind(value, axis, steps):
    count = lax.axis_size(axis)
    pairs = [(source, (source + steps) % count) for source in range(count)]
    return lax.ppermute(value, axis, pairs)


def body(section_inputs, output_grads, w_gate, w_up, w_down, route_ids, route_gates):
    inputs = section_inputs[0]
    grads = output_grads[0]
    route = route_ids[0]
    gate = route_gates[0]
    gate_cols = w_gate[0]
    up_cols = w_up[0]
    down_rows = w_down[0]
    tok_rows, model_width = inputs.shape
    block_width = gate_cols.shape[1]
    live_count = lax.axis_size("group")
    slot_count = CAP
    expert_ids = jnp.arange(live_count, dtype=jnp.int32)
    hit = route[:, :, None] == expert_ids
    member = jnp.sum(hit.astype(jnp.int32), axis=1)
    weight = jnp.sum(jnp.where(hit, gate[:, :, None], 0.0), axis=1)
    position = jnp.cumsum(member, axis=0) - member
    slot_ids = jnp.arange(slot_count, dtype=jnp.int32)
    pick = (member[:, :, None] == 1) & (position[:, :, None] == slot_ids)
    pick_mat = pick.astype(jnp.bfloat16).reshape(tok_rows, live_count * slot_count)
    rows_first = (((0,), (0,)), ((), ()))
    rows_in = lax.dot_general(
        pick_mat, inputs, rows_first, preferred_element_type=jnp.float32
    ).astype(jnp.bfloat16)
    chosen_grads = lax.dot_general(pick_mat, grads, rows_first, preferred_element_type=jnp.float32)
    slot_gate = jnp.sum(pick.astype(jnp.float32) * weight[:, :, None], axis=0).reshape(
        live_count * slot_count, 1
    )
    rows_grad = (chosen_grads * slot_gate).astype(jnp.bfloat16)
    send_in = rows_in.reshape(live_count, slot_count, model_width)
    send_grad = rows_grad.reshape(live_count, slot_count, model_width)
    near_in = lax.all_to_all(send_in, "group", 0, 0, tiled=True)
    near_grad = lax.all_to_all(send_grad, "group", 0, 0, tiled=True)
    got_in = lax.all_gather(near_in, "member", axis=0, tiled=False)
    got_grad = lax.all_gather(near_grad, "member", axis=0, tiled=False)
    members = got_in.shape[0]
    flat_in = got_in.reshape(-1, model_width)
    flat_grad = got_grad.reshape(-1, model_width)
    gate_pre = jnp.dot(flat_in, gate_cols, preferred_element_type=jnp.float32)
    up_pre = jnp.dot(flat_in, up_cols, preferred_element_type=jnp.float32)
    sigma = jax.nn.sigmoid(gate_pre)
    silu_gate = gate_pre * sigma
    hidden = (silu_gate * up_pre).astype(jnp.bfloat16)
    contract = (((1,), (1,)), ((), ()))
    back_hidden = lax.dot_general(
        flat_grad, down_rows, contract, preferred_element_type=jnp.float32
    )
    grad_gate = (back_hidden * up_pre * sigma * (1.0 + gate_pre * (1.0 - sigma))).astype(
        jnp.bfloat16
    )
    grad_up = (back_hidden * silu_gate).astype(jnp.bfloat16)
    partial_value = lax.dot_general(
        grad_gate, gate_cols, contract, preferred_element_type=jnp.float32
    )
    partial_value = partial_value + lax.dot_general(
        grad_up, up_cols, contract, preferred_element_type=jnp.float32
    )
    parts = partial_value.astype(jnp.bfloat16).reshape(members, live_count * slot_count, model_width)
    down_part = lax.dot_general(
        hidden, flat_grad, rows_first, preferred_element_type=jnp.float32
    ).astype(jnp.bfloat16)
    blocks = lax.all_to_all(parts, "member", 0, 0, tiled=True)
    summed = jnp.sum(blocks.astype(jnp.float32), axis=0).reshape(live_count, slot_count, model_width)
    returned = lax.all_to_all(summed, "group", 0, 0, tiled=True)
    branch = jnp.dot(
        pick_mat.astype(jnp.float32),
        returned.reshape(live_count * slot_count, model_width),
        preferred_element_type=jnp.float32,
        precision=lax.Precision.HIGHEST,
    )
    input_grad = (grads.astype(jnp.float32) + branch).astype(jnp.bfloat16)
    handed = from_behind(input_grad, "pipe", -1)
    return (handed[None], down_part[None])


def solution(mesh):
    pipe = mesh.shape["pipe"]
    width = mesh.shape["expert"]
    groups = width // SHARDS
    inner = Mesh(mesh.devices.reshape(pipe, groups, SHARDS), ("pipe", "group", "member"))
    rows = P("pipe", ("group", "member"), None)
    cols = P("pipe", None, ("group", "member"))
    return jax.shard_map(
        body,
        mesh=inner,
        in_specs=(rows, rows, cols, cols, rows, rows, rows),
        out_specs=(rows, rows),
        check_vma=False,
    )
```

time: 1100 us -> 616 us (0.56)
  waiting for transfers between devices: 920 us -> 150 us
  blocking collectives: 0 us -> 331 us
  starting transfers between devices: 48.8 us -> 2.02 us
  between operations: 0.8 us -> 14.2 us
  local copies, waits for them, and re-layouts: 77.8 us -> 64.4 us
    all_to_all x3 -> x0, waiting for transfers between devices: 920 us -> none  [the longest x1 315 us: body(): lax.all_to_all(partial_value, 'expert', split_axis=0, concat_axis=0, tile...]
    all_to_all x0 -> x4, blocking collectives: none -> 331 us  [the longest x1 207 us: body(): blocks = lax.all_to_all(parts, 'member', 0, 0, tiled=True)]
    all_gather x0 -> x2, waiting for transfers between devices: none -> 150 us  [the longest x1 76.2 us: body(): got_in = lax.all_gather(near_in, 'member', axis=0, tiled=False)]
    all_to_all x3 -> x0, starting transfers between devices: 42.7 us -> none  [the longest x1 15 us: body(): lax.all_to_all(send_in, 'expert', split_axis=0, concat_axis=0, tiled=True)]
    reshape x5, local copies, waits for them, and re-layouts: 60.2 us -> 31.1 us  [the longest x1 15.2 us: body(): flat_in = got_in.reshape(-1, model_width)]
    all_gather x0 -> x2, local copies, waits for them, and re-layouts: none -> 27.9 us  [the longest x1 13.9 us: body(): got_in = lax.all_gather(near_in, 'member', axis=0, tiled=False)]
    broadcast_in_dim x5 -> x0, local copies, waits for them, and re-layouts: 14.7 us -> none  [the longest x2 7.32 us: body(): jnp.broadcast_to(rows_in.reshape(live_count, 1, slot_count, model_width),...]
  transfers between devices with their start and end apart: 4 -> 3, of which waited for: 3 -> 2; matrix products, arithmetic and copies ran while one was open for 3% -> 8% of each run, Pallas kernels for 0% -> 0%
where the time goes in v1:
time: 616 us; the launch traced here: 614 us
  blocking collectives  331 us (54%)
  waiting for transfers between devices  150 us (24%)
  local copies, waits for them, and re-layouts  64.4 us (10%)
  matrix products  49.5 us (8%)
  between operations  14.2 us (2%)
    all_to_all x1, blocking collectives, body(): blocks = lax.all_to_all(parts, 'member', 0, 0, tiled=True)  207 us
    all_gather x1, waiting for transfers between devices, body(): got_in = lax.all_gather(near_in, 'member', axis=0, tiled=False)  76.2 us
    all_gather x1, waiting for transfers between devices, body(): got_grad = lax.all_gather(near_grad, 'member', axis=0, tiled=False)  73.8 us
    all_to_all x1, blocking collectives, body(): returned = lax.all_to_all(summed, 'group', 0, 0, tiled=True)  53.2 us
    all_to_all x1, blocking collectives, body(): near_in = lax.all_to_all(send_in, 'group', 0, 0, tiled=True)  36.8 us
    all_to_all x1, blocking collectives, body(): near_grad = lax.all_to_all(send_grad, 'group', 0, 0, tiled=True)  34.6 us
    reshape x1, local copies, waits for them, and re-layouts, body(): flat_in = got_in.reshape(-1, model_width)  15.2 us
    reshape x1, local copies, waits for them, and re-layouts, body(): flat_grad = got_grad.reshape(-1, model_width)  15.2 us
  transfers between devices with their start and end apart: 3, of which 2 were waited for; matrix products, arithmetic and copies ran while one was open for 8% of the time, Pallas kernels for 0%

profile of v1, /device:TPU:33, one launch (start us, length us, event | category | flops | bytes accessed | tf_op | source)
XLA Modules:
  0.0 614.2 jit_solution(13033601772582271242)
XLA Ops:
  7.2 0.0 copy-start
  7.2 0.0 all-gather.7.cloned.1.call-start
  7.2 0.8 convert_reduce_fusion.1
  8.1 0.1 copy.27
  8.2 0.2 reduce_window_sum.11
  8.5 1.9 convolution_convert_fusion.1
  10.3 0.3 reshape.104
  10.6 0.0 copy-start.7
  10.6 0.0 copy-start.8
  10.6 36.8 %all_to_all.20 = bf16[8,5,7168]{2,1,0:T(8,128)(2,1)S(1)} all-to-all(bf16[8,5,7168]{2,1,0:T(8,128)(2,1)S(1)} %reshape.104), channel_id=1, replica_groups=mesh['pipe'=2,'group'=8,'member'=16] {'group'}, dimensions={0} | all-to-all | bytes 1146880 | tf_op jit(solution)/shard_map/all_to_all | solution.py:48
  47.4 1.2 copy.32
  48.6 0.0 all-gather.7.cloned.1.call-update
  48.6 0.0 all-gather.5.cloned.1.call-start
  48.7 0.0 copy-done.7
  48.7 0.0 copy-done.8
  48.7 0.1 select_reduce_fusion
  48.8 0.1 mul.41
  48.9 1.9 fusion.3
  50.8 0.3 reshape.102
  51.0 34.6 %all_to_all.21 = bf16[8,5,7168]{2,1,0:T(8,128)(2,1)S(1)} all-to-all(bf16[8,5,7168]{2,1,0:T(8,128)(2,1)S(1)} %reshape.102), channel_id=1, replica_groups=mesh['pipe'=2,'group'=8,'member'=16] {'group'}, dimensions={0} | all-to-all | bytes 1146880 | tf_op jit(solution)/shard_map/all_to_all | solution.py:49
  85.6 1.2 copy.30
  86.8 0.0 all-gather.5.cloned.1.call-update
  86.9 76.2 %all-gather.7.cloned.1.call-done = bf16[128,5,7168]{2,0,1:T(8,128)(2,1)} async-done(((bf16[8,5,7168]{2,0,1:T(8,128)(2,1)}), bf16[128,5,7168]{2,0,1:T(8,128)(2,1)}) %all-gather.7.cloned.1.call-update) | async-done | bytes 9175056 | tf_op jit(solution)/shard_map/all_gather | solution.py:50
  163.1 13.9 %copy.33 = bf16[128,5,7168]{2,1,0:T(8,128)(2,1)} copy(bf16[128,5,7168]{2,0,1:T(8,128)(2,1)} %all-gather.7.cloned.1.call-done) | data formatting | bytes 18350080 | tf_op jit(solution)/shard_map/all_gather | solution.py:50
  177.0 15.2 %reshape.105 = bf16[640,7168]{1,0:T(8,128)(2,1)} reshape(bf16[128,5,7168]{2,1,0:T(8,128)(2,1)} %copy.33) | data formatting | bytes 18350080 | tf_op jit(solution)/shard_map/reshape | solution.py:53
  192.3 0.0 copy-done
  192.3 0.0 copy-start.2
  192.3 0.0 copy-start.6
  192.3 6.3 %fusion.6 = f32[640,128]{1,0:T(8,128)S(1)} fusion(bf16[640,7168]{1,0:T(8,128)(2,1)} %reshape.105, bf16[1,7168,128]{2,1,0:T(8,128)(2,1)S(1)} %copy-done), kind=kOutput, calls=%fused_computation.12 | convolution fusion | flops 1174405120 | bytes 11337728 | tf_op jit(solution)/shard_map/dot_general | solution.py:55
  198.6 0.0 copy-done.2
  198.7 0.5 copy-done.6
  199.2 2.5 fusion.9
  201.7 0.0 copy-start.3
  201.7 73.8 %all-gather.5.cloned.1.call-done = bf16[128,5,7168]{2,0,1:T(8,128)(2,1)} async-done(((bf16[8,5,7168]{2,0,1:T(8,128)(2,1)}), bf16[128,5,7168]{2,0,1:T(8,128)(2,1)}) %all-gather.5.cloned.1.call-update) | async-done | bytes 9175056 | tf_op jit(solution)/shard_map/all_gather | solution.py:51
  275.4 13.9 %copy.31 = bf16[128,5,7168]{2,1,0:T(8,128)(2,1)} copy(bf16[128,5,7168]{2,0,1:T(8,128)(2,1)} %all-gather.5.cloned.1.call-done) | data formatting | bytes 18350080 | tf_op jit(solution)/shard_map/all_gather | solution.py:51
  289.4 15.2 %reshape.103 = bf16[640,7168]{1,0:T(8,128)(2,1)} reshape(bf16[128,5,7168]{2,1,0:T(8,128)(2,1)} %copy.31) | data formatting | bytes 18350080 | tf_op jit(solution)/shard_map/reshape | solution.py:54
  304.5 6.6 %fusion.12 = f32[640,128]{1,0:T(8,128)S(1)} fusion(bf16[640,7168]{1,0:T(8,128)(2,1)} %reshape.103, bf16[1,128,7168]{2,1,0:T(8,128)(2,1)} %param.11), kind=kOutput, calls=%fused_computation.18 | convolution fusion | flops 1174405120 | bytes 11337728 | tf_op jit(solution)/shard_map/dot_general | solution.py:61
  311.2 0.0 copy-done.3
  311.2 8.9 %fusion.4 = f32[640,7168]{1,0:T(8,128)} fusion(bf16[1,7168,128]{2,1,0:T(8,128)(2,1)S(1)} %copy-done, f32[640,128]{1,0:T(8,128)S(1)} %fusion.6, f32[640,128]{1,0:T(8,128)S(1)} %fusion.12, f32[640,128]{1,0:T(8,128)S(1)} %fusion.9), kind=kOutput, calls=%fused_computation.10 | convolution fusion | flops 1175224320 | bytes 21168128 | tf_op jit(solution)/shard_map/dot_general | solution.py:68
  320.1 12.9 %add_convert_fusion = bf16[640,7168]{1,0:T(8,128)(2,1)} fusion(f32[640,7168]{1,0:T(8,128)} %fusion.4, bf16[1,7168,128]{2,1,0:T(8,128)(2,1)} %param.10, f32[640,128]{1,0:T(8,128)S(1)} %fusion.12, f32[640,128]{1,0:T(8,128)S(1)} %fusion.6), kind=kOutput, calls=%fused_computation.1 | convolution fusion | flops 1184071680 | bytes 30015488 | tf_op jit(solution)/shard_map/dot_general | solution.py:71
  332.9 206.6 %all_to_all.22 = bf16[16,40,7168]{2,1,0:T(8,128)(2,1)S(1)} all-to-all(bf16[16,40,7168]{2,1,0:T(8,128)(2,1)} %bitcast.41), channel_id=1, replica_groups=mesh['pipe'=2,'group'=8,'member'=16] {'member'}, dimensions={0} | all-to-all | bytes 18350080 | tf_op jit(solution)/shard_map/all_to_all | solution.py:78
  539.5 1.8 convert_reduce_fusion
  541.3 0.2 reshape.107
  541.5 0.0 copy-start.5
  541.5 53.2 %all_to_all.23 = f32[8,5,7168]{2,1,0:T(8,128)S(1)} all-to-all(f32[8,5,7168]{2,1,0:T(8,128)S(1)} %reshape.107), channel_id=1, replica_groups=mesh['pipe'=2,'group'=8,'member'=16] {'group'}, dimensions={0} | all-to-all | bytes 2293760 | tf_op jit(solution)/shard_map/all_to_all | solution.py:80
  594.7 0.0 copy-done.5
  594.7 0.0 copy-start.4
  594.7 2.0 fusion.1
  596.7 1.9 collective-permute-start
  598.6 0.0 copy-done.4
  598.6 6.5 %fusion.2 = bf16[1,128,7168]{2,1,0:T(8,128)(2,1)} fusion(bf16[640,7168]{1,0:T(8,128)(2,1)} %reshape.103, f32[640,128]{1,0:T(8,128)S(1)} %copy-done.4, f32[640,128]{1,0:T(8,128)S(1)} %fusion.6), kind=kOutput, calls=%fused_computation.6 | convolution fusion | flops 1175814144 | bytes 11665408 | tf_op jit(solution)/shard_map/dot_general | solution.py:75
  605.2 0.0 collective-permute-done
  605.2 0.0 copy-start.1
  605.2 1.2 copy.35
  606.4 0.9 copy-done.1
  (6 shorter events, 0.1 us)
Async XLA Ops:
  7.2 185.1 %copy-start = (bf16[1,7168,128]{2,1,0:T(8,128)(2,1)S(1)}, bf16[1,7168,128]{2,1,0:T(8,128)(2,1)}, u32[]{:S(2)}) copy-start(bf16[1,7168,128]{2,1,0:T(8,128)(2,1)} %param.9) | copy-start | bytes 5505028
  7.2 155.9 %all-gather.7.cloned.1.call-start = ((), (), s32[]{:S(2)}) async-start(), calls=%async_computation.5 | async-start | bytes 9748480 | tf_op jit(solution)/shard_map/all_gather | solution.py:50
  10.6 38.1 %copy-start.7 = (s32[1,128,8]{1,2,0:T(8,128)S(1)}, s32[1,128,8]{1,2,0:T(8,128)}, u32[]{:S(2)}) copy-start(s32[1,128,8]{1,2,0:T(8,128)} %param.12) | copy-start | bytes 12292
  10.6 38.1 %copy-start.8 = (f32[1,128,8]{1,2,0:T(8,128)S(1)}, f32[1,128,8]{1,2,0:T(8,128)}, u32[]{:S(2)}) copy-start(f32[1,128,8]{1,2,0:T(8,128)} %param.13) | copy-start | bytes 12292
  48.6 226.8 %all-gather.5.cloned.1.call-start = ((), (), s32[]{:S(2)}) async-start(), calls=%async_computation.4 | async-start | bytes 9748480 | tf_op jit(solution)/shard_map/all_gather | solution.py:51
  192.3 6.4 %copy-start.2 = (bf16[640,7168]{1,0:T(8,128)(2,1)S(1)}, bf16[640,7168]{1,0:T(8,128)(2,1)}, u32[]{:S(2)}) copy-start(bf16[640,7168]{1,0:T(8,128)(2,1)} %reshape.105) | copy-start | bytes 27525124
  192.3 6.9 %copy-start.6 = (bf16[1,7168,128]{2,1,0:T(8,128)(2,1)S(1)}, bf16[1,7168,128]{2,1,0:T(8,128)(2,1)}, u32[]{:S(2)}) copy-start(bf16[1,7168,128]{2,1,0:T(8,128)(2,1)} %param.10) | copy-start | bytes 5505028
  201.7 109.5 %copy-start.3 = (f32[640,128]{1,0:T(8,128)}, f32[640,128]{1,0:T(8,128)S(1)}, u32[]{:S(2)}) copy-start(f32[640,128]{1,0:T(8,128)S(1)} %fusion.9) | copy-start | bytes 983044
  541.5 53.2 %copy-start.5 = (bf16[1,128,7168]{2,1,0:T(8,128)(2,1)S(1)}, bf16[1,128,7168]{2,1,0:T(8,128)(2,1)}, u32[]{:S(2)}) copy-start(bf16[1,128,7168]{2,1,0:T(8,128)(2,1)} %param.8) | copy-start | bytes 5505028
  594.7 4.0 copy-start.4
  596.7 8.5 %collective-permute-start = (bf16[128,7168]{1,0:T(8,128)(2,1)S(1)}, bf16[128,7168]{1,0:T(8,128)(2,1)S(1)}, u32[]{:S(2)}, u32[]{:S(2)}) collective-permute-start(bf16[128,7168]{1,0:T(8,128)(2,1)S(1)} %fusion.1), channel_id=1, source_target_pairs={{0,128},{128,0},{1,129},{129,1},{2,130},{130,2},{3,131},{131,3},{4... | collective-permute-start | bytes 5505032 | tf_op jit(solution)/shard_map/ppermute | solution.py:14
  605.2 2.2 copy-start.1
Sparse Core Ops, SparseCore 0:
  48.7 114.2 all-gather.6
  165.4 109.9 all-gather.4

commit v2 on v1

--- a/solution.py
+++ b/solution.py
@@ -47,36 +47,39 @@
     send_grad = rows_grad.reshape(live_count, slot_count, model_width)
     near_in = lax.all_to_all(send_in, "group", 0, 0, tiled=True)
     near_grad = lax.all_to_all(send_grad, "group", 0, 0, tiled=True)
-    got_in = lax.all_gather(near_in, "member", axis=0, tiled=False)
-    got_grad = lax.all_gather(near_grad, "member", axis=0, tiled=False)
-    members = got_in.shape[0]
-    flat_in = got_in.reshape(-1, model_width)
-    flat_grad = got_grad.reshape(-1, model_width)
-    gate_pre = jnp.dot(flat_in, gate_cols, preferred_element_type=jnp.float32)
-    up_pre = jnp.dot(flat_in, up_cols, preferred_element_type=jnp.float32)
+    near_rows = live_count * slot_count
+    got_in = lax.all_gather(near_in.reshape(near_rows, model_width), "member", axis=0, tiled=True)
+    got_grad = lax.all_gather(near_grad.reshape(near_rows, model_width), "member", axis=0, tiled=True)
+    gate_slice = lax.all_to_all(gate_cols, "member", 0, 1, tiled=True)
+    up_slice = lax.all_to_all(up_cols, "member", 0, 1, tiled=True)
+    members = lax.axis_size("member")
+    gate_pre = jnp.dot(got_in, gate_cols, preferred_element_type=jnp.float32)
+    up_pre = jnp.dot(got_in, up_cols, preferred_element_type=jnp.float32)
     sigma = jax.nn.sigmoid(gate_pre)
     silu_gate = gate_pre * sigma
     hidden = (silu_gate * up_pre).astype(jnp.bfloat16)
     contract = (((1,), (1,)), ((), ()))
     back_hidden = lax.dot_general(
-        flat_grad, down_rows, contract, preferred_element_type=jnp.float32
+        got_grad, down_rows, contract, preferred_element_type=jnp.float32
     )
     grad_gate = (back_hidden * up_pre * sigma * (1.0 + gate_pre * (1.0 - sigma))).astype(
         jnp.bfloat16
     )
     grad_up = (back_hidden * silu_gate).astype(jnp.bfloat16)
-    partial_value = lax.dot_general(
-        grad_gate, gate_cols, contract, preferred_element_type=jnp.float32
+    all_gate = lax.all_gather(grad_gate, "member", axis=1, tiled=True)
+    all_up = lax.all_gather(grad_up, "member", axis=1, tiled=True)
+    slice_value = lax.dot_general(
+        all_gate, gate_slice, contract, preferred_element_type=jnp.float32
     )
-    partial_value = partial_value + lax.dot_general(
-        grad_up, up_cols, contract, preferred_element_type=jnp.float32
+    slice_value = slice_value + lax.dot_general(
+        all_up, up_slice, contract, preferred_element_type=jnp.float32
     )
-    parts = partial_value.astype(jnp.bfloat16).reshape(members, live_count * slot_count, model_width)
     down_part = lax.dot_general(
-        hidden, flat_grad, rows_first, preferred_element_type=jnp.float32
+        hidden, got_grad, rows_first, preferred_element_type=jnp.float32
     ).astype(jnp.bfloat16)
-    blocks = lax.all_to_all(parts, "member", 0, 0, tiled=True)
-    summed = jnp.sum(blocks.astype(jnp.float32), axis=0).reshape(live_count, slot_count, model_width)
+    slice_value = slice_value.reshape(members, near_rows, -1)
+    summed = lax.all_to_all(slice_value, "member", 0, 2, tiled=True)
+    summed = summed.reshape(live_count, slot_count, model_width)
     returned = lax.all_to_all(summed, "group", 0, 0, tiled=True)
     branch = jnp.dot(
         pick_mat.astype(jnp.float32),

time: 616 us -> 591 us (0.959)
  waiting for transfers between devices: 150 us -> 349 us
  blocking collectives: 331 us -> 160 us
  local copies, waits for them, and re-layouts: 64.4 us -> 13.4 us
  matrix products: 49.5 us -> 34.3 us
  starting transfers between devices: 2.02 us -> 17.1 us
    all_to_all x1, blocking collectives: 207 us -> 33.6 us  [body(): summed = lax.all_to_all(slice_value, 'member', 0, 2, tiled=True)]
    all_gather x2 -> x4, waiting for transfers between devices: 150 us -> 288 us  [the longest x1 104 us: body(): lax.all_gather(near_in.reshape(near_rows, model_width), 'member', axis=0,...]
    all_to_all x0 -> x2, waiting for transfers between devices: none -> 59.9 us  [the longest x1 54.4 us: body(): up_slice = lax.all_to_all(up_cols, 'member', 0, 1, tiled=True)]
    all_gather x2 -> x0, local copies, waits for them, and re-layouts: 27.9 us -> none  [the longest x1 13.9 us: body(): got_in = lax.all_gather(near_in, 'member', axis=0, tiled=False)]
    reshape x3, local copies, waits for them, and re-layouts: 30.6 us -> 7.42 us  [the longest x1 2.91 us: body(): summed = summed.reshape(live_count, slot_count, model_width)]
    dot_general x6, matrix products: 43.8 us -> 28.5 us  [the longest x1 6.78 us: body(): up_pre = jnp.dot(got_in, up_cols, preferred_element_type=jnp.float32)]
    all_to_all x0 -> x2, starting transfers between devices: none -> 14.4 us  [the longest x1 7.43 us: body(): up_slice = lax.all_to_all(up_cols, 'member', 0, 1, tiled=True)]
  transfers between devices with their start and end apart: 3 -> 7, of which waited for: 2 -> 7; matrix products, arithmetic and copies ran while one was open for 8% -> 3% of each run, Pallas kernels for 0% -> 0%
where the time goes in v2:
time: 591 us; the launch traced here: 590 us
  waiting for transfers between devices  349 us (59%)
  blocking collectives  160 us (27%)
  matrix products  34.3 us (6%)
  starting transfers between devices  17.1 us (3%)
  between operations  13.9 us (2%)
  local copies, waits for them, and re-layouts  13.4 us (2%)
    all_gather x1, waiting for transfers between devices, body(): lax.all_gather(near_in.reshape(near_rows, model_width), 'member', axis=0,...  104 us
    all_gather x1, waiting for transfers between devices, body(): lax.all_gather(near_grad.reshape(near_rows, model_width), 'member', axis=...  75.4 us
    all_gather x1, waiting for transfers between devices, body(): all_gate = lax.all_gather(grad_gate, 'member', axis=1, tiled=True)  70.2 us
    all_to_all x1, waiting for transfers between devices, body(): up_slice = lax.all_to_all(up_cols, 'member', 0, 1, tiled=True)  54.4 us
    all_to_all x1, blocking collectives, body(): returned = lax.all_to_all(summed, 'group', 0, 0, tiled=True)  53.5 us
    all_gather x1, waiting for transfers between devices, body(): all_up = lax.all_gather(grad_up, 'member', axis=1, tiled=True)  39.1 us
    all_to_all x1, blocking collectives, body(): near_grad = lax.all_to_all(send_grad, 'group', 0, 0, tiled=True)  36.9 us
    all_to_all x1, blocking collectives, body(): near_in = lax.all_to_all(send_in, 'group', 0, 0, tiled=True)  36 us
  transfers between devices with their start and end apart: 7, of which 7 were waited for; matrix products, arithmetic and copies ran while one was open for 3% of the time, Pallas kernels for 0%

profile of v2, /device:TPU:33, one launch (start us, length us, event | category | flops | bytes accessed | tf_op | source)
XLA Modules:
  0.0 590.0 jit_solution(13596407574010233969)
XLA Ops:
  7.2 0.0 copy-start
  7.2 0.0 all-gather.5.cloned.1.call-start
  7.2 0.8 convert_reduce_fusion
  8.1 0.1 copy.31
  8.2 0.2 reduce_window_sum.11
  8.5 0.7 select_reduce_fusion.1
  9.2 0.1 select_reduce_fusion
  9.3 0.1 mul.41
  9.3 1.9 fusion.3
  11.2 0.3 reshape.111
  11.5 36.9 %all_to_all.68 = bf16[8,5,7168]{2,1,0:T(8,128)(2,1)} all-to-all(bf16[8,5,7168]{2,1,0:T(8,128)(2,1)S(1)} %reshape.111), channel_id=1, replica_groups=mesh['pipe'=2,'group'=8,'member'=16] {'group'}, dimensions={0} | all-to-all | bytes 1146880 | tf_op jit(solution)/shard_map/all_to_all | solution.py:49
  48.4 2.3 reshape.112
  50.6 0.0 all-gather.5.cloned.1.call-update
  50.7 0.0 all-gather.7.cloned.1.call-start
  50.7 0.0 copy-done
  50.7 0.4 convolution_convert_fusion.1
  51.1 0.3 reshape.113
  51.4 36.0 %all_to_all.69 = bf16[8,5,7168]{2,1,0:T(8,128)(2,1)} all-to-all(bf16[8,5,7168]{2,1,0:T(8,128)(2,1)S(1)} %reshape.113), channel_id=1, replica_groups=mesh['pipe'=2,'group'=8,'member'=16] {'group'}, dimensions={0} | all-to-all | bytes 1146880 | tf_op jit(solution)/shard_map/all_to_all | solution.py:48
  87.4 2.3 reshape.114
  89.6 0.0 all-gather.7.cloned.1.call-update
  89.6 0.0 all-gather.11.cloned.1.call-start
  89.7 75.4 %all-gather.5.cloned.1.call-done = bf16[640,7168]{1,0:T(8,128)(2,1)} async-done(((bf16[40,7168]{1,0:T(8,128)(2,1)}), bf16[640,7168]{1,0:T(8,128)(2,1)}) %all-gather.5.cloned.1.call-update) | async-done | bytes 9175056 | tf_op jit(solution)/shard_map/all_gather | solution.py:52
  165.1 6.6 %fusion.15 = f32[640,128]{1,0:T(8,128)S(1)} fusion(bf16[640,7168]{1,0:T(8,128)(2,1)} %all-gather.5.cloned.1.call-done, bf16[1,128,7168]{2,1,0:T(8,128)(2,1)} %param.11), kind=kOutput, calls=%fused_computation.19 | convolution fusion | flops 1174405120 | bytes 11337728 | tf_op jit(solution)/shard_map/dot_general | solution.py:62
  171.7 103.7 %all-gather.7.cloned.1.call-done = bf16[640,7168]{1,0:T(8,128)(2,1)} async-done(((bf16[40,7168]{1,0:T(8,128)(2,1)}), bf16[640,7168]{1,0:T(8,128)(2,1)}) %all-gather.7.cloned.1.call-update) | async-done | bytes 9175056 | tf_op jit(solution)/shard_map/all_gather | solution.py:51
  275.5 0.0 copy-start.1
  275.5 0.0 copy-start.3
  275.5 6.8 %fusion.12 = f32[640,128]{1,0:T(8,128)S(1)} fusion(bf16[640,7168]{1,0:T(8,128)(2,1)} %all-gather.7.cloned.1.call-done, bf16[1,7168,128]{2,1,0:T(8,128)(2,1)} %param.10), kind=kOutput, calls=%fused_computation.16 | convolution fusion | flops 1174405120 | bytes 11337728 | tf_op jit(solution)/shard_map/dot_general | solution.py:57
  282.3 0.0 copy-done.1
  282.3 0.5 copy-done.3
  282.8 3.4 multiply_convert_fusion.2
  286.1 0.0 all-gather.11.cloned.1.call-update
  286.2 7.4 %all-to-all-start.3 = ((bf16[16,448,128]{2,1,0:T(8,128)(2,1)}), bf16[16,448,128]{2,1,0:T(8,128)(2,1)}, u32[]{:S(2)}, u32[]{:S(2)}) async-start(bf16[16,448,128]{2,1,0:T(8,128)(2,1)} %bitcast.70), calls=%async_computation.3 | async-start | bytes 3670016 | tf_op jit(solution)/shard_map/all_to_all | solution.py:54
  293.6 0.0 all-gather.9.cloned.1.call-start
  293.6 0.5 all-gather.9.cloned.1.call-update
  294.2 54.4 %all-to-all-done.3 = bf16[16,448,128]{2,1,0:T(8,128)(2,1)} async-done(((bf16[16,448,128]{2,1,0:T(8,128)(2,1)}), bf16[16,448,128]{2,1,0:T(8,128)(2,1)}, u32[]{:S(2)}, u32[]{:S(2)}) %all-to-all-start.3) | async-done | bytes 1835040 | tf_op jit(solution)/shard_map/all_to_all | solution.py:54
  348.6 7.0 %all-to-all-start.2 = ((bf16[16,448,128]{2,1,0:T(8,128)(2,1)}), bf16[16,448,128]{2,1,0:T(8,128)(2,1)}, u32[]{:S(2)}, u32[]{:S(2)}) async-start(bf16[16,448,128]{2,1,0:T(8,128)(2,1)} %bitcast.71), calls=%async_computation.2 | async-start | bytes 3670016 | tf_op jit(solution)/shard_map/all_to_all | solution.py:53
  355.6 39.1 %all-gather.11.cloned.1.call-done = bf16[640,2048]{1,0:T(8,128)(2,1)} async-done(((bf16[640,128]{1,0:T(8,128)(2,1)}), bf16[640,2048]{1,0:T(8,128)(2,1)}) %all-gather.11.cloned.1.call-update) | async-done | bytes 2621456 | tf_op jit(solution)/shard_map/all_gather | solution.py:70
  394.7 3.9 fusion.4
  398.6 5.5 all-to-all-done.2
  404.1 70.2 %all-gather.9.cloned.1.call-done = bf16[640,2048]{1,0:T(8,128)(2,1)} async-done(((bf16[640,128]{1,0:T(8,128)(2,1)}), bf16[640,2048]{1,0:T(8,128)(2,1)}) %all-gather.9.cloned.1.call-update) | async-done | bytes 2621456 | tf_op jit(solution)/shard_map/all_gather | solution.py:69
  474.3 4.9 fusion.18
  479.2 1.7 copy.36
  480.9 33.6 %all_to_all.70 = f32[16,40,448]{2,1,0:T(8,128)S(1)} all-to-all(f32[16,40,448]{2,1,0:T(8,128)S(1)} %bitcast.68), channel_id=1, replica_groups=mesh['pipe'=2,'group'=8,'member'=16] {'member'}, dimensions={0} | all-to-all | bytes 2293760 | tf_op jit(solution)/shard_map/all_to_all | solution.py:81
  514.5 0.0 slice-start
  514.5 1.8 copy.37
  516.3 2.9 reshape.116
  519.2 0.0 slice-start.1
  519.2 53.5 %all_to_all.71 = f32[8,5,7168]{2,1,0:T(8,128)S(1)} all-to-all(f32[8,5,7168]{2,1,0:T(8,128)} %reshape.116), channel_id=1, replica_groups=mesh['pipe'=2,'group'=8,'member'=16] {'group'}, dimensions={0} | all-to-all | bytes 2293760 | tf_op jit(solution)/shard_map/all_to_all | solution.py:83
  572.7 0.0 slice-start.2
  572.7 0.0 copy-start.2
  572.7 3.6 fusion.1
  576.3 2.6 collective-permute-start
  578.9 0.0 slice-done
  578.9 0.0 slice-done.1
  578.9 0.0 slice-done.2
  578.9 0.0 copy-done.2
  578.9 2.9 fusion.2
  581.8 0.5 collective-permute-done
  582.3 1.2 copy.51
  (6 shorter events, 0.1 us)
Async XLA Ops:
  7.2 43.5 %copy-start = (bf16[1,128,7168]{2,1,0:T(8,128)(2,1)S(1)}, bf16[1,128,7168]{2,1,0:T(8,128)(2,1)}, u32[]{:S(2)}) copy-start(bf16[1,128,7168]{2,1,0:T(8,128)(2,1)} %param.7) | copy-start | bytes 5505028
  7.2 157.9 %all-gather.5.cloned.1.call-start = ((), (), s32[]{:S(2)}) async-start(), calls=%async_computation.6 | async-start | bytes 9748480 | tf_op jit(solution)/shard_map/all_gather | solution.py:52
  50.7 224.8 %all-gather.7.cloned.1.call-start = ((), (), s32[]{:S(2)}) async-start(), calls=%async_computation.7 | async-start | bytes 9748480 | tf_op jit(solution)/shard_map/all_gather | solution.py:51
  89.6 305.0 %all-gather.11.cloned.1.call-start = ((), (), s32[]{:S(2)}) async-start(), calls=%async_computation.9 | async-start | bytes 2785280 | tf_op jit(solution)/shard_map/all_gather | solution.py:70
  275.5 6.8 %copy-start.1 = (bf16[1,7168,128]{2,1,0:T(8,128)(2,1)S(1)}, bf16[1,7168,128]{2,1,0:T(8,128)(2,1)}, u32[]{:S(2)}) copy-start(bf16[1,7168,128]{2,1,0:T(8,128)(2,1)} %param.9) | copy-start | bytes 5505028
  275.5 7.3 %copy-start.3 = (bf16[640,7168]{1,0:T(8,128)(2,1)S(1)}, bf16[640,7168]{1,0:T(8,128)(2,1)}, u32[]{:S(2)}) copy-start(bf16[640,7168]{1,0:T(8,128)(2,1)} %all-gather.7.cloned.1.call-done) | copy-start | bytes 27525124
  286.2 62.4 %all-to-all-start.3 = ((bf16[16,448,128]{2,1,0:T(8,128)(2,1)}), bf16[16,448,128]{2,1,0:T(8,128)(2,1)}, u32[]{:S(2)}, u32[]{:S(2)}) async-start(bf16[16,448,128]{2,1,0:T(8,128)(2,1)} %bitcast.70), calls=%async_computation.3 | async-start | bytes 3670016 | tf_op jit(solution)/shard_map/all_to_all | solution.py:54
  293.6 180.7 %all-gather.9.cloned.1.call-start = ((), (), s32[]{:S(2)}) async-start(), calls=%async_computation.8 | async-start | bytes 2785280 | tf_op jit(solution)/shard_map/all_gather | solution.py:69
  348.6 55.5 %all-to-all-start.2 = ((bf16[16,448,128]{2,1,0:T(8,128)(2,1)}), bf16[16,448,128]{2,1,0:T(8,128)(2,1)}, u32[]{:S(2)}, u32[]{:S(2)}) async-start(bf16[16,448,128]{2,1,0:T(8,128)(2,1)} %bitcast.71), calls=%async_computation.2 | async-start | bytes 3670016 | tf_op jit(solution)/shard_map/all_to_all | solution.py:53
  514.5 64.4 %slice-start = ((s8[9175040]{0:T(1024)(128)(4,1)}), s8[786432]{0:T(1024)(128)(4,1)S(1)}, s32[]{:S(2)}) async-start(s8[9175040]{0:T(1024)(128)(4,1)} %bitcast.66), calls=%async_computation.10 | async-start | bytes 1572864
  519.2 59.7 %slice-start.1 = ((s8[9175040]{0:T(1024)(128)(4,1)}), s8[4194304]{0:T(1024)(128)(4,1)S(1)}, s32[]{:S(2)}) async-start(s8[9175040]{0:T(1024)(128)(4,1)} %bitcast.66), calls=%async_computation.11 | async-start | bytes 8388608
  572.7 6.2 %slice-start.2 = ((s8[9175040]{0:T(1024)(128)(4,1)}), s8[4194304]{0:T(1024)(128)(4,1)S(1)}, s32[]{:S(2)}) async-start(s8[9175040]{0:T(1024)(128)(4,1)} %bitcast.66), calls=%async_computation.12 | async-start | bytes 8388608
  572.7 6.2 %copy-start.2 = (f32[640,128]{1,0:T(8,128)S(1)}, f32[640,128]{1,0:T(8,128)}, u32[]{:S(2)}) copy-start(f32[640,128]{1,0:T(8,128)} %get-tuple-element.4) | copy-start | bytes 983044
  576.3 6.0 %collective-permute-start = (bf16[128,7168]{1,0:T(8,128)(2,1)S(1)}, bf16[128,7168]{1,0:T(8,128)(2,1)S(1)}, u32[]{:S(2)}, u32[]{:S(2)}) collective-permute-start(bf16[128,7168]{1,0:T(8,128)(2,1)S(1)} %fusion.1), channel_id=1, source_target_pairs={{0,128},{128,0},{1,129},{129,1},{2,130},{130,2},{3,131},{131,3},{4... | collective-permute-start | bytes 5505032 | tf_op jit(solution)/shard_map/ppermute | solution.py:14
Sparse Core Ops, SparseCore 0:
  50.8 114.2 all-gather.4
  167.5 107.9 all-gather.6
  286.3 108.3 all-gather.10
  396.8 77.4 all-gather.8

commit v3 on v2

--- a/solution.py
+++ b/solution.py
@@ -43,16 +43,24 @@
         live_count * slot_count, 1
     )
     rows_grad = (chosen_grads * slot_gate).astype(jnp.bfloat16)
-    send_in = rows_in.reshape(live_count, slot_count, model_width)
-    send_grad = rows_grad.reshape(live_count, slot_count, model_width)
-    near_in = lax.all_to_all(send_in, "group", 0, 0, tiled=True)
-    near_grad = lax.all_to_all(send_grad, "group", 0, 0, tiled=True)
+    send = jnp.concatenate(
+        [
+            rows_in.reshape(live_count, slot_count, model_width),
+            rows_grad.reshape(live_count, slot_count, model_width),
+        ],
+        axis=1,
+    )
+    near = lax.all_to_all(send, "group", 0, 0, tiled=True)
     near_rows = live_count * slot_count
-    got_in = lax.all_gather(near_in.reshape(near_rows, model_width), "member", axis=0, tiled=True)
-    got_grad = lax.all_gather(near_grad.reshape(near_rows, model_width), "member", axis=0, tiled=True)
-    gate_slice = lax.all_to_all(gate_cols, "member", 0, 1, tiled=True)
-    up_slice = lax.all_to_all(up_cols, "member", 0, 1, tiled=True)
+    near_in = near[:, :slot_count].reshape(near_rows, model_width)
+    near_grad = near[:, slot_count:].reshape(near_rows, model_width)
+    got_in = lax.all_gather(near_in, "member", axis=0, tiled=True)
+    got_grad = lax.all_gather(near_grad, "member", axis=0, tiled=True)
+    both_cols = jnp.concatenate([gate_cols, up_cols], axis=1)
+    both_slice = lax.all_to_all(both_cols, "member", 0, 1, tiled=True)
+    both_slice, got_in = lax.optimization_barrier((both_slice, got_in))
     members = lax.axis_size("member")
+    groups = live_count
     gate_pre = jnp.dot(got_in, gate_cols, preferred_element_type=jnp.float32)
     up_pre = jnp.dot(got_in, up_cols, preferred_element_type=jnp.float32)
     sigma = jax.nn.sigmoid(gate_pre)
@@ -66,24 +74,25 @@
         jnp.bfloat16
     )
     grad_up = (back_hidden * silu_gate).astype(jnp.bfloat16)
-    all_gate = lax.all_gather(grad_gate, "member", axis=1, tiled=True)
-    all_up = lax.all_gather(grad_up, "member", axis=1, tiled=True)
+    both_grad = jnp.concatenate([grad_gate, grad_up], axis=1)
+    all_grad = lax.all_gather(both_grad, "member", axis=1, tiled=True)
     slice_value = lax.dot_general(
-        all_gate, gate_slice, contract, preferred_element_type=jnp.float32
-    )
-    slice_value = slice_value + lax.dot_general(
-        all_up, up_slice, contract, preferred_element_type=jnp.float32
+        all_grad, both_slice, contract, preferred_element_type=jnp.float32
     )
     down_part = lax.dot_general(
         hidden, got_grad, rows_first, preferred_element_type=jnp.float32
     ).astype(jnp.bfloat16)
-    slice_value = slice_value.reshape(members, near_rows, -1)
-    summed = lax.all_to_all(slice_value, "member", 0, 2, tiled=True)
-    summed = summed.reshape(live_count, slot_count, model_width)
-    returned = lax.all_to_all(summed, "group", 0, 0, tiled=True)
+    slice_width = slice_value.shape[1]
+    slice_value = slice_value.reshape(members, groups, slot_count, slice_width)
+    slice_value = jnp.transpose(slice_value, (1, 0, 2, 3)).reshape(
+        groups * members, slot_count, slice_width
+    )
+    back = lax.all_to_all(slice_value, ("group", "member"), 0, 0, tiled=True)
+    back = back.reshape(groups, members, slot_count, slice_width)
+    returned = jnp.transpose(back, (0, 2, 1, 3)).reshape(groups * slot_count, model_width)
     branch = jnp.dot(
         pick_mat.astype(jnp.float32),
-        returned.reshape(live_count * slot_count, model_width),
+        returned,
         preferred_element_type=jnp.float32,
         precision=lax.Precision.HIGHEST,
     )

time: 591 us -> 554 us (0.937)
  waiting for transfers between devices: 349 us -> 176 us
  blocking collectives: 160 us -> 292 us
    all_to_all x4 -> x3, blocking collectives: 160 us -> 292 us  [the longest x1 180 us: body(): both_slice = lax.all_to_all(both_cols, 'member', 0, 1, tiled=True)]
    all_gather x4 -> x3, waiting for transfers between devices: 288 us -> 176 us  [the longest x1 98.4 us: body(): got_grad = lax.all_gather(near_grad, 'member', axis=0, tiled=True)]
    all_to_all x2 -> x0, waiting for transfers between devices: 59.9 us -> none  [the longest x1 54.4 us: body(): up_slice = lax.all_to_all(up_cols, 'member', 0, 1, tiled=True)]
    all_to_all x2 -> x0, starting transfers between devices: 14.4 us -> none  [the longest x1 7.43 us: body(): up_slice = lax.all_to_all(up_cols, 'member', 0, 1, tiled=True)]
    ppermute x1, starting transfers between devices: 2.55 us -> 12.1 us  [from_behind(): return lax.ppermute(value, axis, pairs)]
    dot_general x3 -> x2, matrix products: 12.4 us -> 9.6 us  [the longest x1 6.53 us: body(): lax.dot_general(all_grad, both_slice, contract, preferred_element_type=jn...]
  transfers between devices with their start and end apart: 7 -> 4, of which waited for: 7 -> 2; matrix products, arithmetic and copies ran while one was open for 3% -> 3% of each run, Pallas kernels for 0% -> 0%
where the time goes in v3:
time: 554 us; the launch traced here: 552 us
  blocking collectives  292 us (53%)
  waiting for transfers between devices  176 us (32%)
  matrix products  35.5 us (6%)
  local copies, waits for them, and re-layouts  17.2 us (3%)
  between operations  13.9 us (3%)
  starting transfers between devices  12.3 us (2%)
    all_to_all x1, blocking collectives, body(): both_slice = lax.all_to_all(both_cols, 'member', 0, 1, tiled=True)  180 us
    all_gather x1, waiting for transfers between devices, body(): got_grad = lax.all_gather(near_grad, 'member', axis=0, tiled=True)  98.4 us
    all_gather x1, waiting for transfers between devices, body(): all_grad = lax.all_gather(both_grad, 'member', axis=1, tiled=True)  77.2 us
    all_to_all x1, blocking collectives, body(): near = lax.all_to_all(send, 'group', 0, 0, tiled=True)  56.4 us
    all_to_all x1, blocking collectives, body(): back = lax.all_to_all(slice_value, ('group', 'member'), 0, 0, tiled=True)  55.5 us
    ppermute x1, starting transfers between devices, from_behind(): return lax.ppermute(value, axis, pairs)  12.1 us
  transfers between devices with their start and end apart: 4, of which 2 were waited for; matrix products, arithmetic and copies ran while one was open for 3% of the time, Pallas kernels for 0%

profile of v3, /device:TPU:33, one launch (start us, length us, event | category | flops | bytes accessed | tf_op | source)
XLA Modules:
  0.0 552.1 jit_solution(11650318825989745081)
XLA Ops:
  7.2 0.0 copy-start
  7.2 0.0 all-gather.6.cloned.1.call-start
  7.2 0.8 convert_reduce_fusion
  8.1 0.1 copy.29
  8.2 0.2 reduce_window_sum.11
  8.5 0.7 select_reduce_fusion.1
  9.2 0.1 select_reduce_fusion
  9.3 0.1 mul.41
  9.4 1.9 fusion.2
  11.2 0.3 reshape.139
  11.5 0.0 copy-done
  11.5 0.4 convolution_convert_fusion.1
  11.9 0.3 reshape.138
  12.2 0.6 pad_maximum_fusion.1
  12.8 56.4 %all_to_all.26 = bf16[8,10,7168]{2,1,0:T(8,128)(2,1)S(1)} all-to-all(bf16[8,10,7168]{2,1,0:T(8,128)(2,1)S(1)} %pad_maximum_fusion.1), channel_id=1, replica_groups=mesh['pipe'=2,'group'=8,'member'=16] {'group'}, dimensions={0} | all-to-all | bytes 2293760 | tf_op jit(solution)/shard_map/all_to_all | solution.py:53
  69.2 1.3 fusion.15
  70.5 0.0 copy-start.3
  70.5 2.4 reshape.141
  72.9 0.0 all-gather.6.cloned.1.call-update
  72.9 0.0 all-gather.4.cloned.1.call-start
  72.9 1.1 reshape.140
  74.0 0.0 all-gather.4.cloned.1.call-update
  74.0 0.0 all-gather.8.cloned.1.call-start
  74.1 0.0 copy-done.3
  74.1 2.0 pad_maximum_fusion
  76.1 180.4 %all_to_all.27 = bf16[16,448,256]{2,1,0:T(8,128)(2,1)S(1)} all-to-all(bf16[16,448,256]{2,1,0:T(8,128)(2,1)S(1)} %pad_maximum_fusion), channel_id=1, replica_groups=mesh['pipe'=2,'group'=8,'member'=16] {'member'}, dimensions={0} | all-to-all | bytes 7340032 | tf_op jit(solution)/shard_map/all_to_all | solution.py:60
  256.5 2.3 copy.38
  258.8 0.0 all-gather.6.cloned.1.call-done
  258.8 6.4 %fusion.5 = f32[640,128]{0,1:T(8,128)S(1)} fusion(bf16[640,7168]{1,0:T(8,128)(2,1)} %all-gather.6.cloned.1.call-done, bf16[1,7168,128]{2,1,0:T(8,128)(2,1)S(1)} %copy-done.3), kind=kOutput, calls=%fused_computation.11 | convolution fusion | flops 1174405120 | bytes 11337728 | tf_op jit(solution)/shard_map/dot_general | solution.py:65
  265.2 0.0 copy-start.4
  265.2 98.4 %all-gather.4.cloned.1.call-done = bf16[640,7168]{1,0:T(8,128)(2,1)} async-done(((bf16[40,7168]{1,0:T(8,128)(2,1)}), bf16[640,7168]{1,0:T(8,128)(2,1)}) %all-gather.4.cloned.1.call-update) | async-done | bytes 9175056 | tf_op jit(solution)/shard_map/all_gather | solution.py:58
  363.6 0.0 copy-start.2
  363.6 7.2 %fusion.7 = f32[640,128]{0,1:T(8,128)S(1)} fusion(bf16[640,7168]{1,0:T(8,128)(2,1)} %all-gather.4.cloned.1.call-done, bf16[1,128,7168]{2,1,0:T(8,128)(2,1)} %param.11), kind=kOutput, calls=%fused_computation.13 | convolution fusion | flops 1174405120 | bytes 11337728 | tf_op jit(solution)/shard_map/dot_general | solution.py:70
  370.8 0.0 copy-done.4
  370.8 0.0 copy-done.2
  370.8 3.7 multiply_convert_fusion.2
  374.5 0.8 pad_maximum_fusion.2
  375.2 0.0 all-gather.8.cloned.1.call-update
  375.3 77.2 %all-gather.8.cloned.1.call-done = bf16[640,4096]{0,1:T(8,128)(2,1)} async-done(((bf16[640,256]{0,1:T(8,128)(2,1)}), bf16[640,4096]{0,1:T(8,128)(2,1)}) %all-gather.8.cloned.1.call-update) | async-done | bytes 5242896 | tf_op jit(solution)/shard_map/all_gather | solution.py:78
  452.4 6.5 %fusion.16 = f32[640,448]{1,0:T(8,128)S(1)} fusion(bf16[640,4096]{0,1:T(8,128)(2,1)} %all-gather.8.cloned.1.call-done, bf16[448,4096]{1,0:T(8,128)(2,1)} %bitcast.55), kind=kOutput, calls=%fused_computation.33 | convolution fusion | flops 2348810240 | bytes 10059776 | tf_op jit(solution)/shard_map/dot_general | solution.py:79
  458.9 1.6 reshape.142
  460.5 2.4 copy.34
  462.9 1.0 copy.35
  463.9 55.5 %all_to_all.28 = f32[128,5,448]{2,1,0:T(8,128)S(1)} all-to-all(f32[128,5,448]{2,1,0:T(8,128)S(1)} %copy.35), channel_id=1, replica_groups=mesh['pipe'=2,'group'=8,'member'=16] {'group','member'}, dimensions={0} | all-to-all | bytes 2293760 | tf_op jit(solution)/shard_map/all_to_all | solution.py:90
  519.4 0.8 copy.40
  520.2 0.0 copy-start.5
  520.2 1.5 reshape.145
  521.7 0.0 copy-done.5
  521.7 0.0 copy-start.6
  521.7 3.1 fusion
  524.8 12.1 %collective-permute-start = (bf16[128,7168]{1,0:T(8,128)(2,1)S(1)}, bf16[128,7168]{1,0:T(8,128)(2,1)S(1)}, u32[]{:S(2)}, u32[]{:S(2)}) collective-permute-start(bf16[128,7168]{1,0:T(8,128)(2,1)S(1)} %fusion), channel_id=1, source_target_pairs={{0,128},{128,0},{1,129},{129,1},{2,130},{130,2},{3,131},{131,3},{4... | collective-permute-start | bytes 5505032 | tf_op jit(solution)/shard_map/ppermute | solution.py:14
  537.0 0.0 copy-done.6
  537.0 6.5 %fusion.1 = bf16[1,128,7168]{2,1,0:T(8,128)(2,1)} fusion(bf16[640,7168]{1,0:T(8,128)(2,1)} %all-gather.4.cloned.1.call-done, f32[640,128]{0,1:T(8,128)S(1)} %fusion.5, f32[640,128]{0,1:T(8,128)S(1)} %copy-done.6), kind=kOutput, calls=%fused_computation.3 | convolution fusion | flops 1175814144 | bytes 11665408 | tf_op jit(solution)/shard_map/dot_general | solution.py:82
  543.4 0.0 collective-permute-done
  543.4 0.0 copy-start.1
  543.4 1.2 copy.42
  544.6 0.9 copy-done.1
  (5 shorter events, 0.1 us)
Async XLA Ops:
  7.2 4.3 copy-start
  7.2 251.6 %all-gather.6.cloned.1.call-start = ((), (), s32[]{:S(2)}) async-start(), calls=%async_computation.4 | async-start | bytes 9748480 | tf_op jit(solution)/shard_map/all_gather | solution.py:57
  70.5 3.6 copy-start.3
  72.9 290.7 %all-gather.4.cloned.1.call-start = ((), (), s32[]{:S(2)}) async-start(), calls=%async_computation.3 | async-start | bytes 9748480 | tf_op jit(solution)/shard_map/all_gather | solution.py:58
  74.0 378.4 %all-gather.8.cloned.1.call-start = ((), (), s32[]{:S(2)}) async-start(), calls=%async_computation.5 | async-start | bytes 5570560 | tf_op jit(solution)/shard_map/all_gather | solution.py:78
  265.2 105.6 %copy-start.4 = (bf16[1,7168,128]{2,1,0:T(8,128)(2,1)S(1)}, bf16[1,7168,128]{2,1,0:T(8,128)(2,1)}, u32[]{:S(2)}) copy-start(bf16[1,7168,128]{2,1,0:T(8,128)(2,1)} %param.9) | copy-start | bytes 5505028
  363.6 7.2 %copy-start.2 = (bf16[640,7168]{1,0:T(8,128)(2,1)S(1)}, bf16[640,7168]{1,0:T(8,128)(2,1)}, u32[]{:S(2)}) copy-start(bf16[640,7168]{1,0:T(8,128)(2,1)} %all-gather.6.cloned.1.call-done) | copy-start | bytes 27525124
  520.2 1.6 copy-start.5
  521.7 15.2 %copy-start.6 = (f32[640,128]{0,1:T(8,128)S(1)}, f32[640,128]{0,1:T(8,128)}, u32[]{:S(2)}) copy-start(f32[640,128]{0,1:T(8,128)} %get-tuple-element.10) | copy-start | bytes 983044
  524.8 18.6 %collective-permute-start = (bf16[128,7168]{1,0:T(8,128)(2,1)S(1)}, bf16[128,7168]{1,0:T(8,128)(2,1)S(1)}, u32[]{:S(2)}, u32[]{:S(2)}) collective-permute-start(bf16[128,7168]{1,0:T(8,128)(2,1)S(1)} %fusion), channel_id=1, source_target_pairs={{0,128},{128,0},{1,129},{129,1},{2,130},{130,2},{3,131},{131,3},{4... | collective-permute-start | bytes 5505032 | tf_op jit(solution)/shard_map/ppermute | solution.py:14
  543.4 2.2 copy-start.1
Sparse Core Ops, SparseCore 0:
  73.0 176.1 all-gather.5
  251.6 111.9 all-gather.3
  375.4 76.9 all-gather.7

commit v4 on v3

--- a/solution.py
+++ b/solution.py
@@ -43,6 +43,9 @@
         live_count * slot_count, 1
     )
     rows_grad = (chosen_grads * slot_gate).astype(jnp.bfloat16)
+    both_cols = jnp.concatenate([gate_cols, up_cols], axis=1)
+    both_slice = lax.all_to_all(both_cols, "member", 0, 1, tiled=True)
+    both_slice, rows_in, rows_grad = lax.optimization_barrier((both_slice, rows_in, rows_grad))
     send = jnp.concatenate(
         [
             rows_in.reshape(live_count, slot_count, model_width),
@@ -56,9 +59,6 @@
     near_grad = near[:, slot_count:].reshape(near_rows, model_width)
     got_in = lax.all_gather(near_in, "member", axis=0, tiled=True)
     got_grad = lax.all_gather(near_grad, "member", axis=0, tiled=True)
-    both_cols = jnp.concatenate([gate_cols, up_cols], axis=1)
-    both_slice = lax.all_to_all(both_cols, "member", 0, 1, tiled=True)
-    both_slice, got_in = lax.optimization_barrier((both_slice, got_in))
     members = lax.axis_size("member")
     groups = live_count
     gate_pre = jnp.dot(got_in, gate_cols, preferred_element_type=jnp.float32)

time: 554 us -> 568 us (1.025)
  waiting for transfers between devices: 176 us -> 361 us
  blocking collectives: 292 us -> 110 us
  starting transfers between devices: 12.3 us -> 20.7 us
    all_to_all x1 -> x0, blocking collectives: 180 us -> none  [body(): both_slice = lax.all_to_all(both_cols, 'member', 0, 1, tiled=True)]
    all_gather x1, waiting for transfers between devices: 0.01 us -> 105 us  [body(): got_in = lax.all_gather(near_in, 'member', axis=0, tiled=True)]
    all_to_all x0 -> x1, waiting for transfers between devices: none -> 75.5 us  [body(): both_slice = lax.all_to_all(both_cols, 'member', 0, 1, tiled=True)]
    all_to_all x0 -> x1, starting transfers between devices: none -> 8.22 us  [body(): both_slice = lax.all_to_all(both_cols, 'member', 0, 1, tiled=True)]
  transfers between devices with their start and end apart: 4 -> 5, of which waited for: 2 -> 4; matrix products, arithmetic and copies ran while one was open for 3% -> 3% of each run, Pallas kernels for 0% -> 0%
where the time goes in v4:
time: 568 us; the launch traced here: 566 us
  waiting for transfers between devices  361 us (64%)
  blocking collectives  110 us (19%)
  matrix products  34 us (6%)
  starting transfers between devices  20.7 us (4%)
  local copies, waits for them, and re-layouts  20.2 us (4%)
  between operations  13.9 us (2%)
  other arithmetic  6.21 us (1%)
    all_gather x1, waiting for transfers between devices, body(): got_in = lax.all_gather(near_in, 'member', axis=0, tiled=True)  105 us
    all_gather x1, waiting for transfers between devices, body(): got_grad = lax.all_gather(near_grad, 'member', axis=0, tiled=True)  103 us
    all_gather x1, waiting for transfers between devices, body(): all_grad = lax.all_gather(both_grad, 'member', axis=1, tiled=True)  77.2 us
    all_to_all x1, waiting for transfers between devices, body(): both_slice = lax.all_to_all(both_cols, 'member', 0, 1, tiled=True)  75.5 us
    all_to_all x1, blocking collectives, body(): back = lax.all_to_all(slice_value, ('group', 'member'), 0, 0, tiled=True)  55.7 us
    all_to_all x1, blocking collectives, body(): near = lax.all_to_all(send, 'group', 0, 0, tiled=True)  54.7 us
    ppermute x1, starting transfers between devices, from_behind(): return lax.ppermute(value, axis, pairs)  12.1 us
  transfers between devices with their start and end apart: 5, of which 4 were waited for; matrix products, arithmetic and copies ran while one was open for 3% of the time, Pallas kernels for 0%

profile of v4, /device:TPU:33, one launch (start us, length us, event | category | flops | bytes accessed | tf_op | source)
XLA Modules:
  0.0 566.2 jit_solution(4415604724928915688)
XLA Ops:
  7.2 0.0 copy-start
  7.2 4.5 pad_maximum_fusion
  11.7 0.0 copy-start.8
  11.7 0.0 copy-start.9
  11.7 8.2 %all-to-all-start = ((bf16[16,448,256]{2,1,0:T(8,128)(2,1)}), bf16[16,448,256]{2,1,0:T(8,128)(2,1)}, u32[]{:S(2)}, u32[]{:S(2)}) async-start(bf16[16,448,256]{2,1,0:T(8,128)(2,1)} %pad_maximum_fusion), calls=%async_computation | async-start | bytes 7340032 | tf_op jit(solution)/shard_map/all_to_all | solution.py:47
  19.9 0.0 all-gather.6.cloned.1.call-start
  20.0 0.0 copy-done.8
  20.0 0.1 copy.29
  20.1 0.2 reduce_window_sum.11
  20.3 0.0 copy-done.9
  20.4 0.1 select_reduce_fusion
  20.5 0.1 mul.41
  20.6 0.0 copy-done
  20.6 0.0 copy-start.5
  20.6 0.4 convolution_convert_fusion.1
  21.0 1.1 copy-done.5
  22.1 0.4 fusion.2
  22.5 75.5 %all-to-all-done = bf16[16,448,256]{2,1,0:T(8,128)(2,1)} async-done(((bf16[16,448,256]{2,1,0:T(8,128)(2,1)}), bf16[16,448,256]{2,1,0:T(8,128)(2,1)}, u32[]{:S(2)}, u32[]{:S(2)}) %all-to-all-start) | async-done | bytes 3670048 | tf_op jit(solution)/shard_map/all_to_all | solution.py:47
  98.0 4.4 copy.38
  102.4 0.3 reshape.138
  102.6 0.3 reshape.139
  102.9 0.6 pad_maximum_fusion.1
  103.5 54.7 %all_to_all.26 = bf16[8,10,7168]{2,1,0:T(8,128)(2,1)S(1)} all-to-all(bf16[8,10,7168]{2,1,0:T(8,128)(2,1)S(1)} %pad_maximum_fusion.1), channel_id=1, replica_groups=mesh['pipe'=2,'group'=8,'member'=16] {'group'}, dimensions={0} | all-to-all | bytes 2293760 | tf_op jit(solution)/shard_map/all_to_all | solution.py:56
  158.2 1.3 fusion.15
  159.5 0.0 copy-start.3
  159.5 2.4 reshape.141
  161.9 0.0 all-gather.6.cloned.1.call-update
  161.9 0.0 all-gather.4.cloned.1.call-start
  162.0 1.1 reshape.140
  163.0 0.0 all-gather.4.cloned.1.call-update
  163.1 0.2 all-gather.8.cloned.1.call-start
  163.3 104.9 %all-gather.6.cloned.1.call-done = bf16[640,7168]{1,0:T(8,128)(2,1)} async-done(((bf16[40,7168]{1,0:T(8,128)(2,1)}), bf16[640,7168]{1,0:T(8,128)(2,1)}) %all-gather.6.cloned.1.call-update) | async-done | bytes 9175056 | tf_op jit(solution)/shard_map/all_gather | solution.py:60
  268.2 0.0 copy-done.3
  268.2 6.4 %fusion.5 = f32[640,128]{0,1:T(8,128)S(1)} fusion(bf16[640,7168]{1,0:T(8,128)(2,1)} %all-gather.6.cloned.1.call-done, bf16[1,7168,128]{2,1,0:T(8,128)(2,1)S(1)} %copy-done.3), kind=kOutput, calls=%fused_computation.11 | convolution fusion | flops 1174405120 | bytes 11337728 | tf_op jit(solution)/shard_map/dot_general | solution.py:65
  274.6 0.0 copy-start.4
  274.6 103.1 %all-gather.4.cloned.1.call-done = bf16[640,7168]{1,0:T(8,128)(2,1)} async-done(((bf16[40,7168]{1,0:T(8,128)(2,1)}), bf16[640,7168]{1,0:T(8,128)(2,1)}) %all-gather.4.cloned.1.call-update) | async-done | bytes 9175056 | tf_op jit(solution)/shard_map/all_gather | solution.py:61
  377.7 0.0 copy-start.2
  377.7 7.2 %fusion.7 = f32[640,128]{0,1:T(8,128)S(1)} fusion(bf16[640,7168]{1,0:T(8,128)(2,1)} %all-gather.4.cloned.1.call-done, bf16[1,128,7168]{2,1,0:T(8,128)(2,1)} %param.11), kind=kOutput, calls=%fused_computation.13 | convolution fusion | flops 1174405120 | bytes 11337728 | tf_op jit(solution)/shard_map/dot_general | solution.py:70
  384.9 0.0 copy-done.4
  384.9 0.0 copy-done.2
  384.9 3.7 multiply_convert_fusion.2
  388.5 0.8 pad_maximum_fusion.2
  389.3 0.0 all-gather.8.cloned.1.call-update
  389.3 77.2 %all-gather.8.cloned.1.call-done = bf16[640,4096]{0,1:T(8,128)(2,1)} async-done(((bf16[640,256]{0,1:T(8,128)(2,1)}), bf16[640,4096]{0,1:T(8,128)(2,1)}) %all-gather.8.cloned.1.call-update) | async-done | bytes 5242896 | tf_op jit(solution)/shard_map/all_gather | solution.py:78
  466.5 6.5 %fusion.16 = f32[640,448]{1,0:T(8,128)S(1)} fusion(bf16[640,4096]{0,1:T(8,128)(2,1)} %all-gather.8.cloned.1.call-done, bf16[448,4096]{1,0:T(8,128)(2,1)} %bitcast.54), kind=kOutput, calls=%fused_computation.33 | convolution fusion | flops 2348810240 | bytes 10059776 | tf_op jit(solution)/shard_map/dot_general | solution.py:79
  473.0 1.6 reshape.142
  474.6 2.4 copy.34
  476.9 0.8 copy.35
  477.7 55.7 %all_to_all.27 = f32[128,5,448]{2,1,0:T(8,128)S(1)} all-to-all(f32[128,5,448]{2,1,0:T(8,128)S(1)} %copy.35), channel_id=1, replica_groups=mesh['pipe'=2,'group'=8,'member'=16] {'group','member'}, dimensions={0} | all-to-all | bytes 2293760 | tf_op jit(solution)/shard_map/all_to_all | solution.py:90
  533.5 0.8 copy.40
  534.2 0.0 copy-start.6
  534.3 1.5 reshape.145
  535.8 0.0 copy-done.6
  535.8 0.0 copy-start.7
  535.8 3.1 fusion
  538.9 12.1 %collective-permute-start = (bf16[128,7168]{1,0:T(8,128)(2,1)S(1)}, bf16[128,7168]{1,0:T(8,128)(2,1)S(1)}, u32[]{:S(2)}, u32[]{:S(2)}) collective-permute-start(bf16[128,7168]{1,0:T(8,128)(2,1)S(1)} %fusion), channel_id=1, source_target_pairs={{0,128},{128,0},{1,129},{129,1},{2,130},{130,2},{3,131},{131,3},{4... | collective-permute-start | bytes 5505032 | tf_op jit(solution)/shard_map/ppermute | solution.py:14
  551.0 0.0 copy-done.7
  551.0 6.5 %fusion.1 = bf16[1,128,7168]{2,1,0:T(8,128)(2,1)} fusion(bf16[640,7168]{1,0:T(8,128)(2,1)} %all-gather.4.cloned.1.call-done, f32[640,128]{0,1:T(8,128)S(1)} %fusion.5, f32[640,128]{0,1:T(8,128)S(1)} %copy-done.7), kind=kOutput, calls=%fused_computation.3 | convolution fusion | flops 1175814144 | bytes 11665408 | tf_op jit(solution)/shard_map/dot_general | solution.py:82
  557.5 0.0 collective-permute-done
  557.5 0.0 copy-start.1
  557.5 1.2 copy.42
  558.7 0.9 copy-done.1
  (7 shorter events, 0.1 us)
Async XLA Ops:
  7.2 13.4 %copy-start = (bf16[1,128,7168]{2,1,0:T(8,128)(2,1)S(1)}, bf16[1,128,7168]{2,1,0:T(8,128)(2,1)}, u32[]{:S(2)}) copy-start(bf16[1,128,7168]{2,1,0:T(8,128)(2,1)} %param.7) | copy-start | bytes 5505028
  11.7 8.3 %copy-start.8 = (s32[1,128,8]{1,2,0:T(8,128)S(1)}, s32[1,128,8]{1,2,0:T(8,128)}, u32[]{:S(2)}) copy-start(s32[1,128,8]{1,2,0:T(8,128)} %param.12) | copy-start | bytes 12292
  11.7 8.6 %copy-start.9 = (f32[1,128,8]{1,2,0:T(8,128)S(1)}, f32[1,128,8]{1,2,0:T(8,128)}, u32[]{:S(2)}) copy-start(f32[1,128,8]{1,2,0:T(8,128)} %param.13) | copy-start | bytes 12292
  11.7 86.3 %all-to-all-start = ((bf16[16,448,256]{2,1,0:T(8,128)(2,1)}), bf16[16,448,256]{2,1,0:T(8,128)(2,1)}, u32[]{:S(2)}, u32[]{:S(2)}) async-start(bf16[16,448,256]{2,1,0:T(8,128)(2,1)} %pad_maximum_fusion), calls=%async_computation | async-start | bytes 7340032 | tf_op jit(solution)/shard_map/all_to_all | solution.py:47
  19.9 248.2 %all-gather.6.cloned.1.call-start = ((), (), s32[]{:S(2)}) async-start(), calls=%async_computation.4 | async-start | bytes 9748480 | tf_op jit(solution)/shard_map/all_gather | solution.py:60
  20.6 1.5 copy-start.5
  159.5 108.7 %copy-start.3 = (bf16[1,7168,128]{2,1,0:T(8,128)(2,1)S(1)}, bf16[1,7168,128]{2,1,0:T(8,128)(2,1)}, u32[]{:S(2)}) copy-start(bf16[1,7168,128]{2,1,0:T(8,128)(2,1)} %param.10) | copy-start | bytes 5505028
  161.9 215.8 %all-gather.4.cloned.1.call-start = ((), (), s32[]{:S(2)}) async-start(), calls=%async_computation.3 | async-start | bytes 9748480 | tf_op jit(solution)/shard_map/all_gather | solution.py:61
  163.1 303.4 %all-gather.8.cloned.1.call-start = ((), (), s32[]{:S(2)}) async-start(), calls=%async_computation.5 | async-start | bytes 5570560 | tf_op jit(solution)/shard_map/all_gather | solution.py:78
  274.6 110.3 %copy-start.4 = (bf16[1,7168,128]{2,1,0:T(8,128)(2,1)S(1)}, bf16[1,7168,128]{2,1,0:T(8,128)(2,1)}, u32[]{:S(2)}) copy-start(bf16[1,7168,128]{2,1,0:T(8,128)(2,1)} %param.9) | copy-start | bytes 5505028
  377.7 7.2 %copy-start.2 = (bf16[640,7168]{1,0:T(8,128)(2,1)S(1)}, bf16[640,7168]{1,0:T(8,128)(2,1)}, u32[]{:S(2)}) copy-start(bf16[640,7168]{1,0:T(8,128)(2,1)} %all-gather.6.cloned.1.call-done) | copy-start | bytes 27525124
  534.2 1.6 copy-start.6
  535.8 15.2 %copy-start.7 = (f32[640,128]{0,1:T(8,128)S(1)}, f32[640,128]{0,1:T(8,128)}, u32[]{:S(2)}) copy-start(f32[640,128]{0,1:T(8,128)} %get-tuple-element.12) | copy-start | bytes 983044
  538.9 18.6 %collective-permute-start = (bf16[128,7168]{1,0:T(8,128)(2,1)S(1)}, bf16[128,7168]{1,0:T(8,128)(2,1)S(1)}, u32[]{:S(2)}, u32[]{:S(2)}) collective-permute-start(bf16[128,7168]{1,0:T(8,128)(2,1)S(1)} %fusion), channel_id=1, source_target_pairs={{0,128},{128,0},{1,129},{129,1},{2,130},{130,2},{3,131},{131,3},{4... | collective-permute-start | bytes 5505032 | tf_op jit(solution)/shard_map/ppermute | solution.py:14
  557.5 2.2 copy-start.1
Sparse Core Ops, SparseCore 0:
  162.0 106.0 all-gather.5
  270.5 107.1 all-gather.3
  389.4 76.9 all-gather.7

commit v5 on v3

--- a/solution.py
+++ b/solution.py
@@ -26,7 +26,7 @@
     block_width = gate_cols.shape[1]
     live_count = lax.axis_size("group")
     slot_count = CAP
-    expert_ids = jnp.arange(live_count, dtype=jnp.int32)
+    expert_ids = (lax.axis_index("group") + jnp.arange(live_count, dtype=jnp.int32)) % live_count
     hit = route[:, :, None] == expert_ids
     member = jnp.sum(hit.astype(jnp.int32), axis=1)
     weight = jnp.sum(jnp.where(hit, gate[:, :, None], 0.0), axis=1)
@@ -50,7 +50,9 @@
         ],
         axis=1,
     )
-    near = lax.all_to_all(send, "group", 0, 0, tiled=True)
+    near = jnp.stack(
+        [send[0]] + [from_behind(send[s], "group", s) for s in range(1, live_count)], axis=0
+    )
     near_rows = live_count * slot_count
     near_in = near[:, :slot_count].reshape(near_rows, model_width)
     near_grad = near[:, slot_count:].reshape(near_rows, model_width)
@@ -82,14 +84,12 @@
     down_part = lax.dot_general(
         hidden, got_grad, rows_first, preferred_element_type=jnp.float32
     ).astype(jnp.bfloat16)
-    slice_width = slice_value.shape[1]
-    slice_value = slice_value.reshape(members, groups, slot_count, slice_width)
-    slice_value = jnp.transpose(slice_value, (1, 0, 2, 3)).reshape(
-        groups * members, slot_count, slice_width
+    slice_value = slice_value.reshape(members, near_rows, -1)
+    summed = lax.all_to_all(slice_value, "member", 0, 2, tiled=True)
+    summed = summed.reshape(live_count, slot_count, model_width)
+    returned = jnp.concatenate(
+        [summed[0]] + [from_behind(summed[s], "group", -s) for s in range(1, live_count)], axis=0
     )
-    back = lax.all_to_all(slice_value, ("group", "member"), 0, 0, tiled=True)
-    back = back.reshape(groups, members, slot_count, slice_width)
-    returned = jnp.transpose(back, (0, 2, 1, 3)).reshape(groups * slot_count, model_width)
     branch = jnp.dot(
         pick_mat.astype(jnp.float32),
         returned,

time: 554 us -> 580 us (1.047)
  blocking collectives: 292 us -> 219 us
  waiting for transfers between devices: 176 us -> 234 us
  starting transfers between devices: 12.3 us -> 39.7 us
  local copies, waits for them, and re-layouts: 17.2 us -> 30.5 us
    all_to_all x2 -> x1, blocking collectives: 112 us -> 38 us  [body(): summed = lax.all_to_all(slice_value, 'member', 0, 2, tiled=True)]
    ppermute x1 -> x15, waiting for transfers between devices: 0.01 us -> 52.1 us  [from_behind(): return lax.ppermute(value, axis, pairs)]
    ppermute x1 -> x15, starting transfers between devices: 12.1 us -> 39.6 us  [from_behind(): return lax.ppermute(value, axis, pairs)]
    concatenate x0 -> x1, local copies, waits for them, and re-layouts: none -> 11 us  [body(): jnp.concatenate([summed[0]] + [from_behind(summed[s], 'group', -s) for s...]
    all_gather x1, waiting for transfers between devices: 98.4 us -> 105 us  [body(): got_grad = lax.all_gather(near_grad, 'member', axis=0, tiled=True)]
  transfers between devices with their start and end apart: 4 -> 18, of which waited for: 2 -> 10; matrix products, arithmetic and copies ran while one was open for 3% -> 4% of each run, Pallas kernels for 0% -> 0%
where the time goes in v5:
time: 580 us; the launch traced here: 577 us
  waiting for transfers between devices  234 us (40%)
  blocking collectives  219 us (38%)
  starting transfers between devices  39.7 us (7%)
  matrix products  35.1 us (6%)
  local copies, waits for them, and re-layouts  30.5 us (5%)
  between operations  14 us (2%)
    all_to_all x1, blocking collectives, body(): both_slice = lax.all_to_all(both_cols, 'member', 0, 1, tiled=True)  180 us
    all_gather x1, waiting for transfers between devices, body(): got_grad = lax.all_gather(near_grad, 'member', axis=0, tiled=True)  105 us
    all_gather x1, waiting for transfers between devices, body(): all_grad = lax.all_gather(both_grad, 'member', axis=1, tiled=True)  77.2 us
    ppermute x15, waiting for transfers between devices, from_behind(): return lax.ppermute(value, axis, pairs)  52.1 us
    ppermute x15, starting transfers between devices, from_behind(): return lax.ppermute(value, axis, pairs)  39.6 us
    all_to_all x1, blocking collectives, body(): summed = lax.all_to_all(slice_value, 'member', 0, 2, tiled=True)  38 us
  transfers between devices with their start and end apart: 18, of which 10 were waited for; matrix products, arithmetic and copies ran while one was open for 4% of the time, Pallas kernels for 0%

profile of v5, /device:TPU:33, one launch (start us, length us, event | category | flops | bytes accessed | tf_op | source)
XLA Modules:
  0.0 577.0 jit_solution(13867694256355621477)
XLA Ops:
  7.2 0.9 fusion.28
  8.1 0.1 copy.40
  8.2 0.2 reduce_window_sum.11
  8.5 0.8 fusion.29
  9.5 1.9 fusion.2
  11.4 0.3 reshape.139
  11.7 0.4 convolution_convert_fusion.1
  12.0 0.3 reshape.138
  12.3 0.6 fusion.20
  12.9 6.1 %collective-permute-start = (bf16[10,7168]{1,0:T(8,128)(2,1)S(1)}, bf16[10,7168]{1,0:T(8,128)(2,1)S(1)}, u32[]{:S(2)}, u32[]{:S(2)}) collective-permute-start(bf16[10,7168]{1,0:T(8,128)(2,1)S(1)} %get-tuple-element.10), channel_id=1, source_target_pairs={{0,16},{16,32},{32,48},{48,64},{64,80},{80,96},{96,112},{112,0},{1... | collective-permute-start | bytes 430088 | tf_op jit(solution)/shard_map/ppermute | solution.py:14
  19.0 1.2 collective-permute-start.1
  20.2 1.0 collective-permute-start.2
  21.2 1.6 collective-permute-start.3
  22.9 7.6 %collective-permute-start.4 = (bf16[10,7168]{1,0:T(8,128)(2,1)S(1)}, bf16[10,7168]{1,0:T(8,128)(2,1)S(1)}, u32[]{:S(2)}, u32[]{:S(2)}) collective-permute-start(bf16[10,7168]{1,0:T(8,128)(2,1)S(1)} %get-tuple-element.14), channel_id=1, source_target_pairs={{0,80},{16,96},{32,112},{48,0},{64,16},{80,32},{96,48},{112,64},{1... | collective-permute-start | bytes 430088 | tf_op jit(solution)/shard_map/ppermute | solution.py:14
  30.4 2.6 collective-permute-done
  33.0 2.0 collective-permute-start.6
  35.0 4.5 collective-permute-done.2
  39.6 3.3 collective-permute-done.3
  42.9 4.1 collective-permute-done.4
  47.0 13.5 %collective-permute-done.6 = bf16[10,7168]{1,0:T(8,128)(2,1)S(1)} collective-permute-done((bf16[10,7168]{1,0:T(8,128)(2,1)S(1)}, bf16[10,7168]{1,0:T(8,128)(2,1)S(1)}, u32[]{:S(2)}, u32[]{:S(2)}) %collective-permute-start.6) | collective-permute-done | bytes 143392 | tf_op jit(solution)/shard_map/ppermute | solution.py:14
  60.6 1.3 fusion.36
  61.8 2.4 reshape.141
  64.3 1.1 reshape.140
  65.5 2.0 pad_maximum_fusion
  67.5 180.5 %all_to_all.31 = bf16[16,448,256]{2,1,0:T(8,128)(2,1)S(1)} all-to-all(bf16[16,448,256]{2,1,0:T(8,128)(2,1)S(1)} %pad_maximum_fusion), channel_id=1, replica_groups=mesh['pipe'=2,'group'=8,'member'=16] {'member'}, dimensions={0} | all-to-all | bytes 7340032 | tf_op jit(solution)/shard_map/all_to_all | solution.py:62
  247.9 2.4 copy.54
  250.3 6.4 %fusion.5 = f32[640,128]{0,1:T(8,128)S(1)} fusion(bf16[640,7168]{1,0:T(8,128)(2,1)} %all-gather.6.cloned.1.call-done, bf16[1,7168,128]{2,1,0:T(8,128)(2,1)S(1)} %copy-done.3), kind=kOutput, calls=%fused_computation.24 | convolution fusion | flops 1174405120 | bytes 11337728 | tf_op jit(solution)/shard_map/dot_general | solution.py:67
  256.7 104.6 %all-gather.4.cloned.1.call-done = bf16[640,7168]{1,0:T(8,128)(2,1)} async-done(((bf16[40,7168]{1,0:T(8,128)(2,1)}), bf16[640,7168]{1,0:T(8,128)(2,1)}) %all-gather.4.cloned.1.call-update) | async-done | bytes 9175056 | tf_op jit(solution)/shard_map/all_gather | solution.py:60
  361.3 7.2 %fusion.7 = f32[640,128]{0,1:T(8,128)S(1)} fusion(bf16[640,7168]{1,0:T(8,128)(2,1)} %all-gather.4.cloned.1.call-done, bf16[1,128,7168]{2,1,0:T(8,128)(2,1)} %param.11), kind=kOutput, calls=%fused_computation.26 | convolution fusion | flops 1174405120 | bytes 11337728 | tf_op jit(solution)/shard_map/dot_general | solution.py:72
  368.5 3.7 multiply_convert_fusion.2
  372.1 0.8 pad_maximum_fusion.1
  372.9 77.2 %all-gather.8.cloned.1.call-done = bf16[640,4096]{0,1:T(8,128)(2,1)} async-done(((bf16[640,256]{0,1:T(8,128)(2,1)}), bf16[640,4096]{0,1:T(8,128)(2,1)}) %all-gather.8.cloned.1.call-update) | async-done | bytes 5242896 | tf_op jit(solution)/shard_map/all_gather | solution.py:80
  450.0 6.5 %fusion.38 = f32[640,448]{1,0:T(8,128)S(1)} fusion(bf16[640,4096]{0,1:T(8,128)(2,1)} %all-gather.8.cloned.1.call-done, bf16[448,4096]{1,0:T(8,128)(2,1)} %bitcast.95), kind=kOutput, calls=%fused_computation.77 | convolution fusion | flops 2348810240 | bytes 10059776 | tf_op jit(solution)/shard_map/dot_general | solution.py:81
  456.6 38.0 %all_to_all.32 = f32[16,40,448]{2,1,0:T(8,128)S(1)} all-to-all(f32[16,40,448]{2,1,0:T(8,128)S(1)} %bitcast.97), channel_id=1, replica_groups=mesh['pipe'=2,'group'=8,'member'=16] {'member'}, dimensions={0} | all-to-all | bytes 2293760 | tf_op jit(solution)/shard_map/all_to_all | solution.py:88
  494.6 1.0 fusion.37
  495.6 0.1 copy.49
  495.7 0.1 squeeze.76
  495.8 3.0 collective-permute-start.10
  498.8 1.0 copy.50
  499.9 0.1 squeeze.77
  500.0 2.8 collective-permute-start.11
  502.9 0.8 squeeze.78
  503.8 0.8 squeeze.79
  504.6 3.6 collective-permute-start.13
  508.4 0.8 squeeze.73
  509.2 3.8 collective-permute-start.7
  513.1 0.8 squeeze.74
  514.0 0.8 squeeze.75
  514.9 1.5 collective-permute-start.8
  516.3 3.2 collective-permute-start.9
  519.5 0.6 eq.70
  520.3 0.1 copy.45
  520.4 0.1 squeeze.72
  520.5 1.1 collective-permute-done.13
  521.6 14.4 %collective-permute-done.7 = f32[5,7168]{1,0:T(8,128)S(1)} collective-permute-done((f32[5,7168]{1,0:T(8,128)}, f32[5,7168]{1,0:T(8,128)S(1)}, u32[]{:S(2)}, u32[]{:S(2)}) %collective-permute-start.7) | collective-permute-done | bytes 143392 | tf_op jit(solution)/shard_map/ppermute | solution.py:14
  536.0 0.7 copy-done.10
  536.7 0.7 copy-done.11
  537.4 8.6 %collective-permute-done.9 = f32[5,7168]{1,0:T(8,128)} collective-permute-done((f32[5,7168]{1,0:T(8,128)}, f32[5,7168]{1,0:T(8,128)}, u32[]{:S(2)}, u32[]{:S(2)}) %collective-permute-start.9) | collective-permute-done | bytes 143392 | tf_op jit(solution)/shard_map/ppermute | solution.py:14
  546.0 11.0 %concatenate.22 = f32[40,7168]{1,0:T(8,128)S(1)} concatenate(f32[5,7168]{1,0:T(8,128)S(1)} %squeeze.72, f32[5,7168]{1,0:T(8,128)} %copy-done.10, f32[5,7168]{1,0:T(8,128)} %copy-done.11, f32[5,7168]{1,0:T(8,128)} %collective-permute-done.9, f32[5,7168]{1,0:T(8,128)} %copy-done.7, f32[5,7168]{1,0:T(8,128)} %copy-done.8, f32[5,7168]{1,0:T(8,128)} %collective-permute-done.12, ...), dimensions={0} | concatenate | bytes 2293760 | tf_op jit(solution)/shard_map/concatenate | solution.py:90
  557.1 2.6 fusion
  559.7 2.1 collective-permute-start.14
  561.9 6.5 %fusion.1 = bf16[1,128,7168]{2,1,0:T(8,128)(2,1)} fusion(bf16[640,7168]{1,0:T(8,128)(2,1)} %all-gather.4.cloned.1.call-done, f32[640,128]{0,1:T(8,128)S(1)} %fusion.5, f32[640,128]{0,1:T(8,128)S(1)} %copy-done.6), kind=kOutput, calls=%fused_computation.3 | convolution fusion | flops 1175814144 | bytes 11665408 | tf_op jit(solution)/shard_map/dot_general | solution.py:84
  568.3 1.2 copy.63
  569.5 0.9 copy-done.1
  (62 shorter events, 1.2 us)
Async XLA Ops:
  7.2 4.5 copy-start
  7.2 243.1 %all-gather.6.cloned.1.call-start = ((), (), s32[]{:S(2)}) async-start(), calls=%async_computation.3 | async-start | bytes 9748480 | tf_op jit(solution)/shard_map/all_gather | solution.py:59
  12.9 20.1 %collective-permute-start = (bf16[10,7168]{1,0:T(8,128)(2,1)S(1)}, bf16[10,7168]{1,0:T(8,128)(2,1)S(1)}, u32[]{:S(2)}, u32[]{:S(2)}) collective-permute-start(bf16[10,7168]{1,0:T(8,128)(2,1)S(1)} %get-tuple-element.10), channel_id=1, source_target_pairs={{0,16},{16,32},{32,48},{48,64},{64,80},{80,96},{96,112},{112,0},{1... | collective-permute-start | bytes 430088 | tf_op jit(solution)/shard_map/ppermute | solution.py:14
  19.0 14.0 %collective-permute-start.1 = (bf16[10,7168]{1,0:T(8,128)(2,1)S(1)}, bf16[10,7168]{1,0:T(8,128)(2,1)S(1)}, u32[]{:S(2)}, u32[]{:S(2)}) collective-permute-start(bf16[10,7168]{1,0:T(8,128)(2,1)S(1)} %get-tuple-element.11), channel_id=1, source_target_pairs={{0,32},{16,48},{32,64},{48,80},{64,96},{80,112},{96,0},{112,16},{1... | collective-permute-start | bytes 430088 | tf_op jit(solution)/shard_map/ppermute | solution.py:14
  20.2 19.3 %collective-permute-start.2 = (bf16[10,7168]{1,0:T(8,128)(2,1)S(1)}, bf16[10,7168]{1,0:T(8,128)(2,1)S(1)}, u32[]{:S(2)}, u32[]{:S(2)}) collective-permute-start(bf16[10,7168]{1,0:T(8,128)(2,1)S(1)} %get-tuple-element.12), channel_id=1, source_target_pairs={{0,48},{16,64},{32,80},{48,96},{64,112},{80,0},{96,16},{112,32},{1... | collective-permute-start | bytes 430088 | tf_op jit(solution)/shard_map/ppermute | solution.py:14
  21.2 21.6 %collective-permute-start.3 = (bf16[10,7168]{1,0:T(8,128)(2,1)S(1)}, bf16[10,7168]{1,0:T(8,128)(2,1)S(1)}, u32[]{:S(2)}, u32[]{:S(2)}) collective-permute-start(bf16[10,7168]{1,0:T(8,128)(2,1)S(1)} %get-tuple-element.13), channel_id=1, source_target_pairs={{0,64},{16,80},{32,96},{48,112},{64,0},{80,16},{96,32},{112,48},{1... | collective-permute-start | bytes 430088 | tf_op jit(solution)/shard_map/ppermute | solution.py:14
  22.9 24.1 %collective-permute-start.4 = (bf16[10,7168]{1,0:T(8,128)(2,1)S(1)}, bf16[10,7168]{1,0:T(8,128)(2,1)S(1)}, u32[]{:S(2)}, u32[]{:S(2)}) collective-permute-start(bf16[10,7168]{1,0:T(8,128)(2,1)S(1)} %get-tuple-element.14), channel_id=1, source_target_pairs={{0,80},{16,96},{32,112},{48,0},{64,16},{80,32},{96,48},{112,64},{1... | collective-permute-start | bytes 430088 | tf_op jit(solution)/shard_map/ppermute | solution.py:14
  33.0 14.0 %collective-permute-start.5 = (bf16[10,7168]{1,0:T(8,128)(2,1)S(1)}, bf16[10,7168]{1,0:T(8,128)(2,1)S(1)}, u32[]{:S(2)}, u32[]{:S(2)}) collective-permute-start(bf16[10,7168]{1,0:T(8,128)(2,1)S(1)} %get-tuple-element.15), channel_id=1, source_target_pairs={{0,96},{16,112},{32,0},{48,16},{64,32},{80,48},{96,64},{112,80},{1... | collective-permute-start | bytes 430088 | tf_op jit(solution)/shard_map/ppermute | solution.py:14
  33.0 27.5 %collective-permute-start.6 = (bf16[10,7168]{1,0:T(8,128)(2,1)S(1)}, bf16[10,7168]{1,0:T(8,128)(2,1)S(1)}, u32[]{:S(2)}, u32[]{:S(2)}) collective-permute-start(bf16[10,7168]{1,0:T(8,128)(2,1)S(1)} %get-tuple-element.8), channel_id=1, source_target_pairs={{0,112},{16,0},{32,16},{48,32},{64,48},{80,64},{96,80},{112,96},{1... | collective-permute-start | bytes 430088 | tf_op jit(solution)/shard_map/ppermute | solution.py:14
  61.8 3.6 copy-start.3
  64.2 297.0 %all-gather.4.cloned.1.call-start = ((), (), s32[]{:S(2)}) async-start(), calls=%async_computation.2 | async-start | bytes 9748480 | tf_op jit(solution)/shard_map/all_gather | solution.py:60
  65.4 384.6 %all-gather.8.cloned.1.call-start = ((), (), s32[]{:S(2)}) async-start(), calls=%async_computation.4 | async-start | bytes 5570560 | tf_op jit(solution)/shard_map/all_gather | solution.py:80
  256.7 111.8 %copy-start.4 = (bf16[1,7168,128]{2,1,0:T(8,128)(2,1)S(1)}, bf16[1,7168,128]{2,1,0:T(8,128)(2,1)}, u32[]{:S(2)}) copy-start(bf16[1,7168,128]{2,1,0:T(8,128)(2,1)} %param.9) | copy-start | bytes 5505028
  361.3 7.2 %copy-start.2 = (bf16[640,7168]{1,0:T(8,128)(2,1)S(1)}, bf16[640,7168]{1,0:T(8,128)(2,1)}, u32[]{:S(2)}) copy-start(bf16[640,7168]{1,0:T(8,128)(2,1)} %all-gather.6.cloned.1.call-done) | copy-start | bytes 27525124
  495.8 19.1 %collective-permute-start.10 = (f32[5,7168]{1,0:T(8,128)S(1)}, f32[5,7168]{1,0:T(8,128)S(1)}, u32[]{:S(2)}, u32[]{:S(2)}) collective-permute-start(f32[5,7168]{1,0:T(8,128)S(1)} %squeeze.76), channel_id=1, source_target_pairs={{0,64},{16,80},{32,96},{48,112},{64,0},{80,16},{96,32},{112,48},{1... | collective-permute-start | bytes 430088 | tf_op jit(solution)/shard_map/ppermute | solution.py:14
  500.0 16.3 %collective-permute-start.11 = (f32[5,7168]{1,0:T(8,128)S(1)}, f32[5,7168]{1,0:T(8,128)S(1)}, u32[]{:S(2)}, u32[]{:S(2)}) collective-permute-start(f32[5,7168]{1,0:T(8,128)S(1)} %squeeze.77), channel_id=1, source_target_pairs={{0,48},{16,64},{32,80},{48,96},{64,112},{80,0},{96,16},{112,32},{1... | collective-permute-start | bytes 430088 | tf_op jit(solution)/shard_map/ppermute | solution.py:14
  503.7 16.8 %collective-permute-start.12 = (f32[5,7168]{1,0:T(8,128)}, f32[5,7168]{1,0:T(8,128)}, u32[]{:S(2)}, u32[]{:S(2)}) collective-permute-start(f32[5,7168]{1,0:T(8,128)} %squeeze.78), channel_id=1, source_target_pairs={{0,32},{16,48},{32,64},{48,80},{64,96},{80,112},{96,0},{112,16},{1... | collective-permute-start | bytes 430088 | tf_op jit(solution)/shard_map/ppermute | solution.py:14
  504.6 17.0 %collective-permute-start.13 = (f32[5,7168]{1,0:T(8,128)}, f32[5,7168]{1,0:T(8,128)S(1)}, u32[]{:S(2)}, u32[]{:S(2)}) collective-permute-start(f32[5,7168]{1,0:T(8,128)} %squeeze.79), channel_id=1, source_target_pairs={{0,16},{16,32},{32,48},{48,64},{64,80},{80,96},{96,112},{112,0},{1... | collective-permute-start | bytes 430088 | tf_op jit(solution)/shard_map/ppermute | solution.py:14
  509.2 26.9 %collective-permute-start.7 = (f32[5,7168]{1,0:T(8,128)}, f32[5,7168]{1,0:T(8,128)S(1)}, u32[]{:S(2)}, u32[]{:S(2)}) collective-permute-start(f32[5,7168]{1,0:T(8,128)} %squeeze.73), channel_id=1, source_target_pairs={{0,112},{16,0},{32,16},{48,32},{64,48},{80,64},{96,80},{112,96},{1... | collective-permute-start | bytes 430088 | tf_op jit(solution)/shard_map/ppermute | solution.py:14
  514.9 5.4 copy-start.7
  514.9 21.2 %collective-permute-start.8 = (f32[5,7168]{1,0:T(8,128)}, f32[5,7168]{1,0:T(8,128)S(1)}, u32[]{:S(2)}, u32[]{:S(2)}) collective-permute-start(f32[5,7168]{1,0:T(8,128)} %squeeze.74), channel_id=1, source_target_pairs={{0,96},{16,112},{32,0},{48,16},{64,32},{80,48},{96,64},{112,80},{1... | collective-permute-start | bytes 430088 | tf_op jit(solution)/shard_map/ppermute | solution.py:14
  516.3 3.9 copy-start.8
  516.3 29.7 %collective-permute-start.9 = (f32[5,7168]{1,0:T(8,128)}, f32[5,7168]{1,0:T(8,128)}, u32[]{:S(2)}, u32[]{:S(2)}) collective-permute-start(f32[5,7168]{1,0:T(8,128)} %squeeze.75), channel_id=1, source_target_pairs={{0,80},{16,96},{32,112},{48,0},{64,16},{80,32},{96,48},{112,64},{1... | collective-permute-start | bytes 430088 | tf_op jit(solution)/shard_map/ppermute | solution.py:14
  520.3 36.8 %copy-start.5 = (bf16[1,128,7168]{2,1,0:T(8,128)(2,1)S(1)}, bf16[1,128,7168]{2,1,0:T(8,128)(2,1)}, u32[]{:S(2)}) copy-start(bf16[1,128,7168]{2,1,0:T(8,128)(2,1)} %param.8) | copy-start | bytes 5505028
  521.6 14.4 %copy-start.9 = (f32[5,7168]{1,0:T(8,128)}, f32[5,7168]{1,0:T(8,128)S(1)}, u32[]{:S(2)}) copy-start(f32[5,7168]{1,0:T(8,128)S(1)} %collective-permute-done.13) | copy-start | bytes 430084
  536.0 0.7 copy-start.10
  536.7 0.7 copy-start.11
  557.1 4.8 copy-start.6
  559.7 8.6 %collective-permute-start.14 = (bf16[128,7168]{1,0:T(8,128)(2,1)S(1)}, bf16[128,7168]{1,0:T(8,128)(2,1)S(1)}, u32[]{:S(2)}, u32[]{:S(2)}) collective-permute-start(bf16[128,7168]{1,0:T(8,128)(2,1)S(1)} %fusion), channel_id=1, source_target_pairs={{0,128},{128,0},{1,129},{129,1},{2,130},{130,2},{3,131},{131,3},{4... | collective-permute-start | bytes 5505032 | tf_op jit(solution)/shard_map/ppermute | solution.py:14
  568.3 2.2 copy-start.1
Sparse Core Ops, SparseCore 0:
  64.4 178.4 all-gather.5
  245.2 115.9 all-gather.3
  373.0 76.9 all-gather.7

commit v6 on v3

--- a/solution.py
+++ b/solution.py
@@ -43,17 +43,11 @@
         live_count * slot_count, 1
     )
     rows_grad = (chosen_grads * slot_gate).astype(jnp.bfloat16)
-    send = jnp.concatenate(
-        [
-            rows_in.reshape(live_count, slot_count, model_width),
-            rows_grad.reshape(live_count, slot_count, model_width),
-        ],
-        axis=1,
-    )
-    near = lax.all_to_all(send, "group", 0, 0, tiled=True)
+    send_in = rows_in.reshape(live_count, slot_count, model_width)
+    send_grad = rows_grad.reshape(live_count, slot_count, model_width)
     near_rows = live_count * slot_count
-    near_in = near[:, :slot_count].reshape(near_rows, model_width)
-    near_grad = near[:, slot_count:].reshape(near_rows, model_width)
+    near_in = lax.all_to_all(send_in, "group", 0, 0, tiled=True).reshape(near_rows, model_width)
+    near_grad = lax.all_to_all(send_grad, "group", 0, 0, tiled=True).reshape(near_rows, model_width)
     got_in = lax.all_gather(near_in, "member", axis=0, tiled=True)
     got_grad = lax.all_gather(near_grad, "member", axis=0, tiled=True)
     both_cols = jnp.concatenate([gate_cols, up_cols], axis=1)
@@ -74,10 +68,10 @@
         jnp.bfloat16
     )
     grad_up = (back_hidden * silu_gate).astype(jnp.bfloat16)
-    both_grad = jnp.concatenate([grad_gate, grad_up], axis=1)
-    all_grad = lax.all_gather(both_grad, "member", axis=1, tiled=True)
+    both_grad = jnp.concatenate([grad_gate, grad_up], axis=1).T
+    all_grad = lax.all_gather(both_grad, "member", axis=0, tiled=True)
     slice_value = lax.dot_general(
-        all_grad, both_slice, contract, preferred_element_type=jnp.float32
+        all_grad, both_slice, (((0,), (1,)), ((), ())), preferred_element_type=jnp.float32
     )
     down_part = lax.dot_general(
         hidden, got_grad, rows_first, preferred_element_type=jnp.float32

time: 554 us -> 543 us (0.980)
  blocking collectives: 292 us -> 282 us
    all_to_all x1, blocking collectives: 180 us -> 154 us  [body(): both_slice = lax.all_to_all(both_cols, 'member', 0, 1, tiled=True)]
    all_to_all x1 -> x2, blocking collectives: 56.4 us -> 73.1 us  [the longest x1 37 us: body(): lax.all_to_all(send_in, 'group', 0, 0, tiled=True)]
  transfers between devices with their start and end apart: 4 -> 4, of which waited for: 2 -> 2; matrix products, arithmetic and copies ran while one was open for 3% -> 4% of each run, Pallas kernels for 0% -> 0%
where the time goes in v6:
time: 543 us; the launch traced here: 541 us
  blocking collectives  282 us (52%)
  waiting for transfers between devices  177 us (33%)
  matrix products  34 us (6%)
  local copies, waits for them, and re-layouts  17.3 us (3%)
  between operations  13.9 us (3%)
  starting transfers between devices  12.3 us (2%)
    all_to_all x1, blocking collectives, body(): both_slice = lax.all_to_all(both_cols, 'member', 0, 1, tiled=True)  154 us
    all_gather x1, waiting for transfers between devices, body(): got_grad = lax.all_gather(near_grad, 'member', axis=0, tiled=True)  100 us
    all_gather x1, waiting for transfers between devices, body(): all_grad = lax.all_gather(both_grad, 'member', axis=0, tiled=True)  77.2 us
    all_to_all x1, blocking collectives, body(): back = lax.all_to_all(slice_value, ('group', 'member'), 0, 0, tiled=True)  55.5 us
    all_to_all x1, blocking collectives, body(): lax.all_to_all(send_in, 'group', 0, 0, tiled=True)  37 us
    all_to_all x1, blocking collectives, body(): lax.all_to_all(send_grad, 'group', 0, 0, tiled=True)  36.1 us
    ppermute x1, starting transfers between devices, from_behind(): return lax.ppermute(value, axis, pairs)  12.1 us
  transfers between devices with their start and end apart: 4, of which 2 were waited for; matrix products, arithmetic and copies ran while one was open for 4% of the time, Pallas kernels for 0%

profile of v6, /device:TPU:33, one launch (start us, length us, event | category | flops | bytes accessed | tf_op | source)
XLA Modules:
  0.0 541.0 jit_solution(16099030000864008902)
XLA Ops:
  7.2 0.0 copy-start
  7.2 0.0 all-gather.6.cloned.1.call-start
  7.2 0.8 convert_reduce_fusion
  8.1 0.1 copy.29
  8.2 0.2 reduce_window_sum.11
  8.5 0.2 copy-done
  8.7 0.4 convolution_convert_fusion.1
  9.1 0.3 reshape.140
  9.3 0.0 copy-start.8
  9.3 0.0 copy-start.9
  9.4 0.0 copy-start.5
  9.4 37.0 %all_to_all.31 = bf16[8,5,7168]{2,1,0:T(8,128)(2,1)} all-to-all(bf16[8,5,7168]{2,1,0:T(8,128)(2,1)S(1)} %reshape.140), channel_id=1, replica_groups=mesh['pipe'=2,'group'=8,'member'=16] {'group'}, dimensions={0} | all-to-all | bytes 1146880 | tf_op jit(solution)/shard_map/all_to_all | solution.py:49
  46.4 2.3 reshape.141
  48.6 0.0 all-gather.6.cloned.1.call-update
  48.7 0.0 all-gather.4.cloned.1.call-start
  48.7 0.0 copy-done.8
  48.7 0.0 copy-done.9
  48.7 0.1 select_reduce_fusion
  48.8 0.1 mul.41
  48.9 0.0 copy-done.5
  48.9 0.4 fusion.2
  49.3 0.3 reshape.138
  49.6 0.0 copy-start.3
  49.6 36.1 %all_to_all.32 = bf16[8,5,7168]{2,1,0:T(8,128)(2,1)} all-to-all(bf16[8,5,7168]{2,1,0:T(8,128)(2,1)S(1)} %reshape.138), channel_id=1, replica_groups=mesh['pipe'=2,'group'=8,'member'=16] {'group'}, dimensions={0} | all-to-all | bytes 1146880 | tf_op jit(solution)/shard_map/all_to_all | solution.py:50
  85.7 2.3 reshape.139
  88.0 0.0 all-gather.4.cloned.1.call-update
  88.0 0.0 all-gather.8.cloned.1.call-start
  88.0 0.0 copy-done.3
  88.1 2.0 pad_maximum_fusion
  90.1 153.5 %all_to_all.33 = bf16[16,448,256]{2,1,0:T(8,128)(2,1)S(1)} all-to-all(bf16[16,448,256]{2,1,0:T(8,128)(2,1)S(1)} %pad_maximum_fusion), channel_id=1, replica_groups=mesh['pipe'=2,'group'=8,'member'=16] {'member'}, dimensions={0} | all-to-all | bytes 7340032 | tf_op jit(solution)/shard_map/all_to_all | solution.py:54
  243.6 2.3 copy.38
  245.9 0.0 all-gather.6.cloned.1.call-done
  245.9 6.4 %fusion.5 = f32[640,128]{0,1:T(8,128)S(1)} fusion(bf16[640,7168]{1,0:T(8,128)(2,1)} %all-gather.6.cloned.1.call-done, bf16[1,7168,128]{2,1,0:T(8,128)(2,1)S(1)} %copy-done.3), kind=kOutput, calls=%fused_computation.10 | convolution fusion | flops 1174405120 | bytes 11337728 | tf_op jit(solution)/shard_map/dot_general | solution.py:59
  252.3 0.0 copy-start.4
  252.3 100.2 %all-gather.4.cloned.1.call-done = bf16[640,7168]{1,0:T(8,128)(2,1)} async-done(((bf16[40,7168]{1,0:T(8,128)(2,1)}), bf16[640,7168]{1,0:T(8,128)(2,1)}) %all-gather.4.cloned.1.call-update) | async-done | bytes 9175056 | tf_op jit(solution)/shard_map/all_gather | solution.py:52
  352.5 0.0 copy-start.2
  352.5 7.2 %fusion.8 = f32[640,128]{0,1:T(8,128)S(1)} fusion(bf16[640,7168]{1,0:T(8,128)(2,1)} %all-gather.4.cloned.1.call-done, bf16[1,128,7168]{2,1,0:T(8,128)(2,1)} %param.11), kind=kOutput, calls=%fused_computation.13 | convolution fusion | flops 1174405120 | bytes 11337728 | tf_op jit(solution)/shard_map/dot_general | solution.py:64
  359.7 0.0 copy-done.4
  359.7 0.0 copy-done.2
  359.7 3.7 multiply_convert_fusion.2
  363.4 0.8 maximum_bitcast_fusion
  364.1 0.0 all-gather.8.cloned.1.call-update
  364.2 77.2 %all-gather.8.cloned.1.call-done = bf16[4096,640]{1,0:T(8,128)(2,1)} async-done(((bf16[256,640]{1,0:T(8,128)(2,1)}), bf16[4096,640]{1,0:T(8,128)(2,1)}) %all-gather.8.cloned.1.call-update) | async-done | bytes 5242896 | tf_op jit(solution)/shard_map/all_gather | solution.py:72
  441.3 6.5 %fusion.15 = f32[640,448]{1,0:T(8,128)S(1)} fusion(bf16[4096,640]{1,0:T(8,128)(2,1)} %all-gather.8.cloned.1.call-done, bf16[448,4096]{1,0:T(8,128)(2,1)} %bitcast.57), kind=kOutput, calls=%fused_computation.31 | convolution fusion | flops 2348810240 | bytes 10059776 | tf_op jit(solution)/shard_map/dot_general | solution.py:73
  447.8 1.6 reshape.142
  449.4 2.4 copy.34
  451.8 1.0 copy.35
  452.8 55.5 %all_to_all.34 = f32[128,5,448]{2,1,0:T(8,128)S(1)} all-to-all(f32[128,5,448]{2,1,0:T(8,128)S(1)} %copy.35), channel_id=1, replica_groups=mesh['pipe'=2,'group'=8,'member'=16] {'group','member'}, dimensions={0} | all-to-all | bytes 2293760 | tf_op jit(solution)/shard_map/all_to_all | solution.py:84
  508.3 0.8 copy.40
  509.1 0.0 copy-start.6
  509.1 1.5 reshape.145
  510.6 0.0 copy-done.6
  510.6 0.0 copy-start.7
  510.6 3.1 fusion
  513.7 12.1 %collective-permute-start = (bf16[128,7168]{1,0:T(8,128)(2,1)S(1)}, bf16[128,7168]{1,0:T(8,128)(2,1)S(1)}, u32[]{:S(2)}, u32[]{:S(2)}) collective-permute-start(bf16[128,7168]{1,0:T(8,128)(2,1)S(1)} %fusion), channel_id=1, source_target_pairs={{0,128},{128,0},{1,129},{129,1},{2,130},{130,2},{3,131},{131,3},{4... | collective-permute-start | bytes 5505032 | tf_op jit(solution)/shard_map/ppermute | solution.py:14
  525.9 0.0 copy-done.7
  525.9 6.5 %fusion.1 = bf16[1,128,7168]{2,1,0:T(8,128)(2,1)} fusion(bf16[640,7168]{1,0:T(8,128)(2,1)} %all-gather.4.cloned.1.call-done, f32[640,128]{0,1:T(8,128)S(1)} %fusion.5, f32[640,128]{0,1:T(8,128)S(1)} %copy-done.7), kind=kOutput, calls=%fused_computation.3 | convolution fusion | flops 1175814144 | bytes 11665408 | tf_op jit(solution)/shard_map/dot_general | solution.py:76
  532.3 0.0 collective-permute-done
  532.3 0.0 copy-start.1
  532.3 1.2 copy.42
  533.6 0.9 copy-done.1
  (6 shorter events, 0.1 us)
Async XLA Ops:
  7.2 1.5 copy-start
  7.2 238.7 %all-gather.6.cloned.1.call-start = ((), (), s32[]{:S(2)}) async-start(), calls=%async_computation.5 | async-start | bytes 9748480 | tf_op jit(solution)/shard_map/all_gather | solution.py:51
  9.3 39.4 %copy-start.8 = (s32[1,128,8]{1,2,0:T(8,128)S(1)}, s32[1,128,8]{1,2,0:T(8,128)}, u32[]{:S(2)}) copy-start(s32[1,128,8]{1,2,0:T(8,128)} %param.12) | copy-start | bytes 12292
  9.3 39.4 %copy-start.9 = (f32[1,128,8]{1,2,0:T(8,128)S(1)}, f32[1,128,8]{1,2,0:T(8,128)}, u32[]{:S(2)}) copy-start(f32[1,128,8]{1,2,0:T(8,128)} %param.13) | copy-start | bytes 12292
  9.4 39.6 %copy-start.5 = (bf16[1,128,7168]{2,1,0:T(8,128)(2,1)S(1)}, bf16[1,128,7168]{2,1,0:T(8,128)(2,1)}, u32[]{:S(2)}) copy-start(bf16[1,128,7168]{2,1,0:T(8,128)(2,1)} %param.8) | copy-start | bytes 5505028
  48.7 303.9 %all-gather.4.cloned.1.call-start = ((), (), s32[]{:S(2)}) async-start(), calls=%async_computation.4 | async-start | bytes 9748480 | tf_op jit(solution)/shard_map/all_gather | solution.py:52
  49.6 38.5 %copy-start.3 = (bf16[1,7168,128]{2,1,0:T(8,128)(2,1)S(1)}, bf16[1,7168,128]{2,1,0:T(8,128)(2,1)}, u32[]{:S(2)}) copy-start(bf16[1,7168,128]{2,1,0:T(8,128)(2,1)} %param.10) | copy-start | bytes 5505028
  88.0 353.3 %all-gather.8.cloned.1.call-start = ((), (), s32[]{:S(2)}) async-start(), calls=%async_computation.6 | async-start | bytes 5570560 | tf_op jit(solution)/shard_map/all_gather | solution.py:72
  252.3 107.4 %copy-start.4 = (bf16[1,7168,128]{2,1,0:T(8,128)(2,1)S(1)}, bf16[1,7168,128]{2,1,0:T(8,128)(2,1)}, u32[]{:S(2)}) copy-start(bf16[1,7168,128]{2,1,0:T(8,128)(2,1)} %param.9) | copy-start | bytes 5505028
  352.5 7.2 %copy-start.2 = (bf16[640,7168]{1,0:T(8,128)(2,1)S(1)}, bf16[640,7168]{1,0:T(8,128)(2,1)}, u32[]{:S(2)}) copy-start(bf16[640,7168]{1,0:T(8,128)(2,1)} %all-gather.6.cloned.1.call-done) | copy-start | bytes 27525124
  509.1 1.6 copy-start.6
  510.6 15.2 %copy-start.7 = (f32[640,128]{0,1:T(8,128)S(1)}, f32[640,128]{0,1:T(8,128)}, u32[]{:S(2)}) copy-start(f32[640,128]{0,1:T(8,128)} %get-tuple-element.8) | copy-start | bytes 983044
  513.7 18.6 %collective-permute-start = (bf16[128,7168]{1,0:T(8,128)(2,1)S(1)}, bf16[128,7168]{1,0:T(8,128)(2,1)S(1)}, u32[]{:S(2)}, u32[]{:S(2)}) collective-permute-start(bf16[128,7168]{1,0:T(8,128)(2,1)S(1)} %fusion), channel_id=1, source_target_pairs={{0,128},{128,0},{1,129},{129,1},{2,130},{130,2},{3,131},{131,3},{4... | collective-permute-start | bytes 5505032 | tf_op jit(solution)/shard_map/ppermute | solution.py:14
  532.3 2.2 copy-start.1
Sparse Core Ops, SparseCore 0:
  48.8 173.5 all-gather.5
  224.7 127.7 all-gather.3
  364.3 76.9 all-gather.7

commit v7 on v6

--- a/solution.py
+++ b/solution.py
@@ -51,8 +51,8 @@
     got_in = lax.all_gather(near_in, "member", axis=0, tiled=True)
     got_grad = lax.all_gather(near_grad, "member", axis=0, tiled=True)
     both_cols = jnp.concatenate([gate_cols, up_cols], axis=1)
+    both_cols, got_in, got_grad = lax.optimization_barrier((both_cols, got_in, got_grad))
     both_slice = lax.all_to_all(both_cols, "member", 0, 1, tiled=True)
-    both_slice, got_in = lax.optimization_barrier((both_slice, got_in))
     members = lax.axis_size("member")
     groups = live_count
     gate_pre = jnp.dot(got_in, gate_cols, preferred_element_type=jnp.float32)
@@ -69,6 +69,7 @@
     )
     grad_up = (back_hidden * silu_gate).astype(jnp.bfloat16)
     both_grad = jnp.concatenate([grad_gate, grad_up], axis=1).T
+    both_slice, both_grad = lax.optimization_barrier((both_slice, both_grad))
     all_grad = lax.all_gather(both_grad, "member", axis=0, tiled=True)
     slice_value = lax.dot_general(
         all_grad, both_slice, (((0,), (1,)), ((), ())), preferred_element_type=jnp.float32
@@ -81,9 +82,10 @@
     slice_value = jnp.transpose(slice_value, (1, 0, 2, 3)).reshape(
         groups * members, slot_count, slice_width
     )
-    back = lax.all_to_all(slice_value, ("group", "member"), 0, 0, tiled=True)
+    back = lax.all_to_all(slice_value.astype(jnp.bfloat16), ("group", "member"), 0, 0, tiled=True)
     back = back.reshape(groups, members, slot_count, slice_width)
     returned = jnp.transpose(back, (0, 2, 1, 3)).reshape(groups * slot_count, model_width)
+    returned = returned.astype(jnp.float32)
     branch = jnp.dot(
         pick_mat.astype(jnp.float32),
         returned,

time: 543 us -> 521 us (0.959)
  blocking collectives: 282 us -> 106 us
  waiting for transfers between devices: 177 us -> 321 us
  starting transfers between devices: 12.3 us -> 19.7 us
    all_to_all x2 -> x1, blocking collectives: 209 us -> 33.4 us  [body(): lax.all_to_all(slice_value.astype(jnp.bfloat16), ('group', 'member'), 0,...]
    all_gather x1, waiting for transfers between devices: 0.01 us -> 110 us  [body(): got_in = lax.all_gather(near_in, 'member', axis=0, tiled=True)]
    all_to_all x0 -> x1, waiting for transfers between devices: none -> 59.9 us  [body(): both_slice = lax.all_to_all(both_cols, 'member', 0, 1, tiled=True)]
    all_gather x1, waiting for transfers between devices: 100 us -> 71.1 us  [body(): got_grad = lax.all_gather(near_grad, 'member', axis=0, tiled=True)]
    all_to_all x0 -> x1, starting transfers between devices: none -> 7.51 us  [body(): both_slice = lax.all_to_all(both_cols, 'member', 0, 1, tiled=True)]
  transfers between devices with their start and end apart: 4 -> 5, of which waited for: 2 -> 4; matrix products, arithmetic and copies ran while one was open for 4% -> 6% of each run, Pallas kernels for 0% -> 0%
where the time goes in v7:
time: 521 us; the launch traced here: 518 us
  waiting for transfers between devices  321 us (62%)
  blocking collectives  106 us (20%)
  matrix products  34.9 us (7%)
  starting transfers between devices  19.7 us (4%)
  local copies, waits for them, and re-layouts  15.3 us (3%)
  between operations  14 us (3%)
  other arithmetic  6.96 us (1%)
    all_gather x1, waiting for transfers between devices, body(): got_in = lax.all_gather(near_in, 'member', axis=0, tiled=True)  110 us
    all_gather x1, waiting for transfers between devices, body(): all_grad = lax.all_gather(both_grad, 'member', axis=0, tiled=True)  79.7 us
    all_gather x1, waiting for transfers between devices, body(): got_grad = lax.all_gather(near_grad, 'member', axis=0, tiled=True)  71.1 us
    all_to_all x1, waiting for transfers between devices, body(): both_slice = lax.all_to_all(both_cols, 'member', 0, 1, tiled=True)  59.9 us
    all_to_all x1, blocking collectives, body(): lax.all_to_all(send_grad, 'group', 0, 0, tiled=True)  36.9 us
    all_to_all x1, blocking collectives, body(): lax.all_to_all(send_in, 'group', 0, 0, tiled=True)  36 us
    all_to_all x1, blocking collectives, body(): lax.all_to_all(slice_value.astype(jnp.bfloat16), ('group', 'member'), 0,...  33.4 us
    ppermute x1, starting transfers between devices, from_behind(): return lax.ppermute(value, axis, pairs)  11.9 us
  transfers between devices with their start and end apart: 5, of which 4 were waited for; matrix products, arithmetic and copies ran while one was open for 6% of the time, Pallas kernels for 0%

profile of v7, /device:TPU:33, one launch (start us, length us, event | category | flops | bytes accessed | tf_op | source)
XLA Modules:
  0.0 518.1 jit_solution(18055148981991678056)
XLA Ops:
  7.2 0.0 copy-start
  7.2 0.0 all-gather.6.cloned.1.call-start
  7.2 0.8 convert_reduce_fusion
  8.1 0.1 copy.28
  8.2 0.2 reduce_window_sum.11
  8.5 0.7 select_reduce_fusion.1
  9.2 0.1 select_reduce_fusion
  9.3 0.1 mul.41
  9.3 1.9 fusion.2
  11.2 0.3 reshape.134
  11.5 36.9 %all_to_all.34 = bf16[8,5,7168]{2,1,0:T(8,128)(2,1)} all-to-all(bf16[8,5,7168]{2,1,0:T(8,128)(2,1)S(1)} %reshape.134), channel_id=1, replica_groups=mesh['pipe'=2,'group'=8,'member'=16] {'group'}, dimensions={0} | all-to-all | bytes 1146880 | tf_op jit(solution)/shard_map/all_to_all | solution.py:50
  48.4 2.3 reshape.135
  50.6 0.0 all-gather.6.cloned.1.call-update
  50.7 0.0 all-gather.4.cloned.1.call-start
  50.7 0.0 copy-done
  50.7 0.4 convolution_convert_fusion.1
  51.1 0.3 reshape.132
  51.4 36.0 %all_to_all.35 = bf16[8,5,7168]{2,1,0:T(8,128)(2,1)} all-to-all(bf16[8,5,7168]{2,1,0:T(8,128)(2,1)S(1)} %reshape.132), channel_id=1, replica_groups=mesh['pipe'=2,'group'=8,'member'=16] {'group'}, dimensions={0} | all-to-all | bytes 1146880 | tf_op jit(solution)/shard_map/all_to_all | solution.py:49
  87.4 2.3 reshape.133
  89.6 0.0 all-gather.4.cloned.1.call-update
  89.6 4.4 pad_maximum_fusion
  94.0 71.1 %all-gather.6.cloned.1.call-done = bf16[640,7168]{1,0:T(8,128)(2,1)} async-done(((bf16[40,7168]{1,0:T(8,128)(2,1)}), bf16[640,7168]{1,0:T(8,128)(2,1)}) %all-gather.6.cloned.1.call-update) | async-done | bytes 9175056 | tf_op jit(solution)/shard_map/all_gather | solution.py:52
  165.1 110.4 %all-gather.4.cloned.1.call-done = bf16[640,7168]{1,0:T(8,128)(2,1)} async-done(((bf16[40,7168]{1,0:T(8,128)(2,1)}), bf16[640,7168]{1,0:T(8,128)(2,1)}) %all-gather.4.cloned.1.call-update) | async-done | bytes 9175056 | tf_op jit(solution)/shard_map/all_gather | solution.py:51
  275.5 7.5 %all-to-all-start.2 = ((bf16[16,448,256]{2,1,0:T(8,128)(2,1)}), bf16[16,448,256]{2,1,0:T(8,128)(2,1)}, u32[]{:S(2)}, u32[]{:S(2)}) async-start(bf16[16,448,256]{2,1,0:T(8,128)(2,1)} %bitcast.51), calls=%async_computation.2 | async-start | bytes 7340032 | tf_op jit(solution)/shard_map/all_to_all | solution.py:55
  283.0 0.2 all-gather.8.cloned.1.call-start
  283.2 0.0 copy-start.3
  283.2 0.0 slice-start
  283.3 0.0 slice-start.1
  283.3 7.0 %fusion.10 = f32[640,128]{0,1:T(8,128)S(1)} fusion(bf16[640,7168]{1,0:T(8,128)(2,1)} %all-gather.4.cloned.1.call-done, bf16[1,7168,128]{2,1,0:T(8,128)(2,1)} %param.10), kind=kOutput, calls=%fused_computation.27 | convolution fusion | flops 1174405120 | bytes 11337728 | tf_op jit(solution)/shard_map/dot_general | solution.py:59
  290.3 0.0 copy-done.3
  290.3 0.0 slice-start.2
  290.3 0.0 copy-start.1
  290.4 6.7 %fusion.3 = f32[640,128]{0,1:T(8,128)S(1)} fusion(bf16[640,7168]{1,0:T(8,128)(2,1)} %all-gather.6.cloned.1.call-done, bf16[1,128,7168]{2,1,0:T(8,128)(2,1)S(1)} %copy-done.3), kind=kOutput, calls=%fused_computation.8 | convolution fusion | flops 1174405120 | bytes 11337728 | tf_op jit(solution)/shard_map/dot_general | solution.py:64
  297.1 0.0 slice-done
  297.1 0.0 slice-done.1
  297.1 0.0 slice-done.2
  297.1 0.0 copy-done.1
  297.1 3.6 multiply_convert_fusion.2
  300.7 0.8 maximum_bitcast_fusion
  301.5 59.9 %all-to-all-done.2 = bf16[16,448,256]{2,1,0:T(8,128)(2,1)} async-done(((bf16[16,448,256]{2,1,0:T(8,128)(2,1)}), bf16[16,448,256]{2,1,0:T(8,128)(2,1)}, u32[]{:S(2)}, u32[]{:S(2)}) %all-to-all-start.2) | async-done | bytes 3670048 | tf_op jit(solution)/shard_map/all_to_all | solution.py:55
  361.4 4.3 copy.36
  365.7 0.0 all-gather.8.cloned.1.call-update
  365.7 79.7 %all-gather.8.cloned.1.call-done = bf16[4096,640]{1,0:T(8,128)(2,1)} async-done(((bf16[256,640]{1,0:T(8,128)(2,1)}), bf16[4096,640]{1,0:T(8,128)(2,1)}) %all-gather.8.cloned.1.call-update) | async-done | bytes 5242896 | tf_op jit(solution)/shard_map/all_gather | solution.py:73
  445.4 6.6 %convolution_convert_fusion.2 = bf16[640,448]{0,1:T(8,128)(2,1)S(1)} fusion(bf16[448,4096]{1,0:T(8,128)(2,1)} %bitcast.56, bf16[4096,640]{1,0:T(8,128)(2,1)} %all-gather.8.cloned.1.call-done), kind=kOutput, calls=%fused_computation.12 | convolution fusion | flops 2349096960 | bytes 9486336 | tf_op jit(solution)/shard_map/dot_general | solution.py:74
  452.0 1.1 copy.32
  453.1 1.5 convert_element_type.50
  454.6 0.4 copy.33
  455.0 0.4 copy.34
  455.4 33.4 %all_to_all.36 = bf16[128,5,448]{2,1,0:T(8,128)(2,1)S(1)} all-to-all(bf16[128,5,448]{2,1,0:T(8,128)(2,1)S(1)} %copy.34), channel_id=1, replica_groups=mesh['pipe'=2,'group'=8,'member'=16] {'group','member'}, dimensions={0} | all-to-all | bytes 1146880 | tf_op jit(solution)/shard_map/all_to_all | solution.py:85
  488.8 0.2 copy.38
  489.0 0.8 reshape.137
  489.8 0.0 copy-start.2
  489.8 2.2 fusion
  492.0 11.9 %collective-permute-start = (bf16[128,7168]{1,0:T(8,128)(2,1)S(1)}, bf16[128,7168]{1,0:T(8,128)(2,1)S(1)}, u32[]{:S(2)}, u32[]{:S(2)}) collective-permute-start(bf16[128,7168]{1,0:T(8,128)(2,1)S(1)} %fusion), channel_id=1, source_target_pairs={{0,128},{128,0},{1,129},{129,1},{2,130},{130,2},{3,131},{131,3},{4... | collective-permute-start | bytes 5505032 | tf_op jit(solution)/shard_map/ppermute | solution.py:14
  503.9 0.0 copy-done.2
  503.9 6.5 %fusion.1 = bf16[1,128,7168]{2,1,0:T(8,128)(2,1)} fusion(bf16[640,7168]{1,0:T(8,128)(2,1)} %all-gather.6.cloned.1.call-done, f32[640,128]{0,1:T(8,128)S(1)} %fusion.10, f32[640,128]{0,1:T(8,128)S(1)} %copy-done.2), kind=kOutput, calls=%fused_computation.3 | convolution fusion | flops 1175814144 | bytes 11665408 | tf_op jit(solution)/shard_map/dot_general | solution.py:77
  510.4 0.0 collective-permute-done
  510.4 1.2 copy.40
  (6 shorter events, 0.1 us)
Async XLA Ops:
  7.2 43.5 %copy-start = (bf16[1,128,7168]{2,1,0:T(8,128)(2,1)S(1)}, bf16[1,128,7168]{2,1,0:T(8,128)(2,1)}, u32[]{:S(2)}) copy-start(bf16[1,128,7168]{2,1,0:T(8,128)(2,1)} %param.7) | copy-start | bytes 5505028
  7.2 157.9 %all-gather.6.cloned.1.call-start = ((), (), s32[]{:S(2)}) async-start(), calls=%async_computation.5 | async-start | bytes 9748480 | tf_op jit(solution)/shard_map/all_gather | solution.py:52
  50.7 224.8 %all-gather.4.cloned.1.call-start = ((), (), s32[]{:S(2)}) async-start(), calls=%async_computation.4 | async-start | bytes 9748480 | tf_op jit(solution)/shard_map/all_gather | solution.py:51
  275.5 85.9 %all-to-all-start.2 = ((bf16[16,448,256]{2,1,0:T(8,128)(2,1)}), bf16[16,448,256]{2,1,0:T(8,128)(2,1)}, u32[]{:S(2)}, u32[]{:S(2)}) async-start(bf16[16,448,256]{2,1,0:T(8,128)(2,1)} %bitcast.51), calls=%async_computation.2 | async-start | bytes 7340032 | tf_op jit(solution)/shard_map/all_to_all | solution.py:55
  283.0 162.4 %all-gather.8.cloned.1.call-start = ((), (), s32[]{:S(2)}) async-start(), calls=%async_computation.6 | async-start | bytes 5570560 | tf_op jit(solution)/shard_map/all_gather | solution.py:73
  283.2 7.1 %copy-start.3 = (bf16[1,128,7168]{2,1,0:T(8,128)(2,1)S(1)}, bf16[1,128,7168]{2,1,0:T(8,128)(2,1)}, u32[]{:S(2)}) copy-start(bf16[1,128,7168]{2,1,0:T(8,128)(2,1)} %param.11) | copy-start | bytes 5505028
  283.2 13.8 %slice-start = ((s8[9175040]{0:T(1024)(128)(4,1)}), s8[4194304]{0:T(1024)(128)(4,1)S(1)}, s32[]{:S(2)}) async-start(s8[9175040]{0:T(1024)(128)(4,1)} %bitcast.49), calls=%async_computation.7 | async-start | bytes 8388608
  283.3 13.8 %slice-start.1 = ((s8[9175040]{0:T(1024)(128)(4,1)}), s8[4194304]{0:T(1024)(128)(4,1)S(1)}, s32[]{:S(2)}) async-start(s8[9175040]{0:T(1024)(128)(4,1)} %bitcast.49), calls=%async_computation.8 | async-start | bytes 8388608
  290.3 6.8 %slice-start.2 = ((s8[9175040]{0:T(1024)(128)(4,1)}), s8[786432]{0:T(1024)(128)(4,1)S(1)}, s32[]{:S(2)}) async-start(s8[9175040]{0:T(1024)(128)(4,1)} %bitcast.49), calls=%async_computation.9 | async-start | bytes 1572864
  290.3 6.7 %copy-start.1 = (bf16[1,7168,128]{2,1,0:T(8,128)(2,1)S(1)}, bf16[1,7168,128]{2,1,0:T(8,128)(2,1)}, u32[]{:S(2)}) copy-start(bf16[1,7168,128]{2,1,0:T(8,128)(2,1)} %param.9) | copy-start | bytes 5505028
  489.8 14.1 %copy-start.2 = (f32[640,128]{0,1:T(8,128)S(1)}, f32[640,128]{0,1:T(8,128)}, u32[]{:S(2)}) copy-start(f32[640,128]{0,1:T(8,128)} %get-tuple-element.14) | copy-start | bytes 983044
  492.0 18.3 %collective-permute-start = (bf16[128,7168]{1,0:T(8,128)(2,1)S(1)}, bf16[128,7168]{1,0:T(8,128)(2,1)S(1)}, u32[]{:S(2)}, u32[]{:S(2)}) collective-permute-start(bf16[128,7168]{1,0:T(8,128)(2,1)S(1)} %fusion), channel_id=1, source_target_pairs={{0,128},{128,0},{1,129},{129,1},{2,130},{130,2},{3,131},{131,3},{4... | collective-permute-start | bytes 5505032 | tf_op jit(solution)/shard_map/ppermute | solution.py:14
Sparse Core Ops, SparseCore 0:
  50.8 114.2 all-gather.5
  167.5 107.9 all-gather.3
  365.8 79.5 all-gather.7

commit v8 on v7

--- a/solution.py
+++ b/solution.py
@@ -43,13 +43,24 @@
         live_count * slot_count, 1
     )
     rows_grad = (chosen_grads * slot_gate).astype(jnp.bfloat16)
-    send_in = rows_in.reshape(live_count, slot_count, model_width)
-    send_grad = rows_grad.reshape(live_count, slot_count, model_width)
+    send = jnp.concatenate(
+        [
+            rows_in.reshape(live_count, slot_count, model_width),
+            rows_grad.reshape(live_count, slot_count, model_width),
+        ],
+        axis=1,
+    )
+    near = lax.all_to_all(send, "group", 0, 0, tiled=True)
     near_rows = live_count * slot_count
-    near_in = lax.all_to_all(send_in, "group", 0, 0, tiled=True).reshape(near_rows, model_width)
-    near_grad = lax.all_to_all(send_grad, "group", 0, 0, tiled=True).reshape(near_rows, model_width)
-    got_in = lax.all_gather(near_in, "member", axis=0, tiled=True)
-    got_grad = lax.all_gather(near_grad, "member", axis=0, tiled=True)
+    near = jnp.stack(
+        [
+            near[:, :slot_count].reshape(near_rows, model_width),
+            near[:, slot_count:].reshape(near_rows, model_width),
+        ]
+    )
+    got = lax.all_gather(near, "member", axis=1, tiled=True)
+    got_in = got[0]
+    got_grad = got[1]
     both_cols = jnp.concatenate([gate_cols, up_cols], axis=1)
     both_cols, got_in, got_grad = lax.optimization_barrier((both_cols, got_in, got_grad))
     both_slice = lax.all_to_all(both_cols, "member", 0, 1, tiled=True)

time: 521 us -> 530 us (1.017)
  blocking collectives: 106 us -> 89.8 us
  local copies, waits for them, and re-layouts: 15.3 us -> 28.2 us
  waiting for transfers between devices: 321 us -> 333 us
    all_to_all x2 -> x1, blocking collectives: 72.9 us -> 56.4 us  [body(): near = lax.all_to_all(send, 'group', 0, 0, tiled=True)]
    squeeze x0 -> x1, local copies, waits for them, and re-layouts: none -> 14.2 us  [body(): got_grad = got[1]]
    all_gather x2 -> x1, waiting for transfers between devices: 182 us -> 193 us  [body(): got = lax.all_gather(near, 'member', axis=1, tiled=True)]
  transfers between devices with their start and end apart: 5 -> 4, of which waited for: 4 -> 3; matrix products, arithmetic and copies ran while one was open for 6% -> 5% of each run, Pallas kernels for 0% -> 0%
where the time goes in v8:
time: 530 us; the launch traced here: 527 us
  waiting for transfers between devices  333 us (63%)
  blocking collectives  89.8 us (17%)
  matrix products  32.9 us (6%)
  local copies, waits for them, and re-layouts  28.2 us (5%)
  starting transfers between devices  19.5 us (4%)
  between operations  14.3 us (3%)
  other arithmetic  9.22 us (2%)
    all_gather x1, waiting for transfers between devices, body(): got = lax.all_gather(near, 'member', axis=1, tiled=True)  193 us
    all_gather x1, waiting for transfers between devices, body(): all_grad = lax.all_gather(both_grad, 'member', axis=0, tiled=True)  79.8 us
    all_to_all x1, waiting for transfers between devices, body(): both_slice = lax.all_to_all(both_cols, 'member', 0, 1, tiled=True)  60.3 us
    all_to_all x1, blocking collectives, body(): near = lax.all_to_all(send, 'group', 0, 0, tiled=True)  56.4 us
    all_to_all x1, blocking collectives, body(): lax.all_to_all(slice_value.astype(jnp.bfloat16), ('group', 'member'), 0,...  33.4 us
    squeeze x1, local copies, waits for them, and re-layouts, body(): got_grad = got[1]  14.2 us
    ppermute x1, starting transfers between devices, from_behind(): return lax.ppermute(value, axis, pairs)  11.8 us
  transfers between devices with their start and end apart: 4, of which 3 were waited for; matrix products, arithmetic and copies ran while one was open for 5% of the time, Pallas kernels for 0%

profile of v8, /device:TPU:33, one launch (start us, length us, event | category | flops | bytes accessed | tf_op | source)
XLA Modules:
  0.0 526.9 jit_solution(3968877872113071449)
XLA Ops:
  7.2 0.0 copy-start
  7.2 0.0 all-gather.3.cloned.1.call-start
  7.2 0.8 convert_reduce_fusion
  8.1 0.1 copy.28
  8.2 0.7 select_reduce_fusion.1
  8.9 0.2 reduce_window_sum.11
  9.2 0.1 select_reduce_fusion
  9.2 0.1 mul.41
  9.3 1.9 fusion.2
  11.2 0.3 reshape.127
  11.5 0.0 copy-done
  11.5 0.4 convolution_convert_fusion.1
  11.9 0.3 reshape.126
  12.2 0.6 pad_maximum_fusion.1
  12.8 56.4 %all_to_all.29 = bf16[8,10,7168]{2,1,0:T(8,128)(2,1)S(1)} all-to-all(bf16[8,10,7168]{2,1,0:T(8,128)(2,1)S(1)} %pad_maximum_fusion.1), channel_id=1, replica_groups=mesh['pipe'=2,'group'=8,'member'=16] {'group'}, dimensions={0} | all-to-all | bytes 2293760 | tf_op jit(solution)/shard_map/all_to_all | solution.py:53
  69.2 1.3 fusion.15
  70.5 1.4 stack_reshape.6
  71.9 1.1 stack_reshape.7
  73.0 0.0 copy-start.2
  73.0 2.3 pad_maximum_fusion.2
  75.3 0.0 all-gather.3.cloned.1.call-update
  75.3 0.0 copy-done.2
  75.3 3.7 pad_maximum_fusion
  79.0 192.9 %all-gather.3.cloned.1.call-done = bf16[2,640,7168]{2,1,0:T(8,128)(2,1)} async-done(((bf16[2,40,7168]{2,1,0:T(8,128)(2,1)}), bf16[2,640,7168]{2,1,0:T(8,128)(2,1)}) %all-gather.3.cloned.1.call-update) | async-done | bytes 18350096 | tf_op jit(solution)/shard_map/all_gather | solution.py:61
  271.9 14.2 %slice_bitcast_fusion = (bf16[640,7168]{1,0:T(8,128)(2,1)}, bf16[640,7168]{1,0:T(8,128)(2,1)}) fusion(bf16[2,640,7168]{2,1,0:T(8,128)(2,1)} %all-gather.3.cloned.1.call-done), kind=kLoop, calls=%fused_computation | loop fusion | bytes 36700160 | tf_op jit(solution)/shard_map/squeeze | solution.py:63
  286.2 7.5 %all-to-all-start.1 = ((bf16[16,448,256]{2,1,0:T(8,128)(2,1)}), bf16[16,448,256]{2,1,0:T(8,128)(2,1)}, u32[]{:S(2)}, u32[]{:S(2)}) async-start(bf16[16,448,256]{2,1,0:T(8,128)(2,1)} %bitcast.55), calls=%async_computation.1 | async-start | bytes 7340032 | tf_op jit(solution)/shard_map/all_to_all | solution.py:66
  293.6 0.2 all-gather.5.cloned.1.call-start
  293.9 0.0 copy-start.6
  293.9 0.0 slice-start
  293.9 0.0 slice-start.1
  293.9 6.5 %fusion.10 = f32[640,128]{0,1:T(8,128)S(1)} fusion(bf16[640,7168]{1,0:T(8,128)(2,1)} %get-tuple-element.9, bf16[1,7168,128]{2,1,0:T(8,128)(2,1)S(1)} %copy-done.2), kind=kOutput, calls=%fused_computation.31 | convolution fusion | flops 1174405120 | bytes 11337728 | tf_op jit(solution)/shard_map/dot_general | solution.py:70
  300.5 0.0 copy-done.6
  300.5 0.0 slice-start.2
  300.5 0.0 copy-start.3
  300.5 6.7 %fusion.3 = f32[640,128]{0,1:T(8,128)S(1)} fusion(bf16[640,7168]{1,0:T(8,128)(2,1)} %get-tuple-element.8, bf16[1,128,7168]{2,1,0:T(8,128)(2,1)S(1)} %copy-done.6), kind=kOutput, calls=%fused_computation.11 | convolution fusion | flops 1174405120 | bytes 11337728 | tf_op jit(solution)/shard_map/dot_general | solution.py:75
  307.2 0.0 slice-done
  307.2 0.0 slice-done.1
  307.2 0.0 slice-done.2
  307.2 0.0 copy-done.3
  307.2 3.7 multiply_convert_fusion.2
  310.9 0.8 maximum_bitcast_fusion
  311.6 60.3 %all-to-all-done.1 = bf16[16,448,256]{2,1,0:T(8,128)(2,1)} async-done(((bf16[16,448,256]{2,1,0:T(8,128)(2,1)}), bf16[16,448,256]{2,1,0:T(8,128)(2,1)}, u32[]{:S(2)}, u32[]{:S(2)}) %all-to-all-start.1) | async-done | bytes 3670048 | tf_op jit(solution)/shard_map/all_to_all | solution.py:66
  372.0 4.4 copy.36
  376.3 0.0 all-gather.5.cloned.1.call-update
  376.4 79.8 %all-gather.5.cloned.1.call-done = bf16[4096,640]{1,0:T(8,128)(2,1)} async-done(((bf16[256,640]{1,0:T(8,128)(2,1)}), bf16[4096,640]{1,0:T(8,128)(2,1)}) %all-gather.5.cloned.1.call-update) | async-done | bytes 5242896 | tf_op jit(solution)/shard_map/all_gather | solution.py:84
  456.1 6.6 %convolution_convert_fusion.2 = bf16[640,448]{0,1:T(8,128)(2,1)S(1)} fusion(bf16[448,4096]{1,0:T(8,128)(2,1)} %bitcast.60, bf16[4096,640]{1,0:T(8,128)(2,1)} %all-gather.5.cloned.1.call-done), kind=kOutput, calls=%fused_computation.15 | convolution fusion | flops 2349096960 | bytes 9486336 | tf_op jit(solution)/shard_map/dot_general | solution.py:85
  462.7 0.3 copy.32
  463.0 0.3 convert_element_type.50
  463.3 0.4 copy.33
  463.7 0.4 copy.34
  464.1 33.4 %all_to_all.30 = bf16[128,5,448]{2,1,0:T(8,128)(2,1)S(1)} all-to-all(bf16[128,5,448]{2,1,0:T(8,128)(2,1)S(1)} %copy.34), channel_id=1, replica_groups=mesh['pipe'=2,'group'=8,'member'=16] {'group','member'}, dimensions={0} | all-to-all | bytes 1146880 | tf_op jit(solution)/shard_map/all_to_all | solution.py:96
  497.5 0.0 copy-start.4
  497.5 0.2 copy.38
  497.7 0.8 reshape.129
  498.5 0.5 copy-done.4
  499.0 0.0 copy-start.5
  499.0 0.7 fusion
  499.7 11.8 %collective-permute-start = (bf16[128,7168]{1,0:T(8,128)(2,1)S(1)}, bf16[128,7168]{1,0:T(8,128)(2,1)S(1)}, u32[]{:S(2)}, u32[]{:S(2)}) collective-permute-start(bf16[128,7168]{1,0:T(8,128)(2,1)S(1)} %fusion), channel_id=1, source_target_pairs={{0,128},{128,0},{1,129},{129,1},{2,130},{130,2},{3,131},{131,3},{4... | collective-permute-start | bytes 5505032 | tf_op jit(solution)/shard_map/ppermute | solution.py:14
  511.5 0.0 copy-done.5
  511.5 6.5 %fusion.1 = bf16[1,128,7168]{2,1,0:T(8,128)(2,1)} fusion(bf16[640,7168]{1,0:T(8,128)(2,1)} %get-tuple-element.8, f32[640,128]{0,1:T(8,128)S(1)} %fusion.10, f32[640,128]{0,1:T(8,128)S(1)} %copy-done.5), kind=kOutput, calls=%fused_computation.5 | convolution fusion | flops 1175814144 | bytes 11665408 | tf_op jit(solution)/shard_map/dot_general | solution.py:88
  517.9 0.0 collective-permute-done
  517.9 0.0 copy-start.1
  517.9 1.2 copy.40
  519.2 0.9 copy-done.1
  (6 shorter events, 0.1 us)
Async XLA Ops:
  7.2 4.3 copy-start
  7.2 264.8 %all-gather.3.cloned.1.call-start = ((), (), s32[]{:S(2)}) async-start(), calls=%async_computation.3 | async-start | bytes 19496960 | tf_op jit(solution)/shard_map/all_gather | solution.py:61
  73.0 2.3 copy-start.2
  286.2 85.8 %all-to-all-start.1 = ((bf16[16,448,256]{2,1,0:T(8,128)(2,1)}), bf16[16,448,256]{2,1,0:T(8,128)(2,1)}, u32[]{:S(2)}, u32[]{:S(2)}) async-start(bf16[16,448,256]{2,1,0:T(8,128)(2,1)} %bitcast.55), calls=%async_computation.1 | async-start | bytes 7340032 | tf_op jit(solution)/shard_map/all_to_all | solution.py:66
  293.6 162.5 %all-gather.5.cloned.1.call-start = ((), (), s32[]{:S(2)}) async-start(), calls=%async_computation.4 | async-start | bytes 5570560 | tf_op jit(solution)/shard_map/all_gather | solution.py:84
  293.9 6.6 %copy-start.6 = (bf16[1,128,7168]{2,1,0:T(8,128)(2,1)S(1)}, bf16[1,128,7168]{2,1,0:T(8,128)(2,1)}, u32[]{:S(2)}) copy-start(bf16[1,128,7168]{2,1,0:T(8,128)(2,1)} %param.11) | copy-start | bytes 5505028
  293.9 13.3 %slice-start = ((s8[9175040]{0:T(1024)(128)(4,1)}), s8[4194304]{0:T(1024)(128)(4,1)S(1)}, s32[]{:S(2)}) async-start(s8[9175040]{0:T(1024)(128)(4,1)} %bitcast.53), calls=%async_computation.5 | async-start | bytes 8388608
  293.9 13.3 %slice-start.1 = ((s8[9175040]{0:T(1024)(128)(4,1)}), s8[4194304]{0:T(1024)(128)(4,1)S(1)}, s32[]{:S(2)}) async-start(s8[9175040]{0:T(1024)(128)(4,1)} %bitcast.53), calls=%async_computation.6 | async-start | bytes 8388608
  300.5 6.7 %slice-start.2 = ((s8[9175040]{0:T(1024)(128)(4,1)}), s8[786432]{0:T(1024)(128)(4,1)S(1)}, s32[]{:S(2)}) async-start(s8[9175040]{0:T(1024)(128)(4,1)} %bitcast.53), calls=%async_computation.7 | async-start | bytes 1572864
  300.5 6.7 %copy-start.3 = (bf16[1,7168,128]{2,1,0:T(8,128)(2,1)S(1)}, bf16[1,7168,128]{2,1,0:T(8,128)(2,1)}, u32[]{:S(2)}) copy-start(bf16[1,7168,128]{2,1,0:T(8,128)(2,1)} %param.9) | copy-start | bytes 5505028
  497.5 1.5 copy-start.4
  499.0 12.5 %copy-start.5 = (f32[640,128]{0,1:T(8,128)S(1)}, f32[640,128]{0,1:T(8,128)}, u32[]{:S(2)}) copy-start(f32[640,128]{0,1:T(8,128)} %get-tuple-element.18) | copy-start | bytes 983044
  499.7 18.2 %collective-permute-start = (bf16[128,7168]{1,0:T(8,128)(2,1)S(1)}, bf16[128,7168]{1,0:T(8,128)(2,1)S(1)}, u32[]{:S(2)}, u32[]{:S(2)}) collective-permute-start(bf16[128,7168]{1,0:T(8,128)(2,1)S(1)} %fusion), channel_id=1, source_target_pairs={{0,128},{128,0},{1,129},{129,1},{2,130},{130,2},{3,131},{131,3},{4... | collective-permute-start | bytes 5505032 | tf_op jit(solution)/shard_map/ppermute | solution.py:14
  517.9 2.2 copy-start.1
Sparse Core Ops, SparseCore 0:
  75.4 196.4 all-gather.2
  376.5 79.5 all-gather.4

commit v9 on v7

--- a/solution.py
+++ b/solution.py
@@ -50,9 +50,10 @@
     near_grad = lax.all_to_all(send_grad, "group", 0, 0, tiled=True).reshape(near_rows, model_width)
     got_in = lax.all_gather(near_in, "member", axis=0, tiled=True)
     got_grad = lax.all_gather(near_grad, "member", axis=0, tiled=True)
-    both_cols = jnp.concatenate([gate_cols, up_cols], axis=1)
-    both_cols, got_in, got_grad = lax.optimization_barrier((both_cols, got_in, got_grad))
-    both_slice = lax.all_to_all(both_cols, "member", 0, 1, tiled=True)
+    gate_src, got_in, got_grad = lax.optimization_barrier((gate_cols, got_in, got_grad))
+    gate_slice = lax.all_to_all(gate_src, "member", 0, 1, tiled=True)
+    up_src, gate_slice = lax.optimization_barrier((up_cols, gate_slice))
+    up_slice = lax.all_to_all(up_src, "member", 0, 1, tiled=True)
     members = lax.axis_size("member")
     groups = live_count
     gate_pre = jnp.dot(got_in, gate_cols, preferred_element_type=jnp.float32)
@@ -68,11 +69,16 @@
         jnp.bfloat16
     )
     grad_up = (back_hidden * silu_gate).astype(jnp.bfloat16)
-    both_grad = jnp.concatenate([grad_gate, grad_up], axis=1).T
-    both_slice, both_grad = lax.optimization_barrier((both_slice, both_grad))
-    all_grad = lax.all_gather(both_grad, "member", axis=0, tiled=True)
+    gate_slice, grad_gate = lax.optimization_barrier((gate_slice, grad_gate.T))
+    all_gate = lax.all_gather(grad_gate, "member", axis=0, tiled=True)
+    up_slice, grad_up = lax.optimization_barrier((up_slice, grad_up.T))
+    all_up = lax.all_gather(grad_up, "member", axis=0, tiled=True)
+    grad_first = (((0,), (1,)), ((), ()))
     slice_value = lax.dot_general(
-        all_grad, both_slice, (((0,), (1,)), ((), ())), preferred_element_type=jnp.float32
+        all_gate, gate_slice, grad_first, preferred_element_type=jnp.float32
+    )
+    slice_value = slice_value + lax.dot_general(
+        all_up, up_slice, grad_first, preferred_element_type=jnp.float32
     )
     down_part = lax.dot_general(
         hidden, got_grad, rows_first, preferred_element_type=jnp.float32

time: 521 us -> 559 us (1.073)
  blocking collectives: 106 us -> 168 us
  waiting for transfers between devices: 321 us -> 302 us
    all_to_all x0 -> x1, blocking collectives: none -> 65.9 us  [body(): up_slice = lax.all_to_all(up_src, 'member', 0, 1, tiled=True)]
    all_to_all x1, waiting for transfers between devices: 59.9 us -> 23.7 us  [body(): gate_slice = lax.all_to_all(gate_src, 'member', 0, 1, tiled=True)]
    all_gather x1 -> x2, waiting for transfers between devices: 79.7 us -> 92 us  [the longest x1 73.1 us: body(): all_up = lax.all_gather(grad_up, 'member', axis=0, tiled=True)]
  transfers between devices with their start and end apart: 5 -> 6, of which waited for: 4 -> 5; matrix products, arithmetic and copies ran while one was open for 6% -> 6% of each run, Pallas kernels for 0% -> 0%
where the time goes in v9:
time: 559 us; the launch traced here: 556 us
  waiting for transfers between devices  302 us (54%)
  blocking collectives  168 us (30%)
  matrix products  36.5 us (7%)
  starting transfers between devices  19.2 us (3%)
  local copies, waits for them, and re-layouts  14.1 us (3%)
  between operations  14 us (3%)
    all_gather x1, waiting for transfers between devices, body(): got_in = lax.all_gather(near_in, 'member', axis=0, tiled=True)  110 us
    all_gather x1, waiting for transfers between devices, body(): got_grad = lax.all_gather(near_grad, 'member', axis=0, tiled=True)  75.5 us
    all_gather x1, waiting for transfers between devices, body(): all_up = lax.all_gather(grad_up, 'member', axis=0, tiled=True)  73.1 us
    all_to_all x1, blocking collectives, body(): up_slice = lax.all_to_all(up_src, 'member', 0, 1, tiled=True)  65.9 us
    all_to_all x1, blocking collectives, body(): lax.all_to_all(send_grad, 'group', 0, 0, tiled=True)  36.9 us
    all_to_all x1, blocking collectives, body(): lax.all_to_all(send_in, 'group', 0, 0, tiled=True)  36 us
    all_to_all x1, blocking collectives, body(): lax.all_to_all(slice_value.astype(jnp.bfloat16), ('group', 'member'), 0,...  29.6 us
    all_to_all x1, waiting for transfers between devices, body(): gate_slice = lax.all_to_all(gate_src, 'member', 0, 1, tiled=True)  23.7 us
  transfers between devices with their start and end apart: 6, of which 5 were waited for; matrix products, arithmetic and copies ran while one was open for 6% of the time, Pallas kernels for 0%

profile of v9, /device:TPU:33, one launch (start us, length us, event | category | flops | bytes accessed | tf_op | source)
XLA Modules:
  0.0 555.7 jit_solution(1303365051019503134)
XLA Ops:
  7.2 0.0 copy-start
  7.2 0.0 all-gather.7.cloned.1.call-start
  7.2 0.8 convert_reduce_fusion
  8.1 0.1 copy.30
  8.2 0.2 reduce_window_sum.11
  8.5 0.7 select_reduce_fusion.1
  9.2 0.1 select_reduce_fusion
  9.3 0.1 mul.49
  9.4 1.9 fusion.2
  11.2 0.3 reshape.137
  11.5 36.9 %all_to_all.53 = bf16[8,5,7168]{2,1,0:T(8,128)(2,1)} all-to-all(bf16[8,5,7168]{2,1,0:T(8,128)(2,1)S(1)} %reshape.137), channel_id=1, replica_groups=mesh['pipe'=2,'group'=8,'member'=16] {'group'}, dimensions={0} | all-to-all | bytes 1146880 | tf_op jit(solution)/shard_map/all_to_all | solution.py:50
  48.4 2.3 reshape.138
  50.6 0.0 all-gather.7.cloned.1.call-update
  50.7 0.0 all-gather.5.cloned.1.call-start
  50.7 0.0 copy-done
  50.7 0.4 convolution_convert_fusion.1
  51.1 0.3 reshape.135
  51.4 36.0 %all_to_all.54 = bf16[8,5,7168]{2,1,0:T(8,128)(2,1)} all-to-all(bf16[8,5,7168]{2,1,0:T(8,128)(2,1)S(1)} %reshape.135), channel_id=1, replica_groups=mesh['pipe'=2,'group'=8,'member'=16] {'group'}, dimensions={0} | all-to-all | bytes 1146880 | tf_op jit(solution)/shard_map/all_to_all | solution.py:49
  87.4 2.3 reshape.136
  89.6 0.0 all-gather.5.cloned.1.call-update
  89.6 75.5 %all-gather.7.cloned.1.call-done = bf16[640,7168]{1,0:T(8,128)(2,1)} async-done(((bf16[40,7168]{1,0:T(8,128)(2,1)}), bf16[640,7168]{1,0:T(8,128)(2,1)}) %all-gather.7.cloned.1.call-update) | async-done | bytes 9175056 | tf_op jit(solution)/shard_map/all_gather | solution.py:52
  165.1 110.4 %all-gather.5.cloned.1.call-done = bf16[640,7168]{1,0:T(8,128)(2,1)} async-done(((bf16[40,7168]{1,0:T(8,128)(2,1)}), bf16[640,7168]{1,0:T(8,128)(2,1)}) %all-gather.5.cloned.1.call-update) | async-done | bytes 9175056 | tf_op jit(solution)/shard_map/all_gather | solution.py:51
  275.5 7.4 %all-to-all-start.2 = ((bf16[16,448,128]{2,1,0:T(8,128)(2,1)}), bf16[16,448,128]{2,1,0:T(8,128)(2,1)}, u32[]{:S(2)}, u32[]{:S(2)}) async-start(bf16[16,448,128]{2,1,0:T(8,128)(2,1)} %bitcast.99), calls=%async_computation.2 | async-start | bytes 3670016 | tf_op jit(solution)/shard_map/all_to_all | solution.py:54
  282.9 0.0 all-gather.9.cloned.1.call-start
  283.0 0.0 copy-start.1
  283.0 0.0 slice-start
  283.0 0.0 slice-start.1
  283.0 6.8 %fusion.22 = f32[640,128]{1,0:T(8,128)S(1)} fusion(bf16[640,7168]{1,0:T(8,128)(2,1)} %all-gather.5.cloned.1.call-done, bf16[1,7168,128]{2,1,0:T(8,128)(2,1)} %param.9), kind=kOutput, calls=%fused_computation.39 | convolution fusion | flops 1174405120 | bytes 11337728 | tf_op jit(solution)/shard_map/dot_general | solution.py:59
  289.8 0.0 copy-done.1
  289.8 0.0 copy-start.2
  289.8 0.0 slice-start.2
  289.8 0.0 copy-start.6
  289.9 6.3 %fusion.24 = f32[640,128]{1,0:T(8,128)S(1)} fusion(bf16[640,7168]{1,0:T(8,128)(2,1)} %all-gather.5.cloned.1.call-done, bf16[1,7168,128]{2,1,0:T(8,128)(2,1)S(1)} %copy-done.1), kind=kOutput, calls=%fused_computation.41 | convolution fusion | flops 1174405120 | bytes 11337728 | tf_op jit(solution)/shard_map/dot_general | solution.py:60
  296.2 0.0 copy-done.2
  296.2 0.0 copy-start.4
  296.2 0.7 copy-done.4
  296.9 0.0 slice-done
  296.9 0.0 slice-done.1
  296.9 0.0 slice-done.2
  296.9 0.0 copy-done.6
  296.9 3.3 fusion.18
  300.2 23.7 %all-to-all-done.2 = bf16[16,448,128]{2,1,0:T(8,128)(2,1)} async-done(((bf16[16,448,128]{2,1,0:T(8,128)(2,1)}), bf16[16,448,128]{2,1,0:T(8,128)(2,1)}, u32[]{:S(2)}, u32[]{:S(2)}) %all-to-all-start.2) | async-done | bytes 1835040 | tf_op jit(solution)/shard_map/all_to_all | solution.py:54
  323.9 3.0 copy_bitcast_fusion.1
  326.9 0.0 all-gather.9.cloned.1.call-update
  326.9 0.0 all-gather.11.cloned.1.call-start
  327.0 65.9 %all_to_all.55 = bf16[16,448,128]{2,1,0:T(8,128)(2,1)S(1)} all-to-all(bf16[16,448,128]{2,1,0:T(8,128)(2,1)} %bitcast.100), channel_id=1, replica_groups=mesh['pipe'=2,'group'=8,'member'=16] {'member'}, dimensions={0} | all-to-all | bytes 3670016 | tf_op jit(solution)/shard_map/all_to_all | solution.py:56
  392.9 1.5 copy_bitcast_fusion
  394.4 0.0 all-gather.11.cloned.1.call-update
  394.4 18.8 %all-gather.9.cloned.1.call-done = bf16[2048,640]{0,1:T(8,128)(2,1)} async-done(((bf16[128,640]{0,1:T(8,128)(2,1)}), bf16[2048,640]{0,1:T(8,128)(2,1)}) %all-gather.9.cloned.1.call-update) | async-done | bytes 2621456 | tf_op jit(solution)/shard_map/all_gather | solution.py:73
  413.2 4.9 fusion.27
  418.2 73.1 %all-gather.11.cloned.1.call-done = bf16[2048,640]{0,1:T(8,128)(2,1)} async-done(((bf16[128,640]{0,1:T(8,128)(2,1)}), bf16[2048,640]{0,1:T(8,128)(2,1)}) %all-gather.11.cloned.1.call-update) | async-done | bytes 2621456 | tf_op jit(solution)/shard_map/all_gather | solution.py:75
  491.3 4.2 fusion.7
  495.5 0.2 copy.35
  495.8 0.3 convert_element_type.52
  496.1 0.4 copy.36
  496.5 0.4 copy.37
  496.9 29.6 %all_to_all.56 = bf16[128,5,448]{2,1,0:T(8,128)(2,1)S(1)} all-to-all(bf16[128,5,448]{2,1,0:T(8,128)(2,1)S(1)} %copy.37), channel_id=1, replica_groups=mesh['pipe'=2,'group'=8,'member'=16] {'group','member'}, dimensions={0} | all-to-all | bytes 1146880 | tf_op jit(solution)/shard_map/all_to_all | solution.py:91
  526.5 0.2 copy.44
  526.8 0.8 reshape.140
  527.5 2.2 fusion
  529.8 11.6 %collective-permute-start = (bf16[128,7168]{1,0:T(8,128)(2,1)S(1)}, bf16[128,7168]{1,0:T(8,128)(2,1)S(1)}, u32[]{:S(2)}, u32[]{:S(2)}) collective-permute-start(bf16[128,7168]{1,0:T(8,128)(2,1)S(1)} %fusion), channel_id=1, source_target_pairs={{0,128},{128,0},{1,129},{129,1},{2,130},{130,2},{3,131},{131,3},{4... | collective-permute-start | bytes 5505032 | tf_op jit(solution)/shard_map/ppermute | solution.py:14
  541.4 6.5 %fusion.1 = bf16[1,128,7168]{2,1,0:T(8,128)(2,1)} fusion(bf16[640,7168]{1,0:T(8,128)(2,1)} %all-gather.7.cloned.1.call-done, f32[640,128]{1,0:T(8,128)S(1)} %copy-done.5, f32[640,128]{1,0:T(8,128)S(1)} %copy-done.3), kind=kOutput, calls=%fused_computation.3 | convolution fusion | flops 1175814144 | bytes 11665408 | tf_op jit(solution)/shard_map/dot_general | solution.py:83
  548.0 0.0 collective-permute-done
  548.0 1.2 copy.46
  (10 shorter events, 0.1 us)
Async XLA Ops:
  7.2 43.6 %copy-start = (bf16[1,128,7168]{2,1,0:T(8,128)(2,1)S(1)}, bf16[1,128,7168]{2,1,0:T(8,128)(2,1)}, u32[]{:S(2)}) copy-start(bf16[1,128,7168]{2,1,0:T(8,128)(2,1)} %param.7) | copy-start | bytes 5505028
  7.2 157.9 %all-gather.7.cloned.1.call-start = ((), (), s32[]{:S(2)}) async-start(), calls=%async_computation.6 | async-start | bytes 9748480 | tf_op jit(solution)/shard_map/all_gather | solution.py:52
  50.7 224.8 %all-gather.5.cloned.1.call-start = ((), (), s32[]{:S(2)}) async-start(), calls=%async_computation.5 | async-start | bytes 9748480 | tf_op jit(solution)/shard_map/all_gather | solution.py:51
  275.5 48.4 %all-to-all-start.2 = ((bf16[16,448,128]{2,1,0:T(8,128)(2,1)}), bf16[16,448,128]{2,1,0:T(8,128)(2,1)}, u32[]{:S(2)}, u32[]{:S(2)}) async-start(bf16[16,448,128]{2,1,0:T(8,128)(2,1)} %bitcast.99), calls=%async_computation.2 | async-start | bytes 3670016 | tf_op jit(solution)/shard_map/all_to_all | solution.py:54
  282.9 130.3 %all-gather.9.cloned.1.call-start = ((), (), s32[]{:S(2)}) async-start(), calls=%async_computation.7 | async-start | bytes 2785280 | tf_op jit(solution)/shard_map/all_gather | solution.py:73
  283.0 6.8 %copy-start.1 = (bf16[1,7168,128]{2,1,0:T(8,128)(2,1)S(1)}, bf16[1,7168,128]{2,1,0:T(8,128)(2,1)}, u32[]{:S(2)}) copy-start(bf16[1,7168,128]{2,1,0:T(8,128)(2,1)} %param.10) | copy-start | bytes 5505028
  283.0 13.9 %slice-start = ((s8[9175040]{0:T(1024)(128)(4,1)}), s8[4194304]{0:T(1024)(128)(4,1)S(1)}, s32[]{:S(2)}) async-start(s8[9175040]{0:T(1024)(128)(4,1)} %bitcast.93), calls=%async_computation.9 | async-start | bytes 8388608
  283.0 13.9 %slice-start.1 = ((s8[9175040]{0:T(1024)(128)(4,1)}), s8[4194304]{0:T(1024)(128)(4,1)S(1)}, s32[]{:S(2)}) async-start(s8[9175040]{0:T(1024)(128)(4,1)} %bitcast.93), calls=%async_computation.10 | async-start | bytes 8388608
  289.8 6.3 %copy-start.2 = (f32[640,128]{1,0:T(8,128)}, f32[640,128]{1,0:T(8,128)S(1)}, u32[]{:S(2)}) copy-start(f32[640,128]{1,0:T(8,128)S(1)} %fusion.22) | copy-start | bytes 983044
  289.8 7.1 %slice-start.2 = ((s8[9175040]{0:T(1024)(128)(4,1)}), s8[786432]{0:T(1024)(128)(4,1)S(1)}, s32[]{:S(2)}) async-start(s8[9175040]{0:T(1024)(128)(4,1)} %bitcast.93), calls=%async_computation.11 | async-start | bytes 1572864
  289.8 7.1 %copy-start.6 = (bf16[1,128,7168]{2,1,0:T(8,128)(2,1)S(1)}, bf16[1,128,7168]{2,1,0:T(8,128)(2,1)}, u32[]{:S(2)}) copy-start(bf16[1,128,7168]{2,1,0:T(8,128)(2,1)} %param.11) | copy-start | bytes 5505028
  296.2 0.7 copy-start.4
  326.9 164.4 %all-gather.11.cloned.1.call-start = ((), (), s32[]{:S(2)}) async-start(), calls=%async_computation.8 | async-start | bytes 2785280 | tf_op jit(solution)/shard_map/all_gather | solution.py:75
  527.5 13.9 %copy-start.3 = (f32[640,128]{1,0:T(8,128)S(1)}, f32[640,128]{1,0:T(8,128)}, u32[]{:S(2)}) copy-start(f32[640,128]{1,0:T(8,128)} %copy-done.2) | copy-start | bytes 983044
  527.5 13.9 %copy-start.5 = (f32[640,128]{1,0:T(8,128)S(1)}, f32[640,128]{1,0:T(8,128)}, u32[]{:S(2)}) copy-start(f32[640,128]{1,0:T(8,128)} %copy-done.4) | copy-start | bytes 983044
  529.8 18.2 %collective-permute-start = (bf16[128,7168]{1,0:T(8,128)(2,1)S(1)}, bf16[128,7168]{1,0:T(8,128)(2,1)S(1)}, u32[]{:S(2)}, u32[]{:S(2)}) collective-permute-start(bf16[128,7168]{1,0:T(8,128)(2,1)S(1)} %fusion), channel_id=1, source_target_pairs={{0,128},{128,0},{1,129},{129,1},{2,130},{130,2},{3,131},{131,3},{4... | collective-permute-start | bytes 5505032 | tf_op jit(solution)/shard_map/ppermute | solution.py:14
Sparse Core Ops, SparseCore 0:
  50.8 114.2 all-gather.6
  167.5 107.9 all-gather.4
  327.0 86.1 all-gather.8
  414.8 76.4 all-gather.10

commit v10 on v7

--- a/solution.py
+++ b/solution.py
@@ -6,6 +6,7 @@
 
 SHARDS = 16
 CAP = 5
+TILE_ROWS = 16
 
 
 def from_behind(value, axis, steps):
@@ -43,13 +44,16 @@
         live_count * slot_count, 1
     )
     rows_grad = (chosen_grads * slot_gate).astype(jnp.bfloat16)
-    send_in = rows_in.reshape(live_count, slot_count, model_width)
-    send_grad = rows_grad.reshape(live_count, slot_count, model_width)
+    send_in = rows_in.reshape(live_count, TILE_ROWS, -1)
+    send_grad = rows_grad.reshape(live_count, TILE_ROWS, -1)
     near_rows = live_count * slot_count
     near_in = lax.all_to_all(send_in, "group", 0, 0, tiled=True).reshape(near_rows, model_width)
     near_grad = lax.all_to_all(send_grad, "group", 0, 0, tiled=True).reshape(near_rows, model_width)
-    got_in = lax.all_gather(near_in, "member", axis=0, tiled=True)
-    got_grad = lax.all_gather(near_grad, "member", axis=0, tiled=True)
+    piece = (2 * TILE_ROWS, -1)
+    got_in = lax.all_gather(near_in.reshape(piece), "member", axis=0, tiled=True)
+    got_grad = lax.all_gather(near_grad.reshape(piece), "member", axis=0, tiled=True)
+    got_in = got_in.reshape(-1, model_width)
+    got_grad = got_grad.reshape(-1, model_width)
     both_cols = jnp.concatenate([gate_cols, up_cols], axis=1)
     both_cols, got_in, got_grad = lax.optimization_barrier((both_cols, got_in, got_grad))
     both_slice = lax.all_to_all(both_cols, "member", 0, 1, tiled=True)
@@ -70,7 +74,9 @@
     grad_up = (back_hidden * silu_gate).astype(jnp.bfloat16)
     both_grad = jnp.concatenate([grad_gate, grad_up], axis=1).T
     both_slice, both_grad = lax.optimization_barrier((both_slice, both_grad))
-    all_grad = lax.all_gather(both_grad, "member", axis=0, tiled=True)
+    grad_rows = both_grad.shape[1]
+    all_grad = lax.all_gather(both_grad.reshape(piece), "member", axis=0, tiled=True)
+    all_grad = all_grad.reshape(-1, grad_rows)
     slice_value = lax.dot_general(
         all_grad, both_slice, (((0,), (1,)), ((), ())), preferred_element_type=jnp.float32
     )
@@ -82,7 +88,8 @@
     slice_value = jnp.transpose(slice_value, (1, 0, 2, 3)).reshape(
         groups * members, slot_count, slice_width
     )
-    back = lax.all_to_all(slice_value.astype(jnp.bfloat16), ("group", "member"), 0, 0, tiled=True)
+    slice_value = slice_value.astype(jnp.bfloat16).reshape(groups * members, TILE_ROWS, -1)
+    back = lax.all_to_all(slice_value, ("group", "member"), 0, 0, tiled=True)
     back = back.reshape(groups, members, slot_count, slice_width)
     returned = jnp.transpose(back, (0, 2, 1, 3)).reshape(groups * slot_count, model_width)
     returned = returned.astype(jnp.float32)

time: 521 us -> 564 us (1.083)
  local copies, waits for them, and re-layouts: 15.3 us -> 83.1 us
  blocking collectives: 106 us -> 87.1 us
  waiting for transfers between devices: 321 us -> 314 us
    reshape x4 -> x6, local copies, waits for them, and re-layouts: 5.03 us -> 46.6 us  [the longest x1 17.6 us: body(): got_grad = got_grad.reshape(-1, model_width)]
    dot_general x0 -> x2, local copies, waits for them, and re-layouts: none -> 16.4 us  [body(): lax.dot_general(all_grad, both_slice, (((0,), (1,)), ((), ())), preferred...]
    all_to_all x1, blocking collectives: 36 us -> 23.4 us  [body(): lax.all_to_all(send_in, 'group', 0, 0, tiled=True)]
    all_gather x3, waiting for transfers between devices: 261 us -> 252 us  [the longest x1 91.6 us: body(): lax.all_gather(near_in.reshape(piece), 'member', axis=0, tiled=True)]
    all_to_all x1, blocking collectives: 36.9 us -> 30.1 us  [body(): lax.all_to_all(send_grad, 'group', 0, 0, tiled=True)]
  transfers between devices with their start and end apart: 5 -> 5, of which waited for: 4 -> 4; matrix products, arithmetic and copies ran while one was open for 6% -> 8% of each run, Pallas kernels for 0% -> 0%
where the time goes in v10:
time: 564 us; the launch traced here: 560 us
  waiting for transfers between devices  314 us (56%)
  blocking collectives  87.1 us (15%)
  local copies, waits for them, and re-layouts  83.1 us (15%)
  matrix products  37 us (7%)
  starting transfers between devices  19.6 us (3%)
  between operations  14 us (2%)
  other arithmetic  5.69 us (1%)
    all_gather x1, waiting for transfers between devices, body(): lax.all_gather(near_in.reshape(piece), 'member', axis=0, tiled=True)  91.6 us
    all_gather x1, waiting for transfers between devices, body(): lax.all_gather(near_grad.reshape(piece), 'member', axis=0, tiled=True)  80.6 us
    all_gather x1, waiting for transfers between devices, body(): lax.all_gather(both_grad.reshape(piece), 'member', axis=0, tiled=True)  79.7 us
    all_to_all x1, waiting for transfers between devices, body(): both_slice = lax.all_to_all(both_cols, 'member', 0, 1, tiled=True)  61.7 us
    all_to_all x1, blocking collectives, body(): back = lax.all_to_all(slice_value, ('group', 'member'), 0, 0, tiled=True)  33.6 us
    all_to_all x1, blocking collectives, body(): lax.all_to_all(send_grad, 'group', 0, 0, tiled=True)  30.1 us
    all_to_all x1, blocking collectives, body(): lax.all_to_all(send_in, 'group', 0, 0, tiled=True)  23.4 us
    reshape x1, local copies, waits for them, and re-layouts, body(): got_grad = got_grad.reshape(-1, model_width)  17.6 us
  transfers between devices with their start and end apart: 5, of which 4 were waited for; matrix products, arithmetic and copies ran while one was open for 8% of the time, Pallas kernels for 0%

profile of v10, /device:TPU:33, one launch (start us, length us, event | category | flops | bytes accessed | tf_op | source)
XLA Modules:
  0.0 560.1 jit_solution(6593004753852997106)
XLA Ops:
  7.2 0.0 copy-start
  7.2 0.0 all-gather.6.cloned.1.call-start
  7.2 0.8 convert_reduce_fusion
  8.1 0.1 copy.28
  8.2 0.7 select_reduce_fusion.1
  8.9 0.2 reduce_window_sum.11
  9.2 0.1 select_reduce_fusion
  9.2 0.1 mul.41
  9.3 1.9 fusion.2
  11.2 1.0 reshape.142
  12.2 30.1 %all_to_all.34 = bf16[8,16,2240]{2,1,0:T(8,128)(2,1)S(1)} all-to-all(bf16[8,16,2240]{2,1,0:T(8,128)(2,1)S(1)} %reshape.142), channel_id=1, replica_groups=mesh['pipe'=2,'group'=8,'member'=16] {'group'}, dimensions={0} | all-to-all | bytes 1146880 | tf_op jit(solution)/shard_map/all_to_all | solution.py:51
  42.3 1.5 reshape_reshape.7
  43.7 0.0 all-gather.6.cloned.1.call-update
  43.7 0.0 all-gather.4.cloned.1.call-start
  43.8 0.0 copy-done
  43.8 0.4 convolution_convert_fusion.1
  44.2 0.0 copy-start.2
  44.2 1.0 reshape.140
  45.2 23.4 %all_to_all.35 = bf16[8,16,2240]{2,1,0:T(8,128)(2,1)S(1)} all-to-all(bf16[8,16,2240]{2,1,0:T(8,128)(2,1)S(1)} %reshape.140), channel_id=1, replica_groups=mesh['pipe'=2,'group'=8,'member'=16] {'group'}, dimensions={0} | all-to-all | bytes 1146880 | tf_op jit(solution)/shard_map/all_to_all | solution.py:50
  68.6 1.5 reshape_reshape.6
  70.1 0.0 all-gather.4.cloned.1.call-update
  70.1 0.0 copy-done.2
  70.1 3.8 pad_maximum_fusion
  73.9 80.6 %all-gather.6.cloned.1.call-done = bf16[512,8960]{1,0:T(8,128)(2,1)} async-done(((bf16[32,8960]{1,0:T(8,128)(2,1)}), bf16[512,8960]{1,0:T(8,128)(2,1)}) %all-gather.6.cloned.1.call-update) | async-done | bytes 9175056 | tf_op jit(solution)/shard_map/all_gather | solution.py:54
  154.5 17.6 %reshape.143 = bf16[640,7168]{1,0:T(8,128)(2,1)} reshape(bf16[512,8960]{1,0:T(8,128)(2,1)} %all-gather.6.cloned.1.call-done) | data formatting | bytes 18350080 | tf_op jit(solution)/shard_map/reshape | solution.py:56
  172.0 91.6 %all-gather.4.cloned.1.call-done = bf16[512,8960]{1,0:T(8,128)(2,1)} async-done(((bf16[32,8960]{1,0:T(8,128)(2,1)}), bf16[512,8960]{1,0:T(8,128)(2,1)}) %all-gather.4.cloned.1.call-update) | async-done | bytes 9175056 | tf_op jit(solution)/shard_map/all_gather | solution.py:53
  263.6 17.5 %reshape.141 = bf16[640,7168]{1,0:T(8,128)(2,1)} reshape(bf16[512,8960]{1,0:T(8,128)(2,1)} %all-gather.4.cloned.1.call-done) | data formatting | bytes 18350080 | tf_op jit(solution)/shard_map/reshape | solution.py:55
  281.1 7.5 %all-to-all-start.2 = ((bf16[16,448,256]{2,1,0:T(8,128)(2,1)}), bf16[16,448,256]{2,1,0:T(8,128)(2,1)}, u32[]{:S(2)}, u32[]{:S(2)}) async-start(bf16[16,448,256]{2,1,0:T(8,128)(2,1)} %bitcast.58), calls=%async_computation.2 | async-start | bytes 7340032 | tf_op jit(solution)/shard_map/all_to_all | solution.py:59
  288.6 0.2 all-gather.8.cloned.1.call-start
  288.9 0.0 copy-start.5
  288.9 0.0 slice-start
  288.9 0.0 slice-start.1
  288.9 6.5 %fusion.18 = f32[640,128]{0,1:T(8,128)S(1)} fusion(bf16[640,7168]{1,0:T(8,128)(2,1)} %reshape.141, bf16[1,7168,128]{2,1,0:T(8,128)(2,1)S(1)} %copy-done.2), kind=kOutput, calls=%fused_computation.29 | convolution fusion | flops 1174405120 | bytes 11337728 | tf_op jit(solution)/shard_map/dot_general | solution.py:63
  295.4 0.0 copy-done.5
  295.4 0.0 slice-start.2
  295.5 0.0 copy-start.3
  295.5 6.7 %fusion.5 = f32[640,128]{0,1:T(8,128)S(1)} fusion(bf16[640,7168]{1,0:T(8,128)(2,1)} %reshape.143, bf16[1,128,7168]{2,1,0:T(8,128)(2,1)S(1)} %copy-done.5), kind=kOutput, calls=%fused_computation.10 | convolution fusion | flops 1174405120 | bytes 11337728 | tf_op jit(solution)/shard_map/dot_general | solution.py:68
  302.2 0.0 slice-done
  302.2 0.0 slice-done.1
  302.2 0.0 slice-done.2
  302.2 0.0 copy-done.3
  302.2 3.0 multiply_convert_fusion.2
  305.3 61.7 %all-to-all-done.2 = bf16[16,448,256]{2,1,0:T(8,128)(2,1)} async-done(((bf16[16,448,256]{2,1,0:T(8,128)(2,1)}), bf16[16,448,256]{2,1,0:T(8,128)(2,1)}, u32[]{:S(2)}, u32[]{:S(2)}) %all-to-all-start.2) | async-done | bytes 3670048 | tf_op jit(solution)/shard_map/all_to_all | solution.py:59
  367.0 4.4 copy.36
  371.4 0.9 reshape.144
  372.3 0.0 all-gather.8.cloned.1.call-update
  372.3 79.7 %all-gather.8.cloned.1.call-done = bf16[512,5120]{1,0:T(8,128)(2,1)} async-done(((bf16[32,5120]{1,0:T(8,128)(2,1)}), bf16[512,5120]{1,0:T(8,128)(2,1)}) %all-gather.8.cloned.1.call-update) | async-done | bytes 5242896 | tf_op jit(solution)/shard_map/all_gather | solution.py:78
  452.0 8.7 %reshape.145 = bf16[4096,640]{1,0:T(8,128)(2,1)} reshape(bf16[512,5120]{1,0:T(8,128)(2,1)} %all-gather.8.cloned.1.call-done) | data formatting | bytes 10485760 | tf_op jit(solution)/shard_map/reshape | solution.py:79
  460.7 8.0 %copy.32 = bf16[640,4096]{1,0:T(8,128)(2,1)} copy(bf16[640,4096]{0,1:T(8,128)(2,1)} %bitcast.57) | data formatting | bytes 10485760 | tf_op jit(solution)/shard_map/dot_general | solution.py:80
  468.7 8.4 %dot_general.34 = bf16[16,8,5,4096]{3,2,1,0:T(8,128)(2,1)} reshape(bf16[640,4096]{1,0:T(8,128)(2,1)} %copy.32) | data formatting | bytes 10485760 | tf_op jit(solution)/shard_map/dot_general | solution.py:80
  477.1 11.3 %fusion.12 = bf16[8,16,5,448]{3,2,0,1:T(8,128)(2,1)S(1)} fusion(bf16[16,8,5,4096]{3,2,1,0:T(8,128)(2,1)} %dot_general.34, bf16[448,4096]{1,0:T(8,128)(2,1)} %bitcast.62), kind=kOutput, calls=%fused_computation.15 | convolution fusion | flops 2349096960 | bytes 9486336 | tf_op jit(solution)/shard_map/dot_general | solution.py:80
  488.3 0.1 copy.33
  488.4 3.6 convert_element_type.49
  492.1 0.0 copy-start.4
  492.1 33.6 %all_to_all.36 = bf16[128,16,140]{2,1,0:T(8,128)(2,1)} all-to-all(bf16[128,16,140]{2,1,0:T(8,128)(2,1)S(1)} %convert_element_type.49), channel_id=1, replica_groups=mesh['pipe'=2,'group'=8,'member'=16] {'group','member'}, dimensions={0} | all-to-all | bytes 1146880 | tf_op jit(solution)/shard_map/all_to_all | solution.py:92
  525.7 4.6 reshape.146
  530.3 1.1 copy.34
  531.4 1.9 reshape.147
  533.3 0.0 copy-done.4
  533.3 0.7 fusion
  534.0 11.8 %collective-permute-start = (bf16[128,7168]{1,0:T(8,128)(2,1)S(1)}, bf16[128,7168]{1,0:T(8,128)(2,1)S(1)}, u32[]{:S(2)}, u32[]{:S(2)}) collective-permute-start(bf16[128,7168]{1,0:T(8,128)(2,1)S(1)} %fusion), channel_id=1, source_target_pairs={{0,128},{128,0},{1,129},{129,1},{2,130},{130,2},{3,131},{131,3},{4... | collective-permute-start | bytes 5505032 | tf_op jit(solution)/shard_map/ppermute | solution.py:15
  545.8 6.6 %fusion.1 = bf16[1,128,7168]{2,1,0:T(8,128)(2,1)} fusion(bf16[640,7168]{1,0:T(8,128)(2,1)} %reshape.143, f32[640,128]{0,1:T(8,128)S(1)} %fusion.18, f32[640,128]{0,1:T(8,128)S(1)} %get-tuple-element.14), kind=kOutput, calls=%fused_computation.3 | convolution fusion | flops 1175814144 | bytes 11665408 | tf_op jit(solution)/shard_map/dot_general | solution.py:83
  552.3 0.0 collective-permute-done
  552.3 1.2 copy.38
  (9 shorter events, 0.1 us)
Async XLA Ops:
  7.2 36.6 %copy-start = (bf16[1,128,7168]{2,1,0:T(8,128)(2,1)S(1)}, bf16[1,128,7168]{2,1,0:T(8,128)(2,1)}, u32[]{:S(2)}) copy-start(bf16[1,128,7168]{2,1,0:T(8,128)(2,1)} %param.7) | copy-start | bytes 5505028
  7.2 147.3 %all-gather.6.cloned.1.call-start = ((), (), s32[]{:S(2)}) async-start(), calls=%async_computation.5 | async-start | bytes 9748480 | tf_op jit(solution)/shard_map/all_gather | solution.py:54
  43.7 219.9 %all-gather.4.cloned.1.call-start = ((), (), s32[]{:S(2)}) async-start(), calls=%async_computation.4 | async-start | bytes 9748480 | tf_op jit(solution)/shard_map/all_gather | solution.py:53
  44.2 25.9 %copy-start.2 = (bf16[1,7168,128]{2,1,0:T(8,128)(2,1)S(1)}, bf16[1,7168,128]{2,1,0:T(8,128)(2,1)}, u32[]{:S(2)}) copy-start(bf16[1,7168,128]{2,1,0:T(8,128)(2,1)} %param.10) | copy-start | bytes 5505028
  281.1 85.9 %all-to-all-start.2 = ((bf16[16,448,256]{2,1,0:T(8,128)(2,1)}), bf16[16,448,256]{2,1,0:T(8,128)(2,1)}, u32[]{:S(2)}, u32[]{:S(2)}) async-start(bf16[16,448,256]{2,1,0:T(8,128)(2,1)} %bitcast.58), calls=%async_computation.2 | async-start | bytes 7340032 | tf_op jit(solution)/shard_map/all_to_all | solution.py:59
  288.6 163.3 %all-gather.8.cloned.1.call-start = ((), (), s32[]{:S(2)}) async-start(), calls=%async_computation.6 | async-start | bytes 5570560 | tf_op jit(solution)/shard_map/all_gather | solution.py:78
  288.9 6.6 %copy-start.5 = (bf16[1,128,7168]{2,1,0:T(8,128)(2,1)S(1)}, bf16[1,128,7168]{2,1,0:T(8,128)(2,1)}, u32[]{:S(2)}) copy-start(bf16[1,128,7168]{2,1,0:T(8,128)(2,1)} %param.11) | copy-start | bytes 5505028
  288.9 13.3 %slice-start = ((s8[9175040]{0:T(1024)(128)(4,1)}), s8[4194304]{0:T(1024)(128)(4,1)S(1)}, s32[]{:S(2)}) async-start(s8[9175040]{0:T(1024)(128)(4,1)} %bitcast.55), calls=%async_computation.7 | async-start | bytes 8388608
  288.9 13.3 %slice-start.1 = ((s8[9175040]{0:T(1024)(128)(4,1)}), s8[4194304]{0:T(1024)(128)(4,1)S(1)}, s32[]{:S(2)}) async-start(s8[9175040]{0:T(1024)(128)(4,1)} %bitcast.55), calls=%async_computation.8 | async-start | bytes 8388608
  295.4 6.7 %slice-start.2 = ((s8[9175040]{0:T(1024)(128)(4,1)}), s8[786432]{0:T(1024)(128)(4,1)S(1)}, s32[]{:S(2)}) async-start(s8[9175040]{0:T(1024)(128)(4,1)} %bitcast.55), calls=%async_computation.9 | async-start | bytes 1572864
  295.5 6.7 %copy-start.3 = (bf16[1,7168,128]{2,1,0:T(8,128)(2,1)S(1)}, bf16[1,7168,128]{2,1,0:T(8,128)(2,1)}, u32[]{:S(2)}) copy-start(bf16[1,7168,128]{2,1,0:T(8,128)(2,1)} %param.9) | copy-start | bytes 5505028
  492.1 41.2 %copy-start.4 = (bf16[1,128,7168]{2,1,0:T(8,128)(2,1)S(1)}, bf16[1,128,7168]{2,1,0:T(8,128)(2,1)}, u32[]{:S(2)}) copy-start(bf16[1,128,7168]{2,1,0:T(8,128)(2,1)} %param.8) | copy-start | bytes 5505028
  534.0 18.4 %collective-permute-start = (bf16[128,7168]{1,0:T(8,128)(2,1)S(1)}, bf16[128,7168]{1,0:T(8,128)(2,1)S(1)}, u32[]{:S(2)}, u32[]{:S(2)}) collective-permute-start(bf16[128,7168]{1,0:T(8,128)(2,1)S(1)} %fusion), channel_id=1, source_target_pairs={{0,128},{128,0},{1,129},{129,1},{2,130},{130,2},{3,131},{131,3},{4... | collective-permute-start | bytes 5505032 | tf_op jit(solution)/shard_map/ppermute | solution.py:15
  545.8 7.8 %copy-start.1 = (bf16[1,128,7168]{2,1,0:T(8,128)(2,1)S(1)}, bf16[1,128,7168]{2,1,0:T(8,128)(2,1)}, u32[]{:S(2)}) copy-start(bf16[1,128,7168]{2,1,0:T(8,128)(2,1)} %param.7) | copy-start | bytes 5505028
Sparse Core Ops, SparseCore 0:
  43.9 110.5 all-gather.5
  156.8 106.7 all-gather.3
  372.4 79.5 all-gather.7

commit v11 on v7

--- a/solution.py
+++ b/solution.py
@@ -6,6 +6,7 @@
 
 SHARDS = 16
 CAP = 5
+TILE_ROWS = 16
 
 
 def from_behind(value, axis, steps):
@@ -43,8 +44,8 @@
         live_count * slot_count, 1
     )
     rows_grad = (chosen_grads * slot_gate).astype(jnp.bfloat16)
-    send_in = rows_in.reshape(live_count, slot_count, model_width)
-    send_grad = rows_grad.reshape(live_count, slot_count, model_width)
+    send_in = rows_in.reshape(live_count, TILE_ROWS, -1)
+    send_grad = rows_grad.reshape(live_count, TILE_ROWS, -1)
     near_rows = live_count * slot_count
     near_in = lax.all_to_all(send_in, "group", 0, 0, tiled=True).reshape(near_rows, model_width)
     near_grad = lax.all_to_all(send_grad, "group", 0, 0, tiled=True).reshape(near_rows, model_width)

time: 521 us -> 509 us (0.977)
  blocking collectives: 106 us -> 86.8 us
  waiting for transfers between devices: 321 us -> 329 us
    all_to_all x1, blocking collectives: 36 us -> 23.4 us  [body(): lax.all_to_all(send_in, 'group', 0, 0, tiled=True)]
    all_gather x1, waiting for transfers between devices: 71.1 us -> 79.8 us  [body(): got_grad = lax.all_gather(near_grad, 'member', axis=0, tiled=True)]
    all_to_all x1, blocking collectives: 36.9 us -> 30 us  [body(): lax.all_to_all(send_grad, 'group', 0, 0, tiled=True)]
where the time goes in v11:
time: 509 us; the launch traced here: 506 us
  waiting for transfers between devices  329 us (65%)
  blocking collectives  86.8 us (17%)
  matrix products  34.9 us (7%)
  starting transfers between devices  19.6 us (4%)
  local copies, waits for them, and re-layouts  15.6 us (3%)
  between operations  14 us (3%)
  other arithmetic  6.96 us (1%)
    all_gather x1, waiting for transfers between devices, body(): got_in = lax.all_gather(near_in, 'member', axis=0, tiled=True)  109 us
    all_gather x1, waiting for transfers between devices, body(): got_grad = lax.all_gather(near_grad, 'member', axis=0, tiled=True)  79.8 us
    all_gather x1, waiting for transfers between devices, body(): all_grad = lax.all_gather(both_grad, 'member', axis=0, tiled=True)  79.7 us
    all_to_all x1, waiting for transfers between devices, body(): both_slice = lax.all_to_all(both_cols, 'member', 0, 1, tiled=True)  59.9 us
    all_to_all x1, blocking collectives, body(): lax.all_to_all(slice_value.astype(jnp.bfloat16), ('group', 'member'), 0,...  33.3 us
    all_to_all x1, blocking collectives, body(): lax.all_to_all(send_grad, 'group', 0, 0, tiled=True)  30 us
    all_to_all x1, blocking collectives, body(): lax.all_to_all(send_in, 'group', 0, 0, tiled=True)  23.4 us
    ppermute x1, starting transfers between devices, from_behind(): return lax.ppermute(value, axis, pairs)  11.8 us
  transfers between devices with their start and end apart: 5, of which 4 were waited for; matrix products, arithmetic and copies ran while one was open for 6% of the time, Pallas kernels for 0%

profile of v11, /device:TPU:33, one launch (start us, length us, event | category | flops | bytes accessed | tf_op | source)
XLA Modules:
  0.0 506.4 jit_solution(13493357357899167285)
XLA Ops:
  7.2 0.0 copy-start
  7.2 0.0 all-gather.6.cloned.1.call-start
  7.2 0.8 convert_reduce_fusion
  8.1 0.1 copy.28
  8.2 0.2 reduce_window_sum.11
  8.5 0.7 select_reduce_fusion.1
  9.2 0.1 select_reduce_fusion
  9.3 0.1 mul.41
  9.3 1.9 fusion.2
  11.2 1.0 reshape.134
  12.2 30.0 %all_to_all.34 = bf16[8,16,2240]{2,1,0:T(8,128)(2,1)S(1)} all-to-all(bf16[8,16,2240]{2,1,0:T(8,128)(2,1)S(1)} %reshape.134), channel_id=1, replica_groups=mesh['pipe'=2,'group'=8,'member'=16] {'group'}, dimensions={0} | all-to-all | bytes 1146880 | tf_op jit(solution)/shard_map/all_to_all | solution.py:51
  42.3 1.7 reshape.135
  44.0 0.0 all-gather.6.cloned.1.call-update
  44.0 0.0 all-gather.4.cloned.1.call-start
  44.0 0.0 copy-done
  44.1 0.4 convolution_convert_fusion.1
  44.4 1.0 reshape.132
  45.4 23.4 %all_to_all.35 = bf16[8,16,2240]{2,1,0:T(8,128)(2,1)S(1)} all-to-all(bf16[8,16,2240]{2,1,0:T(8,128)(2,1)S(1)} %reshape.132), channel_id=1, replica_groups=mesh['pipe'=2,'group'=8,'member'=16] {'group'}, dimensions={0} | all-to-all | bytes 1146880 | tf_op jit(solution)/shard_map/all_to_all | solution.py:50
  68.8 1.7 reshape.133
  70.5 0.0 all-gather.4.cloned.1.call-update
  70.6 4.4 pad_maximum_fusion
  74.9 79.8 %all-gather.6.cloned.1.call-done = bf16[640,7168]{1,0:T(8,128)(2,1)} async-done(((bf16[40,7168]{1,0:T(8,128)(2,1)}), bf16[640,7168]{1,0:T(8,128)(2,1)}) %all-gather.6.cloned.1.call-update) | async-done | bytes 9175056 | tf_op jit(solution)/shard_map/all_gather | solution.py:53
  154.7 109.1 %all-gather.4.cloned.1.call-done = bf16[640,7168]{1,0:T(8,128)(2,1)} async-done(((bf16[40,7168]{1,0:T(8,128)(2,1)}), bf16[640,7168]{1,0:T(8,128)(2,1)}) %all-gather.4.cloned.1.call-update) | async-done | bytes 9175056 | tf_op jit(solution)/shard_map/all_gather | solution.py:52
  263.9 7.5 %all-to-all-start.2 = ((bf16[16,448,256]{2,1,0:T(8,128)(2,1)}), bf16[16,448,256]{2,1,0:T(8,128)(2,1)}, u32[]{:S(2)}, u32[]{:S(2)}) async-start(bf16[16,448,256]{2,1,0:T(8,128)(2,1)} %bitcast.51), calls=%async_computation.2 | async-start | bytes 7340032 | tf_op jit(solution)/shard_map/all_to_all | solution.py:56
  271.4 0.2 all-gather.8.cloned.1.call-start
  271.6 0.0 copy-start.3
  271.6 0.0 slice-start
  271.6 0.0 slice-start.1
  271.6 7.0 %fusion.10 = f32[640,128]{0,1:T(8,128)S(1)} fusion(bf16[640,7168]{1,0:T(8,128)(2,1)} %all-gather.4.cloned.1.call-done, bf16[1,7168,128]{2,1,0:T(8,128)(2,1)} %param.10), kind=kOutput, calls=%fused_computation.27 | convolution fusion | flops 1174405120 | bytes 11337728 | tf_op jit(solution)/shard_map/dot_general | solution.py:60
  278.7 0.0 copy-done.3
  278.7 0.0 slice-start.2
  278.7 0.0 copy-start.1
  278.7 6.7 %fusion.3 = f32[640,128]{0,1:T(8,128)S(1)} fusion(bf16[640,7168]{1,0:T(8,128)(2,1)} %all-gather.6.cloned.1.call-done, bf16[1,128,7168]{2,1,0:T(8,128)(2,1)S(1)} %copy-done.3), kind=kOutput, calls=%fused_computation.8 | convolution fusion | flops 1174405120 | bytes 11337728 | tf_op jit(solution)/shard_map/dot_general | solution.py:65
  285.4 0.0 slice-done
  285.4 0.0 slice-done.1
  285.4 0.0 slice-done.2
  285.5 0.0 copy-done.1
  285.5 3.6 multiply_convert_fusion.2
  289.1 0.8 maximum_bitcast_fusion
  289.8 59.9 %all-to-all-done.2 = bf16[16,448,256]{2,1,0:T(8,128)(2,1)} async-done(((bf16[16,448,256]{2,1,0:T(8,128)(2,1)}), bf16[16,448,256]{2,1,0:T(8,128)(2,1)}, u32[]{:S(2)}, u32[]{:S(2)}) %all-to-all-start.2) | async-done | bytes 3670048 | tf_op jit(solution)/shard_map/all_to_all | solution.py:56
  349.7 4.3 copy.36
  354.1 0.0 all-gather.8.cloned.1.call-update
  354.1 79.7 %all-gather.8.cloned.1.call-done = bf16[4096,640]{1,0:T(8,128)(2,1)} async-done(((bf16[256,640]{1,0:T(8,128)(2,1)}), bf16[4096,640]{1,0:T(8,128)(2,1)}) %all-gather.8.cloned.1.call-update) | async-done | bytes 5242896 | tf_op jit(solution)/shard_map/all_gather | solution.py:74
  433.8 6.6 %convolution_convert_fusion.2 = bf16[640,448]{0,1:T(8,128)(2,1)S(1)} fusion(bf16[448,4096]{1,0:T(8,128)(2,1)} %bitcast.56, bf16[4096,640]{1,0:T(8,128)(2,1)} %all-gather.8.cloned.1.call-done), kind=kOutput, calls=%fused_computation.12 | convolution fusion | flops 2349096960 | bytes 9486336 | tf_op jit(solution)/shard_map/dot_general | solution.py:75
  440.4 1.1 copy.32
  441.5 1.5 convert_element_type.50
  443.0 0.4 copy.33
  443.4 0.4 copy.34
  443.8 33.3 %all_to_all.36 = bf16[128,5,448]{2,1,0:T(8,128)(2,1)S(1)} all-to-all(bf16[128,5,448]{2,1,0:T(8,128)(2,1)S(1)} %copy.34), channel_id=1, replica_groups=mesh['pipe'=2,'group'=8,'member'=16] {'group','member'}, dimensions={0} | all-to-all | bytes 1146880 | tf_op jit(solution)/shard_map/all_to_all | solution.py:86
  477.1 0.2 copy.38
  477.4 0.8 reshape.137
  478.1 0.0 copy-start.2
  478.2 2.2 fusion
  480.4 11.8 %collective-permute-start = (bf16[128,7168]{1,0:T(8,128)(2,1)S(1)}, bf16[128,7168]{1,0:T(8,128)(2,1)S(1)}, u32[]{:S(2)}, u32[]{:S(2)}) collective-permute-start(bf16[128,7168]{1,0:T(8,128)(2,1)S(1)} %fusion), channel_id=1, source_target_pairs={{0,128},{128,0},{1,129},{129,1},{2,130},{130,2},{3,131},{131,3},{4... | collective-permute-start | bytes 5505032 | tf_op jit(solution)/shard_map/ppermute | solution.py:15
  492.2 0.0 copy-done.2
  492.2 6.5 %fusion.1 = bf16[1,128,7168]{2,1,0:T(8,128)(2,1)} fusion(bf16[640,7168]{1,0:T(8,128)(2,1)} %all-gather.6.cloned.1.call-done, f32[640,128]{0,1:T(8,128)S(1)} %fusion.10, f32[640,128]{0,1:T(8,128)S(1)} %copy-done.2), kind=kOutput, calls=%fused_computation.3 | convolution fusion | flops 1175814144 | bytes 11665408 | tf_op jit(solution)/shard_map/dot_general | solution.py:78
  498.6 0.0 collective-permute-done
  498.6 1.2 copy.40
  (6 shorter events, 0.1 us)
Async XLA Ops:
  7.2 36.9 %copy-start = (bf16[1,128,7168]{2,1,0:T(8,128)(2,1)S(1)}, bf16[1,128,7168]{2,1,0:T(8,128)(2,1)}, u32[]{:S(2)}) copy-start(bf16[1,128,7168]{2,1,0:T(8,128)(2,1)} %param.7) | copy-start | bytes 5505028
  7.2 147.6 %all-gather.6.cloned.1.call-start = ((), (), s32[]{:S(2)}) async-start(), calls=%async_computation.5 | async-start | bytes 9748480 | tf_op jit(solution)/shard_map/all_gather | solution.py:53
  44.0 219.9 %all-gather.4.cloned.1.call-start = ((), (), s32[]{:S(2)}) async-start(), calls=%async_computation.4 | async-start | bytes 9748480 | tf_op jit(solution)/shard_map/all_gather | solution.py:52
  263.9 85.9 %all-to-all-start.2 = ((bf16[16,448,256]{2,1,0:T(8,128)(2,1)}), bf16[16,448,256]{2,1,0:T(8,128)(2,1)}, u32[]{:S(2)}, u32[]{:S(2)}) async-start(bf16[16,448,256]{2,1,0:T(8,128)(2,1)} %bitcast.51), calls=%async_computation.2 | async-start | bytes 7340032 | tf_op jit(solution)/shard_map/all_to_all | solution.py:56
  271.4 162.4 %all-gather.8.cloned.1.call-start = ((), (), s32[]{:S(2)}) async-start(), calls=%async_computation.6 | async-start | bytes 5570560 | tf_op jit(solution)/shard_map/all_gather | solution.py:74
  271.6 7.1 %copy-start.3 = (bf16[1,128,7168]{2,1,0:T(8,128)(2,1)S(1)}, bf16[1,128,7168]{2,1,0:T(8,128)(2,1)}, u32[]{:S(2)}) copy-start(bf16[1,128,7168]{2,1,0:T(8,128)(2,1)} %param.11) | copy-start | bytes 5505028
  271.6 13.8 %slice-start = ((s8[9175040]{0:T(1024)(128)(4,1)}), s8[4194304]{0:T(1024)(128)(4,1)S(1)}, s32[]{:S(2)}) async-start(s8[9175040]{0:T(1024)(128)(4,1)} %bitcast.49), calls=%async_computation.7 | async-start | bytes 8388608
  271.6 13.8 %slice-start.1 = ((s8[9175040]{0:T(1024)(128)(4,1)}), s8[4194304]{0:T(1024)(128)(4,1)S(1)}, s32[]{:S(2)}) async-start(s8[9175040]{0:T(1024)(128)(4,1)} %bitcast.49), calls=%async_computation.8 | async-start | bytes 8388608
  278.7 6.7 %slice-start.2 = ((s8[9175040]{0:T(1024)(128)(4,1)}), s8[786432]{0:T(1024)(128)(4,1)S(1)}, s32[]{:S(2)}) async-start(s8[9175040]{0:T(1024)(128)(4,1)} %bitcast.49), calls=%async_computation.9 | async-start | bytes 1572864
  278.7 6.7 %copy-start.1 = (bf16[1,7168,128]{2,1,0:T(8,128)(2,1)S(1)}, bf16[1,7168,128]{2,1,0:T(8,128)(2,1)}, u32[]{:S(2)}) copy-start(bf16[1,7168,128]{2,1,0:T(8,128)(2,1)} %param.9) | copy-start | bytes 5505028
  478.1 14.0 %copy-start.2 = (f32[640,128]{0,1:T(8,128)S(1)}, f32[640,128]{0,1:T(8,128)}, u32[]{:S(2)}) copy-start(f32[640,128]{0,1:T(8,128)} %get-tuple-element.14) | copy-start | bytes 983044
  480.4 18.2 %collective-permute-start = (bf16[128,7168]{1,0:T(8,128)(2,1)S(1)}, bf16[128,7168]{1,0:T(8,128)(2,1)S(1)}, u32[]{:S(2)}, u32[]{:S(2)}) collective-permute-start(bf16[128,7168]{1,0:T(8,128)(2,1)S(1)} %fusion), channel_id=1, source_target_pairs={{0,128},{128,0},{1,129},{129,1},{2,130},{130,2},{3,131},{131,3},{4... | collective-permute-start | bytes 5505032 | tf_op jit(solution)/shard_map/ppermute | solution.py:15
Sparse Core Ops, SparseCore 0:
  44.1 110.5 all-gather.5
  157.1 106.7 all-gather.3
  354.2 79.5 all-gather.7

commit v12 on v11

--- a/solution.py
+++ b/solution.py
@@ -70,14 +70,14 @@
     )
     grad_up = (back_hidden * silu_gate).astype(jnp.bfloat16)
     both_grad = jnp.concatenate([grad_gate, grad_up], axis=1).T
-    both_slice, both_grad = lax.optimization_barrier((both_slice, both_grad))
+    down_part = lax.dot_general(
+        hidden, got_grad, rows_first, preferred_element_type=jnp.float32
+    ).astype(jnp.bfloat16)
+    both_slice, both_grad, down_part = lax.optimization_barrier((both_slice, both_grad, down_part))
     all_grad = lax.all_gather(both_grad, "member", axis=0, tiled=True)
     slice_value = lax.dot_general(
         all_grad, both_slice, (((0,), (1,)), ((), ())), preferred_element_type=jnp.float32
     )
-    down_part = lax.dot_general(
-        hidden, got_grad, rows_first, preferred_element_type=jnp.float32
-    ).astype(jnp.bfloat16)
     slice_width = slice_value.shape[1]
     slice_value = slice_value.reshape(members, groups, slot_count, slice_width)
     slice_value = jnp.transpose(slice_value, (1, 0, 2, 3)).reshape(

time: 509 us -> 504 us (level)
    all_to_all x1, waiting for transfers between devices: 59.9 us -> 54.1 us  [body(): both_slice = lax.all_to_all(both_cols, 'member', 0, 1, tiled=True)]
  transfers between devices with their start and end apart: 5 -> 5, of which waited for: 4 -> 5; matrix products, arithmetic and copies ran while one was open for 6% -> 6% of each run, Pallas kernels for 0% -> 0%
where the time goes in v12:
time: 504 us; the launch traced here: 502 us
  waiting for transfers between devices  326 us (65%)
  blocking collectives  86.8 us (17%)
  matrix products  34.2 us (7%)
  starting transfers between devices  19.6 us (4%)
  between operations  14 us (3%)
  local copies, waits for them, and re-layouts  13.9 us (3%)
  other arithmetic  6.96 us (1%)
    all_gather x1, waiting for transfers between devices, body(): got_in = lax.all_gather(near_in, 'member', axis=0, tiled=True)  109 us
    all_gather x1, waiting for transfers between devices, body(): got_grad = lax.all_gather(near_grad, 'member', axis=0, tiled=True)  79.8 us
    all_gather x1, waiting for transfers between devices, body(): all_grad = lax.all_gather(both_grad, 'member', axis=0, tiled=True)  79.7 us
    all_to_all x1, waiting for transfers between devices, body(): both_slice = lax.all_to_all(both_cols, 'member', 0, 1, tiled=True)  54.1 us
    all_to_all x1, blocking collectives, body(): lax.all_to_all(slice_value.astype(jnp.bfloat16), ('group', 'member'), 0,...  33.4 us
    all_to_all x1, blocking collectives, body(): lax.all_to_all(send_grad, 'group', 0, 0, tiled=True)  30 us
    all_to_all x1, blocking collectives, body(): lax.all_to_all(send_in, 'group', 0, 0, tiled=True)  23.4 us
    ppermute x1, starting transfers between devices, from_behind(): return lax.ppermute(value, axis, pairs)  11.8 us
  transfers between devices with their start and end apart: 5, of which 5 were waited for; matrix products, arithmetic and copies ran while one was open for 6% of the time, Pallas kernels for 0%

profile of v12, /device:TPU:33, one launch (start us, length us, event | category | flops | bytes accessed | tf_op | source)
XLA Modules:
  0.0 501.6 jit_solution(18375566876619419569)
XLA Ops:
  7.2 0.0 copy-start
  7.2 0.0 all-gather.6.cloned.1.call-start
  7.2 0.8 convert_reduce_fusion
  8.0 0.1 copy.28
  8.2 0.2 reduce_window_sum.11
  8.5 0.7 select_reduce_fusion.1
  9.2 0.1 select_reduce_fusion
  9.3 0.1 mul.41
  9.3 1.9 fusion.1
  11.2 1.0 reshape.134
  12.2 30.0 %all_to_all.34 = bf16[8,16,2240]{2,1,0:T(8,128)(2,1)S(1)} all-to-all(bf16[8,16,2240]{2,1,0:T(8,128)(2,1)S(1)} %reshape.134), channel_id=1, replica_groups=mesh['pipe'=2,'group'=8,'member'=16] {'group'}, dimensions={0} | all-to-all | bytes 1146880 | tf_op jit(solution)/shard_map/all_to_all | solution.py:51
  42.3 1.7 reshape.135
  44.0 0.0 all-gather.6.cloned.1.call-update
  44.0 0.0 all-gather.4.cloned.1.call-start
  44.0 0.0 copy-done
  44.1 0.4 convolution_convert_fusion.1
  44.4 1.0 reshape.132
  45.4 23.4 %all_to_all.35 = bf16[8,16,2240]{2,1,0:T(8,128)(2,1)S(1)} all-to-all(bf16[8,16,2240]{2,1,0:T(8,128)(2,1)S(1)} %reshape.132), channel_id=1, replica_groups=mesh['pipe'=2,'group'=8,'member'=16] {'group'}, dimensions={0} | all-to-all | bytes 1146880 | tf_op jit(solution)/shard_map/all_to_all | solution.py:50
  68.8 1.7 reshape.133
  70.5 0.0 all-gather.4.cloned.1.call-update
  70.6 4.4 pad_maximum_fusion
  74.9 79.8 %all-gather.6.cloned.1.call-done = bf16[640,7168]{1,0:T(8,128)(2,1)} async-done(((bf16[40,7168]{1,0:T(8,128)(2,1)}), bf16[640,7168]{1,0:T(8,128)(2,1)}) %all-gather.6.cloned.1.call-update) | async-done | bytes 9175056 | tf_op jit(solution)/shard_map/all_gather | solution.py:53
  154.7 109.1 %all-gather.4.cloned.1.call-done = bf16[640,7168]{1,0:T(8,128)(2,1)} async-done(((bf16[40,7168]{1,0:T(8,128)(2,1)}), bf16[640,7168]{1,0:T(8,128)(2,1)}) %all-gather.4.cloned.1.call-update) | async-done | bytes 9175056 | tf_op jit(solution)/shard_map/all_gather | solution.py:52
  263.9 7.5 %all-to-all-start.2 = ((bf16[16,448,256]{2,1,0:T(8,128)(2,1)}), bf16[16,448,256]{2,1,0:T(8,128)(2,1)}, u32[]{:S(2)}, u32[]{:S(2)}) async-start(bf16[16,448,256]{2,1,0:T(8,128)(2,1)} %bitcast.50), calls=%async_computation.2 | async-start | bytes 7340032 | tf_op jit(solution)/shard_map/all_to_all | solution.py:56
  271.4 0.2 all-gather.8.cloned.1.call-start
  271.6 0.0 copy-start.2
  271.6 0.0 slice-start
  271.6 0.0 slice-start.1
  271.6 7.0 %fusion.9 = f32[640,128]{0,1:T(8,128)S(1)} fusion(bf16[640,7168]{1,0:T(8,128)(2,1)} %all-gather.4.cloned.1.call-done, bf16[1,7168,128]{2,1,0:T(8,128)(2,1)} %param.10), kind=kOutput, calls=%fused_computation.26 | convolution fusion | flops 1174405120 | bytes 11337728 | tf_op jit(solution)/shard_map/dot_general | solution.py:60
  278.7 0.0 copy-done.2
  278.7 0.0 slice-start.2
  278.7 0.0 copy-start.1
  278.7 6.7 %fusion.2 = f32[640,128]{0,1:T(8,128)S(1)} fusion(bf16[640,7168]{1,0:T(8,128)(2,1)} %all-gather.6.cloned.1.call-done, bf16[1,128,7168]{2,1,0:T(8,128)(2,1)S(1)} %copy-done.2), kind=kOutput, calls=%fused_computation.7 | convolution fusion | flops 1174405120 | bytes 11337728 | tf_op jit(solution)/shard_map/dot_general | solution.py:65
  285.4 0.0 slice-done
  285.4 0.0 slice-done.1
  285.5 0.0 slice-done.2
  285.5 0.0 copy-done.1
  285.5 3.0 multiply_convert_fusion.2
  288.4 0.8 maximum_bitcast_fusion
  289.2 6.5 %convolution_convert_fusion = bf16[128,7168]{1,0:T(8,128)(2,1)} fusion(bf16[640,7168]{1,0:T(8,128)(2,1)} %all-gather.6.cloned.1.call-done, f32[640,128]{0,1:T(8,128)S(1)} %fusion.9, f32[640,128]{0,1:T(8,128)S(1)} %get-tuple-element.16), kind=kOutput, calls=%fused_computation.2 | convolution fusion | flops 1175814144 | bytes 11665408 | tf_op jit(solution)/shard_map/dot_general | solution.py:73
  295.7 54.1 %all-to-all-done.2 = bf16[16,448,256]{2,1,0:T(8,128)(2,1)} async-done(((bf16[16,448,256]{2,1,0:T(8,128)(2,1)}), bf16[16,448,256]{2,1,0:T(8,128)(2,1)}, u32[]{:S(2)}, u32[]{:S(2)}) %all-to-all-start.2) | async-done | bytes 3670048 | tf_op jit(solution)/shard_map/all_to_all | solution.py:56
  349.7 4.4 copy.36
  354.1 0.0 all-gather.8.cloned.1.call-update
  354.2 79.7 %all-gather.8.cloned.1.call-done = bf16[4096,640]{1,0:T(8,128)(2,1)} async-done(((bf16[256,640]{1,0:T(8,128)(2,1)}), bf16[4096,640]{1,0:T(8,128)(2,1)}) %all-gather.8.cloned.1.call-update) | async-done | bytes 5242896 | tf_op jit(solution)/shard_map/all_gather | solution.py:77
  433.8 6.6 %convolution_convert_fusion.2 = bf16[640,448]{0,1:T(8,128)(2,1)S(1)} fusion(bf16[448,4096]{1,0:T(8,128)(2,1)} %bitcast.55, bf16[4096,640]{1,0:T(8,128)(2,1)} %all-gather.8.cloned.1.call-done), kind=kOutput, calls=%fused_computation.11 | convolution fusion | flops 2349096960 | bytes 9486336 | tf_op jit(solution)/shard_map/dot_general | solution.py:78
  440.4 0.2 copy.32
  440.7 0.3 convert_element_type.52
  441.0 0.7 copy.33
  441.7 0.4 copy.34
  442.1 33.4 %all_to_all.36 = bf16[128,5,448]{2,1,0:T(8,128)(2,1)S(1)} all-to-all(bf16[128,5,448]{2,1,0:T(8,128)(2,1)S(1)} %copy.34), channel_id=1, replica_groups=mesh['pipe'=2,'group'=8,'member'=16] {'group','member'}, dimensions={0} | all-to-all | bytes 1146880 | tf_op jit(solution)/shard_map/all_to_all | solution.py:86
  475.4 0.2 copy.38
  475.7 0.8 reshape.137
  476.4 2.2 fusion
  478.6 11.8 %collective-permute-start = (bf16[128,7168]{1,0:T(8,128)(2,1)S(1)}, bf16[128,7168]{1,0:T(8,128)(2,1)S(1)}, u32[]{:S(2)}, u32[]{:S(2)}) collective-permute-start(bf16[128,7168]{1,0:T(8,128)(2,1)S(1)} %fusion), channel_id=1, source_target_pairs={{0,128},{128,0},{1,129},{129,1},{2,130},{130,2},{3,131},{131,3},{4... | collective-permute-start | bytes 5505032 | tf_op jit(solution)/shard_map/ppermute | solution.py:15
  490.4 3.4 collective-permute-done
  493.8 1.2 copy.40
  (6 shorter events, 0.1 us)
Async XLA Ops:
  7.2 36.9 %copy-start = (bf16[1,128,7168]{2,1,0:T(8,128)(2,1)S(1)}, bf16[1,128,7168]{2,1,0:T(8,128)(2,1)}, u32[]{:S(2)}) copy-start(bf16[1,128,7168]{2,1,0:T(8,128)(2,1)} %param.7) | copy-start | bytes 5505028
  7.2 147.6 %all-gather.6.cloned.1.call-start = ((), (), s32[]{:S(2)}) async-start(), calls=%async_computation.5 | async-start | bytes 9748480 | tf_op jit(solution)/shard_map/all_gather | solution.py:53
  44.0 219.9 %all-gather.4.cloned.1.call-start = ((), (), s32[]{:S(2)}) async-start(), calls=%async_computation.4 | async-start | bytes 9748480 | tf_op jit(solution)/shard_map/all_gather | solution.py:52
  263.9 85.9 %all-to-all-start.2 = ((bf16[16,448,256]{2,1,0:T(8,128)(2,1)}), bf16[16,448,256]{2,1,0:T(8,128)(2,1)}, u32[]{:S(2)}, u32[]{:S(2)}) async-start(bf16[16,448,256]{2,1,0:T(8,128)(2,1)} %bitcast.50), calls=%async_computation.2 | async-start | bytes 7340032 | tf_op jit(solution)/shard_map/all_to_all | solution.py:56
  271.4 162.5 %all-gather.8.cloned.1.call-start = ((), (), s32[]{:S(2)}) async-start(), calls=%async_computation.6 | async-start | bytes 5570560 | tf_op jit(solution)/shard_map/all_gather | solution.py:77
  271.6 7.1 %copy-start.2 = (bf16[1,128,7168]{2,1,0:T(8,128)(2,1)S(1)}, bf16[1,128,7168]{2,1,0:T(8,128)(2,1)}, u32[]{:S(2)}) copy-start(bf16[1,128,7168]{2,1,0:T(8,128)(2,1)} %param.11) | copy-start | bytes 5505028
  271.6 13.8 %slice-start = ((s8[9175040]{0:T(1024)(128)(4,1)}), s8[4194304]{0:T(1024)(128)(4,1)S(1)}, s32[]{:S(2)}) async-start(s8[9175040]{0:T(1024)(128)(4,1)} %bitcast.48), calls=%async_computation.7 | async-start | bytes 8388608
  271.6 13.8 %slice-start.1 = ((s8[9175040]{0:T(1024)(128)(4,1)}), s8[4194304]{0:T(1024)(128)(4,1)S(1)}, s32[]{:S(2)}) async-start(s8[9175040]{0:T(1024)(128)(4,1)} %bitcast.48), calls=%async_computation.8 | async-start | bytes 8388608
  278.7 6.7 %slice-start.2 = ((s8[9175040]{0:T(1024)(128)(4,1)}), s8[786432]{0:T(1024)(128)(4,1)S(1)}, s32[]{:S(2)}) async-start(s8[9175040]{0:T(1024)(128)(4,1)} %bitcast.48), calls=%async_computation.9 | async-start | bytes 1572864
  278.7 6.7 %copy-start.1 = (bf16[1,7168,128]{2,1,0:T(8,128)(2,1)S(1)}, bf16[1,7168,128]{2,1,0:T(8,128)(2,1)}, u32[]{:S(2)}) copy-start(bf16[1,7168,128]{2,1,0:T(8,128)(2,1)} %param.9) | copy-start | bytes 5505028
  478.6 15.2 %collective-permute-start = (bf16[128,7168]{1,0:T(8,128)(2,1)S(1)}, bf16[128,7168]{1,0:T(8,128)(2,1)S(1)}, u32[]{:S(2)}, u32[]{:S(2)}) collective-permute-start(bf16[128,7168]{1,0:T(8,128)(2,1)S(1)} %fusion), channel_id=1, source_target_pairs={{0,128},{128,0},{1,129},{129,1},{2,130},{130,2},{3,131},{131,3},{4... | collective-permute-start | bytes 5505032 | tf_op jit(solution)/shard_map/ppermute | solution.py:15
Sparse Core Ops, SparseCore 0:
  44.1 110.5 all-gather.5
  157.1 106.7 all-gather.3
  354.3 79.5 all-gather.7

commit v13 on v12

--- a/solution.py
+++ b/solution.py
@@ -53,7 +53,9 @@
     got_grad = lax.all_gather(near_grad, "member", axis=0, tiled=True)
     both_cols = jnp.concatenate([gate_cols, up_cols], axis=1)
     both_cols, got_in, got_grad = lax.optimization_barrier((both_cols, got_in, got_grad))
-    both_slice = lax.all_to_all(both_cols, "member", 0, 1, tiled=True)
+    both_slice = lax.all_to_all(
+        both_cols.reshape(SHARDS, -1, both_cols.shape[1]), "member", 0, 0, tiled=True
+    )
     members = lax.axis_size("member")
     groups = live_count
     gate_pre = jnp.dot(got_in, gate_cols, preferred_element_type=jnp.float32)
@@ -74,9 +76,9 @@
         hidden, got_grad, rows_first, preferred_element_type=jnp.float32
     ).astype(jnp.bfloat16)
     both_slice, both_grad, down_part = lax.optimization_barrier((both_slice, both_grad, down_part))
-    all_grad = lax.all_gather(both_grad, "member", axis=0, tiled=True)
+    all_grad = lax.all_gather(both_grad, "member", axis=0, tiled=False)
     slice_value = lax.dot_general(
-        all_grad, both_slice, (((0,), (1,)), ((), ())), preferred_element_type=jnp.float32
+        all_grad, both_slice, (((0, 1), (0, 2)), ((), ())), preferred_element_type=jnp.float32
     )
     slice_width = slice_value.shape[1]
     slice_value = slice_value.reshape(members, groups, slot_count, slice_width)

time: 504 us -> 500 us (level)
  no operation moved by 1% of the time
where the time goes in v13:
time: 500 us; the launch traced here: 497 us
  waiting for transfers between devices  326 us (65%)
  blocking collectives  87 us (17%)
  matrix products  34.2 us (7%)
  starting transfers between devices  19.6 us (4%)
  between operations  14 us (3%)
  local copies, waits for them, and re-layouts  9.25 us (2%)
  other arithmetic  6.96 us (1%)
    all_gather x1, waiting for transfers between devices, body(): got_in = lax.all_gather(near_in, 'member', axis=0, tiled=True)  109 us
    all_gather x1, waiting for transfers between devices, body(): got_grad = lax.all_gather(near_grad, 'member', axis=0, tiled=True)  79.8 us
    all_gather x1, waiting for transfers between devices, body(): all_grad = lax.all_gather(both_grad, 'member', axis=0, tiled=False)  79.7 us
    all_to_all x1, waiting for transfers between devices, body(): lax.all_to_all(both_cols.reshape(SHARDS, -1, both_cols.shape[1]), 'member...  54.1 us
    all_to_all x1, blocking collectives, body(): lax.all_to_all(slice_value.astype(jnp.bfloat16), ('group', 'member'), 0,...  33.6 us
    all_to_all x1, blocking collectives, body(): lax.all_to_all(send_grad, 'group', 0, 0, tiled=True)  30 us
    all_to_all x1, blocking collectives, body(): lax.all_to_all(send_in, 'group', 0, 0, tiled=True)  23.4 us
    ppermute x1, starting transfers between devices, from_behind(): return lax.ppermute(value, axis, pairs)  11.8 us
  transfers between devices with their start and end apart: 5, of which 5 were waited for; matrix products, arithmetic and copies ran while one was open for 6% of the time, Pallas kernels for 0%

profile of v13, /device:TPU:33, one launch (start us, length us, event | category | flops | bytes accessed | tf_op | source)
XLA Modules:
  0.0 497.2 jit_solution(16557067532943355824)
XLA Ops:
  7.2 0.0 copy-start
  7.2 0.0 all-gather.7.cloned.1.call-start
  7.2 0.8 convert_reduce_fusion
  8.0 0.1 copy.26
  8.2 0.2 reduce_window_sum.11
  8.5 0.7 select_reduce_fusion.1
  9.2 0.1 select_reduce_fusion
  9.3 0.1 mul.41
  9.3 1.9 fusion.1
  11.2 1.0 reshape.134
  12.2 30.0 %all_to_all.20 = bf16[8,16,2240]{2,1,0:T(8,128)(2,1)S(1)} all-to-all(bf16[8,16,2240]{2,1,0:T(8,128)(2,1)S(1)} %reshape.134), channel_id=1, replica_groups=mesh['pipe'=2,'group'=8,'member'=16] {'group'}, dimensions={0} | all-to-all | bytes 1146880 | tf_op jit(solution)/shard_map/all_to_all | solution.py:51
  42.3 1.7 reshape.135
  44.0 0.0 all-gather.7.cloned.1.call-update
  44.0 0.0 all-gather.5.cloned.1.call-start
  44.0 0.0 copy-done
  44.1 0.4 convolution_convert_fusion.1
  44.4 1.0 reshape.132
  45.4 23.4 %all_to_all.21 = bf16[8,16,2240]{2,1,0:T(8,128)(2,1)S(1)} all-to-all(bf16[8,16,2240]{2,1,0:T(8,128)(2,1)S(1)} %reshape.132), channel_id=1, replica_groups=mesh['pipe'=2,'group'=8,'member'=16] {'group'}, dimensions={0} | all-to-all | bytes 1146880 | tf_op jit(solution)/shard_map/all_to_all | solution.py:50
  68.8 1.7 reshape.133
  70.5 0.0 all-gather.5.cloned.1.call-update
  70.6 4.4 pad_maximum_fusion
  74.9 79.8 %all-gather.7.cloned.1.call-done = bf16[640,7168]{1,0:T(8,128)(2,1)} async-done(((bf16[40,7168]{1,0:T(8,128)(2,1)}), bf16[640,7168]{1,0:T(8,128)(2,1)}) %all-gather.7.cloned.1.call-update) | async-done | bytes 9175056 | tf_op jit(solution)/shard_map/all_gather | solution.py:53
  154.7 109.1 %all-gather.5.cloned.1.call-done = bf16[640,7168]{1,0:T(8,128)(2,1)} async-done(((bf16[40,7168]{1,0:T(8,128)(2,1)}), bf16[640,7168]{1,0:T(8,128)(2,1)}) %all-gather.5.cloned.1.call-update) | async-done | bytes 9175056 | tf_op jit(solution)/shard_map/all_gather | solution.py:52
  263.9 7.5 %all-to-all-start.2 = ((bf16[16,448,256]{2,1,0:T(8,128)(2,1)}), bf16[16,448,256]{2,1,0:T(8,128)(2,1)}, u32[]{:S(2)}, u32[]{:S(2)}) async-start(bf16[16,448,256]{2,1,0:T(8,128)(2,1)} %bitcast.52), calls=%async_computation.2 | async-start | bytes 7340032 | tf_op jit(solution)/shard_map/all_to_all | solution.py:56
  271.4 0.2 all-gather.9.cloned.1.call-start
  271.6 0.0 copy-start.2
  271.6 0.0 slice-start
  271.6 0.0 slice-start.1
  271.6 7.0 %fusion.10 = f32[640,128]{0,1:T(8,128)S(1)} fusion(bf16[640,7168]{1,0:T(8,128)(2,1)} %all-gather.5.cloned.1.call-done, bf16[1,7168,128]{2,1,0:T(8,128)(2,1)} %param.10), kind=kOutput, calls=%fused_computation.27 | convolution fusion | flops 1174405120 | bytes 11337728 | tf_op jit(solution)/shard_map/dot_general | solution.py:62
  278.7 0.0 copy-done.2
  278.7 0.0 slice-start.2
  278.7 0.0 copy-start.1
  278.7 6.7 %fusion.2 = f32[640,128]{0,1:T(8,128)S(1)} fusion(bf16[640,7168]{1,0:T(8,128)(2,1)} %all-gather.7.cloned.1.call-done, bf16[1,128,7168]{2,1,0:T(8,128)(2,1)S(1)} %copy-done.2), kind=kOutput, calls=%fused_computation.7 | convolution fusion | flops 1174405120 | bytes 11337728 | tf_op jit(solution)/shard_map/dot_general | solution.py:67
  285.4 0.0 slice-done
  285.4 0.0 slice-done.1
  285.5 0.0 slice-done.2
  285.5 0.0 copy-done.1
  285.5 3.0 multiply_convert_fusion.2
  288.4 0.8 maximum_bitcast_fusion
  289.2 6.5 %convolution_convert_fusion = bf16[128,7168]{1,0:T(8,128)(2,1)} fusion(bf16[640,7168]{1,0:T(8,128)(2,1)} %all-gather.7.cloned.1.call-done, f32[640,128]{0,1:T(8,128)S(1)} %fusion.10, f32[640,128]{0,1:T(8,128)S(1)} %get-tuple-element.16), kind=kOutput, calls=%fused_computation.2 | convolution fusion | flops 1175814144 | bytes 11665408 | tf_op jit(solution)/shard_map/dot_general | solution.py:75
  295.7 54.1 %all-to-all-done.2 = bf16[16,448,256]{2,1,0:T(8,128)(2,1)} async-done(((bf16[16,448,256]{2,1,0:T(8,128)(2,1)}), bf16[16,448,256]{2,1,0:T(8,128)(2,1)}, u32[]{:S(2)}, u32[]{:S(2)}) %all-to-all-start.2) | async-done | bytes 3670048 | tf_op jit(solution)/shard_map/all_to_all | solution.py:56
  349.7 0.0 all-gather.9.cloned.1.call-update
  349.8 79.7 %all-gather.9.cloned.1.call-done = bf16[4096,640]{1,0:T(8,128)(2,1)} async-done(((bf16[256,640]{1,0:T(8,128)(2,1)}), bf16[4096,640]{1,0:T(8,128)(2,1)}) %all-gather.9.cloned.1.call-update) | async-done | bytes 5242896 | tf_op jit(solution)/shard_map/all_gather | solution.py:79
  429.4 6.6 %fusion.6 = bf16[640,448]{0,1:T(8,128)(2,1)S(1)} fusion(bf16[16,448,256]{2,1,0:T(8,128)(2,1)} %all-to-all-done.2, bf16[16,256,640]{2,1,0:T(8,128)(2,1)} %bitcast.64), kind=kOutput, calls=%fused_computation.12 | convolution fusion | flops 2349096960 | bytes 9486336 | tf_op jit(solution)/shard_map/dot_general | solution.py:80
  436.0 0.2 copy.29
  436.3 0.3 convert_element_type.52
  436.6 0.4 copy.30
  437.1 0.4 copy.31
  437.4 33.6 %all_to_all.22 = bf16[128,5,448]{2,1,0:T(8,128)(2,1)S(1)} all-to-all(bf16[128,5,448]{2,1,0:T(8,128)(2,1)S(1)} %copy.31), channel_id=1, replica_groups=mesh['pipe'=2,'group'=8,'member'=16] {'group','member'}, dimensions={0} | all-to-all | bytes 1146880 | tf_op jit(solution)/shard_map/all_to_all | solution.py:88
  471.0 0.2 copy.34
  471.3 0.8 reshape.138
  472.0 2.2 fusion
  474.2 11.8 %collective-permute-start = (bf16[128,7168]{1,0:T(8,128)(2,1)S(1)}, bf16[128,7168]{1,0:T(8,128)(2,1)S(1)}, u32[]{:S(2)}, u32[]{:S(2)}) collective-permute-start(bf16[128,7168]{1,0:T(8,128)(2,1)S(1)} %fusion), channel_id=1, source_target_pairs={{0,128},{128,0},{1,129},{129,1},{2,130},{130,2},{3,131},{131,3},{4... | collective-permute-start | bytes 5505032 | tf_op jit(solution)/shard_map/ppermute | solution.py:15
  486.0 3.4 collective-permute-done
  489.4 1.2 copy.36
  (6 shorter events, 0.1 us)
Async XLA Ops:
  7.2 36.9 %copy-start = (bf16[1,128,7168]{2,1,0:T(8,128)(2,1)S(1)}, bf16[1,128,7168]{2,1,0:T(8,128)(2,1)}, u32[]{:S(2)}) copy-start(bf16[1,128,7168]{2,1,0:T(8,128)(2,1)} %param.7) | copy-start | bytes 5505028
  7.2 147.6 %all-gather.7.cloned.1.call-start = ((), (), s32[]{:S(2)}) async-start(), calls=%async_computation.5 | async-start | bytes 9748480 | tf_op jit(solution)/shard_map/all_gather | solution.py:53
  44.0 219.9 %all-gather.5.cloned.1.call-start = ((), (), s32[]{:S(2)}) async-start(), calls=%async_computation.4 | async-start | bytes 9748480 | tf_op jit(solution)/shard_map/all_gather | solution.py:52
  263.9 85.9 %all-to-all-start.2 = ((bf16[16,448,256]{2,1,0:T(8,128)(2,1)}), bf16[16,448,256]{2,1,0:T(8,128)(2,1)}, u32[]{:S(2)}, u32[]{:S(2)}) async-start(bf16[16,448,256]{2,1,0:T(8,128)(2,1)} %bitcast.52), calls=%async_computation.2 | async-start | bytes 7340032 | tf_op jit(solution)/shard_map/all_to_all | solution.py:56
  271.4 158.1 %all-gather.9.cloned.1.call-start = ((), (), s32[]{:S(2)}) async-start(), calls=%async_computation.6 | async-start | bytes 5570560 | tf_op jit(solution)/shard_map/all_gather | solution.py:79
  271.6 7.1 %copy-start.2 = (bf16[1,128,7168]{2,1,0:T(8,128)(2,1)S(1)}, bf16[1,128,7168]{2,1,0:T(8,128)(2,1)}, u32[]{:S(2)}) copy-start(bf16[1,128,7168]{2,1,0:T(8,128)(2,1)} %param.11) | copy-start | bytes 5505028
  271.6 13.8 %slice-start = ((s8[9175040]{0:T(1024)(128)(4,1)}), s8[4194304]{0:T(1024)(128)(4,1)S(1)}, s32[]{:S(2)}) async-start(s8[9175040]{0:T(1024)(128)(4,1)} %bitcast.50), calls=%async_computation.7 | async-start | bytes 8388608
  271.6 13.8 %slice-start.1 = ((s8[9175040]{0:T(1024)(128)(4,1)}), s8[4194304]{0:T(1024)(128)(4,1)S(1)}, s32[]{:S(2)}) async-start(s8[9175040]{0:T(1024)(128)(4,1)} %bitcast.50), calls=%async_computation.8 | async-start | bytes 8388608
  278.7 6.7 %slice-start.2 = ((s8[9175040]{0:T(1024)(128)(4,1)}), s8[786432]{0:T(1024)(128)(4,1)S(1)}, s32[]{:S(2)}) async-start(s8[9175040]{0:T(1024)(128)(4,1)} %bitcast.50), calls=%async_computation.9 | async-start | bytes 1572864
  278.7 6.7 %copy-start.1 = (bf16[1,7168,128]{2,1,0:T(8,128)(2,1)S(1)}, bf16[1,7168,128]{2,1,0:T(8,128)(2,1)}, u32[]{:S(2)}) copy-start(bf16[1,7168,128]{2,1,0:T(8,128)(2,1)} %param.9) | copy-start | bytes 5505028
  474.2 15.2 %collective-permute-start = (bf16[128,7168]{1,0:T(8,128)(2,1)S(1)}, bf16[128,7168]{1,0:T(8,128)(2,1)S(1)}, u32[]{:S(2)}, u32[]{:S(2)}) collective-permute-start(bf16[128,7168]{1,0:T(8,128)(2,1)S(1)} %fusion), channel_id=1, source_target_pairs={{0,128},{128,0},{1,129},{129,1},{2,130},{130,2},{3,131},{131,3},{4... | collective-permute-start | bytes 5505032 | tf_op jit(solution)/shard_map/ppermute | solution.py:15
Sparse Core Ops, SparseCore 0:
  44.1 110.5 all-gather.6
  157.1 106.7 all-gather.4
  349.9 79.5 all-gather.8

commit v14 on v13

--- a/solution.py
+++ b/solution.py
@@ -88,15 +88,11 @@
     back = lax.all_to_all(slice_value.astype(jnp.bfloat16), ("group", "member"), 0, 0, tiled=True)
     back = back.reshape(groups, members, slot_count, slice_width)
     returned = jnp.transpose(back, (0, 2, 1, 3)).reshape(groups * slot_count, model_width)
-    returned = returned.astype(jnp.float32)
-    branch = jnp.dot(
-        pick_mat.astype(jnp.float32),
-        returned,
-        preferred_element_type=jnp.float32,
-        precision=lax.Precision.HIGHEST,
-    )
-    input_grad = (grads.astype(jnp.float32) + branch).astype(jnp.bfloat16)
-    handed = from_behind(input_grad, "pipe", -1)
+    other_grads = from_behind(grads, "pipe", -1)
+    other_pick = from_behind(pick_mat, "pipe", -1)
+    other_returned = from_behind(returned, "pipe", -1)
+    branch = jnp.dot(other_pick, other_returned, preferred_element_type=jnp.float32)
+    handed = (other_grads.astype(jnp.float32) + branch).astype(jnp.bfloat16)
     return (handed[None], down_part[None])
 
 

time: 500 us -> 498 us (level)
    ppermute x1 -> x3, starting transfers between devices: 11.8 us -> 14.2 us  [from_behind(): return lax.ppermute(value, axis, pairs)]
  transfers between devices with their start and end apart: 5 -> 7, of which waited for: 5 -> 5; matrix products, arithmetic and copies ran while one was open for 6% -> 8% of each run, Pallas kernels for 0% -> 0%
where the time goes in v14:
time: 498 us; the launch traced here: 495 us
  waiting for transfers between devices  322 us (65%)
  blocking collectives  86.8 us (17%)
  matrix products  35.4 us (7%)
  starting transfers between devices  22 us (4%)
  between operations  14 us (3%)
  local copies, waits for them, and re-layouts  8.14 us (2%)
  other arithmetic  7.03 us (1%)
    all_gather x1, waiting for transfers between devices, body(): got_in = lax.all_gather(near_in, 'member', axis=0, tiled=True)  109 us
    all_gather x1, waiting for transfers between devices, body(): got_grad = lax.all_gather(near_grad, 'member', axis=0, tiled=True)  79.8 us
    all_gather x1, waiting for transfers between devices, body(): all_grad = lax.all_gather(both_grad, 'member', axis=0, tiled=False)  77.3 us
    all_to_all x1, waiting for transfers between devices, body(): lax.all_to_all(both_cols.reshape(SHARDS, -1, both_cols.shape[1]), 'member...  54.1 us
    all_to_all x1, blocking collectives, body(): lax.all_to_all(slice_value.astype(jnp.bfloat16), ('group', 'member'), 0,...  33.4 us
    all_to_all x1, blocking collectives, body(): lax.all_to_all(send_grad, 'group', 0, 0, tiled=True)  30 us
    all_to_all x1, blocking collectives, body(): lax.all_to_all(send_in, 'group', 0, 0, tiled=True)  23.4 us
    ppermute x3, starting transfers between devices, from_behind(): return lax.ppermute(value, axis, pairs)  14.2 us
  transfers between devices with their start and end apart: 7, of which 5 were waited for; matrix products, arithmetic and copies ran while one was open for 8% of the time, Pallas kernels for 0%

profile of v14, /device:TPU:33, one launch (start us, length us, event | category | flops | bytes accessed | tf_op | source)
XLA Modules:
  0.0 495.1 jit_solution(12213174864542856389)
XLA Ops:
  7.2 0.0 copy-start
  7.2 0.0 all-gather.7.cloned.1.call-start
  7.2 0.8 convert_reduce_fusion
  8.0 0.1 copy.26
  8.2 0.2 reduce_window_sum.11
  8.5 0.7 select_reduce_fusion.1
  9.2 0.1 select_reduce_fusion
  9.3 0.1 mul.41
  9.3 1.9 fusion
  11.2 1.0 reshape.113
  12.2 30.0 %all_to_all.20 = bf16[8,16,2240]{2,1,0:T(8,128)(2,1)S(1)} all-to-all(bf16[8,16,2240]{2,1,0:T(8,128)(2,1)S(1)} %reshape.113), channel_id=1, replica_groups=mesh['pipe'=2,'group'=8,'member'=16] {'group'}, dimensions={0} | all-to-all | bytes 1146880 | tf_op jit(solution)/shard_map/all_to_all | solution.py:51
  42.3 1.7 reshape.114
  44.0 0.0 all-gather.7.cloned.1.call-update
  44.0 0.0 all-gather.5.cloned.1.call-start
  44.0 0.0 copy-done
  44.1 0.4 convolution_convert_fusion.1
  44.4 1.0 reshape.111
  45.4 23.4 %all_to_all.21 = bf16[8,16,2240]{2,1,0:T(8,128)(2,1)S(1)} all-to-all(bf16[8,16,2240]{2,1,0:T(8,128)(2,1)S(1)} %reshape.111), channel_id=1, replica_groups=mesh['pipe'=2,'group'=8,'member'=16] {'group'}, dimensions={0} | all-to-all | bytes 1146880 | tf_op jit(solution)/shard_map/all_to_all | solution.py:50
  68.8 1.7 reshape.112
  70.5 0.0 all-gather.5.cloned.1.call-update
  70.6 4.3 pad_maximum_fusion
  74.9 79.8 %all-gather.7.cloned.1.call-done = bf16[640,7168]{1,0:T(8,128)(2,1)} async-done(((bf16[40,7168]{1,0:T(8,128)(2,1)}), bf16[640,7168]{1,0:T(8,128)(2,1)}) %all-gather.7.cloned.1.call-update) | async-done | bytes 9175056 | tf_op jit(solution)/shard_map/all_gather | solution.py:53
  154.7 109.1 %all-gather.5.cloned.1.call-done = bf16[640,7168]{1,0:T(8,128)(2,1)} async-done(((bf16[40,7168]{1,0:T(8,128)(2,1)}), bf16[640,7168]{1,0:T(8,128)(2,1)}) %all-gather.5.cloned.1.call-update) | async-done | bytes 9175056 | tf_op jit(solution)/shard_map/all_gather | solution.py:52
  263.9 7.5 %all-to-all-start.2 = ((bf16[16,448,256]{2,1,0:T(8,128)(2,1)}), bf16[16,448,256]{2,1,0:T(8,128)(2,1)}, u32[]{:S(2)}, u32[]{:S(2)}) async-start(bf16[16,448,256]{2,1,0:T(8,128)(2,1)} %bitcast.56), calls=%async_computation.2 | async-start | bytes 7340032 | tf_op jit(solution)/shard_map/all_to_all | solution.py:56
  271.4 0.2 all-gather.9.cloned.1.call-start
  271.6 0.0 copy-start.2
  271.6 0.0 slice-start
  271.6 0.0 slice-start.1
  271.6 7.0 %fusion.9 = f32[640,128]{0,1:T(8,128)S(1)} fusion(bf16[640,7168]{1,0:T(8,128)(2,1)} %all-gather.5.cloned.1.call-done, bf16[1,7168,128]{2,1,0:T(8,128)(2,1)} %param.10), kind=kOutput, calls=%fused_computation.27 | convolution fusion | flops 1174405120 | bytes 11337728 | tf_op jit(solution)/shard_map/dot_general | solution.py:62
  278.7 0.0 copy-done.2
  278.7 0.0 slice-start.2
  278.7 0.0 copy-start.1
  278.7 6.7 %fusion.2 = f32[640,128]{0,1:T(8,128)S(1)} fusion(bf16[640,7168]{1,0:T(8,128)(2,1)} %all-gather.7.cloned.1.call-done, bf16[1,128,7168]{2,1,0:T(8,128)(2,1)S(1)} %copy-done.2), kind=kOutput, calls=%fused_computation.7 | convolution fusion | flops 1174405120 | bytes 11337728 | tf_op jit(solution)/shard_map/dot_general | solution.py:67
  285.4 0.0 slice-done
  285.4 0.0 slice-done.1
  285.5 0.0 slice-done.2
  285.5 0.0 copy-done.1
  285.5 3.0 multiply_convert_fusion.2
  288.5 0.8 maximum_bitcast_fusion
  289.2 6.5 %convolution_convert_fusion = bf16[128,7168]{1,0:T(8,128)(2,1)} fusion(bf16[640,7168]{1,0:T(8,128)(2,1)} %all-gather.7.cloned.1.call-done, f32[640,128]{0,1:T(8,128)S(1)} %fusion.9, f32[640,128]{0,1:T(8,128)S(1)} %get-tuple-element.16), kind=kOutput, calls=%fused_computation | convolution fusion | flops 1175814144 | bytes 11665408 | tf_op jit(solution)/shard_map/dot_general | solution.py:75
  295.7 54.1 %all-to-all-done.2 = bf16[16,448,256]{2,1,0:T(8,128)(2,1)} async-done(((bf16[16,448,256]{2,1,0:T(8,128)(2,1)}), bf16[16,448,256]{2,1,0:T(8,128)(2,1)}, u32[]{:S(2)}, u32[]{:S(2)}) %all-to-all-start.2) | async-done | bytes 3670048 | tf_op jit(solution)/shard_map/all_to_all | solution.py:56
  349.7 0.0 all-gather.9.cloned.1.call-update
  349.8 2.3 collective-permute-start
  352.1 77.3 %all-gather.9.cloned.1.call-done = bf16[4096,640]{1,0:T(8,128)(2,1)} async-done(((bf16[256,640]{1,0:T(8,128)(2,1)}), bf16[4096,640]{1,0:T(8,128)(2,1)}) %all-gather.9.cloned.1.call-update) | async-done | bytes 5242896 | tf_op jit(solution)/shard_map/all_gather | solution.py:79
  429.4 6.6 %fusion.5 = bf16[640,448]{0,1:T(8,128)(2,1)S(1)} fusion(bf16[16,448,256]{2,1,0:T(8,128)(2,1)} %all-to-all-done.2, bf16[16,256,640]{2,1,0:T(8,128)(2,1)} %bitcast.68), kind=kOutput, calls=%fused_computation.11 | convolution fusion | flops 2349096960 | bytes 9486336 | tf_op jit(solution)/shard_map/dot_general | solution.py:80
  436.1 0.2 copy.29
  436.3 0.3 convert_element_type.54
  436.6 0.4 copy.30
  437.1 0.4 copy.31
  437.4 33.4 %all_to_all.22 = bf16[128,5,448]{2,1,0:T(8,128)(2,1)S(1)} all-to-all(bf16[128,5,448]{2,1,0:T(8,128)(2,1)S(1)} %copy.31), channel_id=1, replica_groups=mesh['pipe'=2,'group'=8,'member'=16] {'group','member'}, dimensions={0} | all-to-all | bytes 1146880 | tf_op jit(solution)/shard_map/all_to_all | solution.py:88
  470.8 0.2 copy.34
  471.0 0.8 reshape.117
  471.8 11.8 %collective-permute-start.2 = (bf16[40,7168]{1,0:T(8,128)(2,1)S(1)}, bf16[40,7168]{1,0:T(8,128)(2,1)S(1)}, u32[]{:S(2)}, u32[]{:S(2)}) collective-permute-start(bf16[40,7168]{1,0:T(8,128)(2,1)S(1)} %reshape.117), channel_id=1, source_target_pairs={{0,128},{128,0},{1,129},{129,1},{2,130},{130,2},{3,131},{131,3},{4... | collective-permute-start | bytes 1720328 | tf_op jit(solution)/shard_map/ppermute | solution.py:15
  483.6 0.1 eq.71
  483.7 0.1 and_convert_fusion
  483.8 0.1 collective-permute-start.1
  483.9 1.3 collective-permute-done.1
  485.2 0.0 collective-permute-done
  485.2 0.0 collective-permute-done.2
  485.2 3.4 fusion.1
  (11 shorter events, 0.2 us)
Async XLA Ops:
  7.2 36.9 %copy-start = (bf16[1,128,7168]{2,1,0:T(8,128)(2,1)S(1)}, bf16[1,128,7168]{2,1,0:T(8,128)(2,1)}, u32[]{:S(2)}) copy-start(bf16[1,128,7168]{2,1,0:T(8,128)(2,1)} %param.7) | copy-start | bytes 5505028
  7.2 147.6 %all-gather.7.cloned.1.call-start = ((), (), s32[]{:S(2)}) async-start(), calls=%async_computation.5 | async-start | bytes 9748480 | tf_op jit(solution)/shard_map/all_gather | solution.py:53
  44.0 219.9 %all-gather.5.cloned.1.call-start = ((), (), s32[]{:S(2)}) async-start(), calls=%async_computation.4 | async-start | bytes 9748480 | tf_op jit(solution)/shard_map/all_gather | solution.py:52
  263.9 85.9 %all-to-all-start.2 = ((bf16[16,448,256]{2,1,0:T(8,128)(2,1)}), bf16[16,448,256]{2,1,0:T(8,128)(2,1)}, u32[]{:S(2)}, u32[]{:S(2)}) async-start(bf16[16,448,256]{2,1,0:T(8,128)(2,1)} %bitcast.56), calls=%async_computation.2 | async-start | bytes 7340032 | tf_op jit(solution)/shard_map/all_to_all | solution.py:56
  271.4 158.1 %all-gather.9.cloned.1.call-start = ((), (), s32[]{:S(2)}) async-start(), calls=%async_computation.6 | async-start | bytes 5570560 | tf_op jit(solution)/shard_map/all_gather | solution.py:79
  271.6 7.1 %copy-start.2 = (bf16[1,128,7168]{2,1,0:T(8,128)(2,1)S(1)}, bf16[1,128,7168]{2,1,0:T(8,128)(2,1)}, u32[]{:S(2)}) copy-start(bf16[1,128,7168]{2,1,0:T(8,128)(2,1)} %param.11) | copy-start | bytes 5505028
  271.6 13.8 %slice-start = ((s8[9175040]{0:T(1024)(128)(4,1)}), s8[4194304]{0:T(1024)(128)(4,1)S(1)}, s32[]{:S(2)}) async-start(s8[9175040]{0:T(1024)(128)(4,1)} %bitcast.54), calls=%async_computation.7 | async-start | bytes 8388608
  271.6 13.8 %slice-start.1 = ((s8[9175040]{0:T(1024)(128)(4,1)}), s8[4194304]{0:T(1024)(128)(4,1)S(1)}, s32[]{:S(2)}) async-start(s8[9175040]{0:T(1024)(128)(4,1)} %bitcast.54), calls=%async_computation.8 | async-start | bytes 8388608
  278.7 6.8 %slice-start.2 = ((s8[9175040]{0:T(1024)(128)(4,1)}), s8[786432]{0:T(1024)(128)(4,1)S(1)}, s32[]{:S(2)}) async-start(s8[9175040]{0:T(1024)(128)(4,1)} %bitcast.54), calls=%async_computation.9 | async-start | bytes 1572864
  278.7 6.7 %copy-start.1 = (bf16[1,7168,128]{2,1,0:T(8,128)(2,1)S(1)}, bf16[1,7168,128]{2,1,0:T(8,128)(2,1)}, u32[]{:S(2)}) copy-start(bf16[1,7168,128]{2,1,0:T(8,128)(2,1)} %param.9) | copy-start | bytes 5505028
  349.8 135.4 %collective-permute-start = (bf16[128,7168]{1,0:T(8,128)(2,1)}, bf16[128,7168]{1,0:T(8,128)(2,1)}, u32[]{:S(2)}, u32[]{:S(2)}) collective-permute-start(bf16[128,7168]{1,0:T(8,128)(2,1)} %bitcast.63), channel_id=1, source_target_pairs={{0,128},{128,0},{1,129},{129,1},{2,130},{130,2},{3,131},{131,3},{4... | collective-permute-start | bytes 5505032 | tf_op jit(solution)/shard_map/ppermute | solution.py:15
  471.8 13.4 %collective-permute-start.2 = (bf16[40,7168]{1,0:T(8,128)(2,1)S(1)}, bf16[40,7168]{1,0:T(8,128)(2,1)S(1)}, u32[]{:S(2)}, u32[]{:S(2)}) collective-permute-start(bf16[40,7168]{1,0:T(8,128)(2,1)S(1)} %reshape.117), channel_id=1, source_target_pairs={{0,128},{128,0},{1,129},{129,1},{2,130},{130,2},{3,131},{131,3},{4... | collective-permute-start | bytes 1720328 | tf_op jit(solution)/shard_map/ppermute | solution.py:15
  483.8 1.4 collective-permute-start.1
Sparse Core Ops, SparseCore 0:
  44.1 110.5 all-gather.6
  157.1 106.7 all-gather.4
  349.9 79.5 all-gather.8

commit v15 on v14

--- a/solution.py
+++ b/solution.py
@@ -52,7 +52,10 @@
     got_in = lax.all_gather(near_in, "member", axis=0, tiled=True)
     got_grad = lax.all_gather(near_grad, "member", axis=0, tiled=True)
     both_cols = jnp.concatenate([gate_cols, up_cols], axis=1)
-    both_cols, got_in, got_grad = lax.optimization_barrier((both_cols, got_in, got_grad))
+    other_pick = from_behind(pick_mat, "pipe", -1)
+    both_cols, got_in, got_grad, other_pick = lax.optimization_barrier(
+        (both_cols, got_in, got_grad, other_pick)
+    )
     both_slice = lax.all_to_all(
         both_cols.reshape(SHARDS, -1, both_cols.shape[1]), "member", 0, 0, tiled=True
     )
@@ -89,7 +92,6 @@
     back = back.reshape(groups, members, slot_count, slice_width)
     returned = jnp.transpose(back, (0, 2, 1, 3)).reshape(groups * slot_count, model_width)
     other_grads = from_behind(grads, "pipe", -1)
-    other_pick = from_behind(pick_mat, "pipe", -1)
     other_returned = from_behind(returned, "pipe", -1)
     branch = jnp.dot(other_pick, other_returned, preferred_element_type=jnp.float32)
     handed = (other_grads.astype(jnp.float32) + branch).astype(jnp.bfloat16)

time: 498 us -> 498 us (level)
  no operation moved by 1% of the time
where the time goes in v15:
time: 498 us; the launch traced here: 495 us
  waiting for transfers between devices  318 us (64%)
  blocking collectives  86.8 us (17%)
  matrix products  35.5 us (7%)
  starting transfers between devices  26.1 us (5%)
  between operations  14 us (3%)
  local copies, waits for them, and re-layouts  8.13 us (2%)
  other arithmetic  7.03 us (1%)
    all_gather x1, waiting for transfers between devices, body(): got_in = lax.all_gather(near_in, 'member', axis=0, tiled=True)  109 us
    all_gather x1, waiting for transfers between devices, body(): all_grad = lax.all_gather(both_grad, 'member', axis=0, tiled=False)  77.3 us
    all_gather x1, waiting for transfers between devices, body(): got_grad = lax.all_gather(near_grad, 'member', axis=0, tiled=True)  75.4 us
    all_to_all x1, waiting for transfers between devices, body(): lax.all_to_all(both_cols.reshape(SHARDS, -1, both_cols.shape[1]), 'member...  54 us
    all_to_all x1, blocking collectives, body(): lax.all_to_all(slice_value.astype(jnp.bfloat16), ('group', 'member'), 0,...  33.4 us
    all_to_all x1, blocking collectives, body(): lax.all_to_all(send_grad, 'group', 0, 0, tiled=True)  30 us
    all_to_all x1, blocking collectives, body(): lax.all_to_all(send_in, 'group', 0, 0, tiled=True)  23.4 us
    ppermute x3, starting transfers between devices, from_behind(): return lax.ppermute(value, axis, pairs)  18.3 us
  transfers between devices with their start and end apart: 7, of which 5 were waited for; matrix products, arithmetic and copies ran while one was open for 8% of the time, Pallas kernels for 0%

profile of v15, /device:TPU:33, one launch (start us, length us, event | category | flops | bytes accessed | tf_op | source)
XLA Modules:
  0.0 495.1 jit_solution(384363827478749847)
XLA Ops:
  7.2 0.0 copy-start
  7.2 0.0 all-gather.7.cloned.1.call-start
  7.2 0.8 convert_reduce_fusion
  8.0 0.1 copy.26
  8.2 0.2 reduce_window_sum.11
  8.5 0.7 select_reduce_fusion.1
  9.2 0.1 select_reduce_fusion
  9.3 0.1 mul.41
  9.3 1.9 fusion
  11.2 1.0 reshape.113
  12.2 30.0 %all_to_all.20 = bf16[8,16,2240]{2,1,0:T(8,128)(2,1)S(1)} all-to-all(bf16[8,16,2240]{2,1,0:T(8,128)(2,1)S(1)} %reshape.113), channel_id=1, replica_groups=mesh['pipe'=2,'group'=8,'member'=16] {'group'}, dimensions={0} | all-to-all | bytes 1146880 | tf_op jit(solution)/shard_map/all_to_all | solution.py:51
  42.3 1.7 reshape.114
  44.0 0.0 all-gather.7.cloned.1.call-update
  44.0 0.0 all-gather.5.cloned.1.call-start
  44.0 0.0 copy-done
  44.1 0.4 convolution_convert_fusion.1
  44.4 1.0 reshape.111
  45.4 23.4 %all_to_all.21 = bf16[8,16,2240]{2,1,0:T(8,128)(2,1)S(1)} all-to-all(bf16[8,16,2240]{2,1,0:T(8,128)(2,1)S(1)} %reshape.111), channel_id=1, replica_groups=mesh['pipe'=2,'group'=8,'member'=16] {'group'}, dimensions={0} | all-to-all | bytes 1146880 | tf_op jit(solution)/shard_map/all_to_all | solution.py:50
  68.8 1.7 reshape.112
  70.5 0.0 all-gather.5.cloned.1.call-update
  70.6 0.1 eq.73
  70.7 0.1 and_convert_fusion
  70.8 4.1 collective-permute-start.1
  74.9 4.3 pad_maximum_fusion
  79.3 0.0 collective-permute-done.1
  79.3 75.4 %all-gather.7.cloned.1.call-done = bf16[640,7168]{1,0:T(8,128)(2,1)} async-done(((bf16[40,7168]{1,0:T(8,128)(2,1)}), bf16[640,7168]{1,0:T(8,128)(2,1)}) %all-gather.7.cloned.1.call-update) | async-done | bytes 9175056 | tf_op jit(solution)/shard_map/all_gather | solution.py:53
  154.7 109.1 %all-gather.5.cloned.1.call-done = bf16[640,7168]{1,0:T(8,128)(2,1)} async-done(((bf16[40,7168]{1,0:T(8,128)(2,1)}), bf16[640,7168]{1,0:T(8,128)(2,1)}) %all-gather.5.cloned.1.call-update) | async-done | bytes 9175056 | tf_op jit(solution)/shard_map/all_gather | solution.py:52
  263.9 7.5 %all-to-all-start.2 = ((bf16[16,448,256]{2,1,0:T(8,128)(2,1)}), bf16[16,448,256]{2,1,0:T(8,128)(2,1)}, u32[]{:S(2)}, u32[]{:S(2)}) async-start(bf16[16,448,256]{2,1,0:T(8,128)(2,1)} %bitcast.54), calls=%async_computation.2 | async-start | bytes 7340032 | tf_op jit(solution)/shard_map/all_to_all | solution.py:59
  271.4 0.2 all-gather.9.cloned.1.call-start
  271.6 0.0 copy-start.1
  271.6 0.0 slice-start
  271.6 0.0 slice-start.1
  271.6 7.0 %fusion.11 = f32[640,128]{0,1:T(8,128)S(1)} fusion(bf16[640,7168]{1,0:T(8,128)(2,1)} %all-gather.5.cloned.1.call-done, bf16[1,7168,128]{2,1,0:T(8,128)(2,1)} %param.9), kind=kOutput, calls=%fused_computation.29 | convolution fusion | flops 1174405120 | bytes 11337728 | tf_op jit(solution)/shard_map/dot_general | solution.py:64
  278.7 0.0 copy-done.1
  278.7 0.0 slice-start.2
  278.7 5.2 %fusion.9 = f32[640,128]{0,1:T(8,128)S(1)} fusion(bf16[640,7168]{1,0:T(8,128)(2,1)S(1)} %copy-done.1, bf16[1,7168,128]{2,1,0:T(8,128)(2,1)} %param.10), kind=kOutput, calls=%fused_computation.27 | convolution fusion | flops 1174405120 | bytes 11337728 | tf_op jit(solution)/shard_map/dot_general | solution.py:65
  283.9 0.0 slice-done
  283.9 0.0 slice-done.1
  283.9 0.0 slice-done.2
  284.0 4.5 multiply_convert_fusion.2
  288.5 0.8 maximum_bitcast_fusion
  289.2 6.5 %convolution_convert_fusion = bf16[128,7168]{1,0:T(8,128)(2,1)} fusion(bf16[640,7168]{1,0:T(8,128)(2,1)} %all-gather.7.cloned.1.call-done, f32[640,128]{0,1:T(8,128)S(1)} %fusion.9, f32[640,128]{0,1:T(8,128)S(1)} %fusion.11), kind=kOutput, calls=%fused_computation | convolution fusion | flops 1175814144 | bytes 11665408 | tf_op jit(solution)/shard_map/dot_general | solution.py:78
  295.7 54.0 %all-to-all-done.2 = bf16[16,448,256]{2,1,0:T(8,128)(2,1)} async-done(((bf16[16,448,256]{2,1,0:T(8,128)(2,1)}), bf16[16,448,256]{2,1,0:T(8,128)(2,1)}, u32[]{:S(2)}, u32[]{:S(2)}) %all-to-all-start.2) | async-done | bytes 3670048 | tf_op jit(solution)/shard_map/all_to_all | solution.py:59
  349.7 0.0 all-gather.9.cloned.1.call-update
  349.8 2.3 collective-permute-start
  352.1 77.3 %all-gather.9.cloned.1.call-done = bf16[4096,640]{1,0:T(8,128)(2,1)} async-done(((bf16[256,640]{1,0:T(8,128)(2,1)}), bf16[4096,640]{1,0:T(8,128)(2,1)}) %all-gather.9.cloned.1.call-update) | async-done | bytes 5242896 | tf_op jit(solution)/shard_map/all_gather | solution.py:82
  429.4 6.6 %fusion.5 = bf16[640,448]{0,1:T(8,128)(2,1)S(1)} fusion(bf16[16,448,256]{2,1,0:T(8,128)(2,1)} %all-to-all-done.2, bf16[16,256,640]{2,1,0:T(8,128)(2,1)} %bitcast.68), kind=kOutput, calls=%fused_computation.11 | convolution fusion | flops 2349096960 | bytes 9486336 | tf_op jit(solution)/shard_map/dot_general | solution.py:83
  436.0 0.2 copy.29
  436.3 0.3 convert_element_type.54
  436.6 0.4 copy.30
  437.1 0.4 copy.31
  437.4 33.4 %all_to_all.22 = bf16[128,5,448]{2,1,0:T(8,128)(2,1)S(1)} all-to-all(bf16[128,5,448]{2,1,0:T(8,128)(2,1)S(1)} %copy.31), channel_id=1, replica_groups=mesh['pipe'=2,'group'=8,'member'=16] {'group','member'}, dimensions={0} | all-to-all | bytes 1146880 | tf_op jit(solution)/shard_map/all_to_all | solution.py:91
  470.8 0.2 copy.34
  471.0 0.8 reshape.117
  471.8 11.8 %collective-permute-start.2 = (bf16[40,7168]{1,0:T(8,128)(2,1)S(1)}, bf16[40,7168]{1,0:T(8,128)(2,1)S(1)}, u32[]{:S(2)}, u32[]{:S(2)}) collective-permute-start(bf16[40,7168]{1,0:T(8,128)(2,1)S(1)} %reshape.117), channel_id=1, source_target_pairs={{0,128},{128,0},{1,129},{129,1},{2,130},{130,2},{3,131},{131,3},{4... | collective-permute-start | bytes 1720328 | tf_op jit(solution)/shard_map/ppermute | solution.py:15
  483.6 0.0 collective-permute-done
  483.6 1.6 collective-permute-done.2
  485.2 3.4 fusion.1
  (11 shorter events, 0.2 us)
Async XLA Ops:
  7.2 36.9 %copy-start = (bf16[1,128,7168]{2,1,0:T(8,128)(2,1)S(1)}, bf16[1,128,7168]{2,1,0:T(8,128)(2,1)}, u32[]{:S(2)}) copy-start(bf16[1,128,7168]{2,1,0:T(8,128)(2,1)} %param.7) | copy-start | bytes 5505028
  7.2 147.6 %all-gather.7.cloned.1.call-start = ((), (), s32[]{:S(2)}) async-start(), calls=%async_computation.5 | async-start | bytes 9748480 | tf_op jit(solution)/shard_map/all_gather | solution.py:53
  44.0 219.9 %all-gather.5.cloned.1.call-start = ((), (), s32[]{:S(2)}) async-start(), calls=%async_computation.4 | async-start | bytes 9748480 | tf_op jit(solution)/shard_map/all_gather | solution.py:52
  70.8 8.5 %collective-permute-start.1 = (bf16[128,40]{0,1:T(8,128)(2,1)S(1)}, bf16[128,40]{0,1:T(8,128)(2,1)S(1)}, u32[]{:S(2)}, u32[]{:S(2)}) collective-permute-start(bf16[128,40]{0,1:T(8,128)(2,1)S(1)} %and_convert_fusion), channel_id=1, source_target_pairs={{0,128},{128,0},{1,129},{129,1},{2,130},{130,2},{3,131},{131,3},{4... | collective-permute-start | bytes 30728 | tf_op jit(solution)/shard_map/ppermute | solution.py:15
  263.9 85.9 %all-to-all-start.2 = ((bf16[16,448,256]{2,1,0:T(8,128)(2,1)}), bf16[16,448,256]{2,1,0:T(8,128)(2,1)}, u32[]{:S(2)}, u32[]{:S(2)}) async-start(bf16[16,448,256]{2,1,0:T(8,128)(2,1)} %bitcast.54), calls=%async_computation.2 | async-start | bytes 7340032 | tf_op jit(solution)/shard_map/all_to_all | solution.py:59
  271.4 158.1 %all-gather.9.cloned.1.call-start = ((), (), s32[]{:S(2)}) async-start(), calls=%async_computation.6 | async-start | bytes 5570560 | tf_op jit(solution)/shard_map/all_gather | solution.py:82
  271.6 7.1 %copy-start.1 = (bf16[640,7168]{1,0:T(8,128)(2,1)S(1)}, bf16[640,7168]{1,0:T(8,128)(2,1)}, u32[]{:S(2)}) copy-start(bf16[640,7168]{1,0:T(8,128)(2,1)} %all-gather.5.cloned.1.call-done) | copy-start | bytes 27525124
  271.6 12.3 %slice-start = ((s8[9175040]{0:T(1024)(128)(4,1)}), s8[4194304]{0:T(1024)(128)(4,1)S(1)}, s32[]{:S(2)}) async-start(s8[9175040]{0:T(1024)(128)(4,1)} %bitcast.55), calls=%async_computation.7 | async-start | bytes 8388608
  271.6 12.3 %slice-start.1 = ((s8[9175040]{0:T(1024)(128)(4,1)}), s8[4194304]{0:T(1024)(128)(4,1)S(1)}, s32[]{:S(2)}) async-start(s8[9175040]{0:T(1024)(128)(4,1)} %bitcast.55), calls=%async_computation.8 | async-start | bytes 8388608
  278.7 5.2 %slice-start.2 = ((s8[9175040]{0:T(1024)(128)(4,1)}), s8[786432]{0:T(1024)(128)(4,1)S(1)}, s32[]{:S(2)}) async-start(s8[9175040]{0:T(1024)(128)(4,1)} %bitcast.55), calls=%async_computation.9 | async-start | bytes 1572864
  349.8 133.8 %collective-permute-start = (bf16[128,7168]{1,0:T(8,128)(2,1)}, bf16[128,7168]{1,0:T(8,128)(2,1)}, u32[]{:S(2)}, u32[]{:S(2)}) collective-permute-start(bf16[128,7168]{1,0:T(8,128)(2,1)} %bitcast.63), channel_id=1, source_target_pairs={{0,128},{128,0},{1,129},{129,1},{2,130},{130,2},{3,131},{131,3},{4... | collective-permute-start | bytes 5505032 | tf_op jit(solution)/shard_map/ppermute | solution.py:15
  471.8 13.4 %collective-permute-start.2 = (bf16[40,7168]{1,0:T(8,128)(2,1)S(1)}, bf16[40,7168]{1,0:T(8,128)(2,1)S(1)}, u32[]{:S(2)}, u32[]{:S(2)}) collective-permute-start(bf16[40,7168]{1,0:T(8,128)(2,1)S(1)} %reshape.117), channel_id=1, source_target_pairs={{0,128},{128,0},{1,129},{129,1},{2,130},{130,2},{3,131},{131,3},{4... | collective-permute-start | bytes 1720328 | tf_op jit(solution)/shard_map/ppermute | solution.py:15
Sparse Core Ops, SparseCore 0:
  44.1 110.5 all-gather.6
  157.1 106.7 all-gather.4
  349.9 79.5 all-gather.8
